TPU v7x, 256 devices: a whole 4x4x8 slice. The times are simulated.
256 devices in a mesh: space: 32 (over y_lo, z, core), chan: 8 (over x, y_hi).
Axes of the slice: x: 4, y: 4 (y_hi: 2, y_lo: 2; y = y_hi * 2 + y_lo), z: 8, core: 2. Of those that a mesh axis runs over, the one named last changes fastest.
Arguments:
- inputs: bfloat16 [32, 256, 2048], P('space', 'chan'), may hold values from -6 to 6
- weights: bfloat16 [27, 256, 256], P(None, 'chan'), may hold values from -0.078125 to 0.078125
- cotangent: bfloat16 [32, 256, 2048], P('space', 'chan'), may hold values from -6 to 6
Outputs:
- output: bfloat16 [32, 256, 2048], P('space', 'chan')
- input_grad: bfloat16 [32, 256, 2048], P('space', 'chan')
- weight_grad: float32 [27, 256, 256], P(None, 'chan')
All inputs are finite; a program needn't handle non-finite values.
Results may differ from a plain program's by a relative error of at most 0.001.
Values may be sent and summed in bfloat16 or wider, within the bound.
No kernel may reach another device: no remote copies, remote signals or barrier semaphores. Data moves between devices by JAX's collectives and lax.ppermute only.
A program may use at most 192 MiB of HBM per device.

v0:
```python
import jax
import jax.numpy as jnp
from jax import lax
from jax.sharding import PartitionSpec as P
from jax.experimental import pallas as pl
from jax.experimental.pallas import tpu as pltpu

PLANE_ROWS = 32
ROW_CELLS = 64


def extended(block, sides, width):
    for axis, dim in sides:
        count = lax.axis_size(axis)
        forward = [(i, i + 1) for i in range(count - 1)]
        backward = [(target, source) for source, target in forward]
        low = lax.ppermute(
            lax.slice_in_dim(block, block.shape[dim] - width, None, axis=dim), axis, forward
        )
        high = lax.ppermute(lax.slice_in_dim(block, 0, width, axis=dim), axis, backward)
        block = jnp.concatenate([low, block, high], axis=dim)
    return block


def partner_masks(count, first):
    masks = [1 << b for b in range(count.bit_length() - 1)]
    return [first] + [m for m in masks if m != first]


def halving_sum(block, axis, masks, dim):
    count = lax.axis_size(axis)
    index = lax.axis_index(axis)
    for mask in masks:
        half = block.shape[dim] // 2
        upper = (index // mask) % 2 == 1
        low = lax.slice_in_dim(block, 0, half, axis=dim)
        high = lax.slice_in_dim(block, half, 2 * half, axis=dim)
        keep = jnp.where(upper, high, low)
        send = jnp.where(upper, low, high)
        block = keep + lax.ppermute(send, axis, [(i, i ^ mask) for i in range(count)])
    return block


def doubling_gather(block, axis, masks, dim):
    count = lax.axis_size(axis)
    index = lax.axis_index(axis)
    for mask in masks:
        upper = (index // mask) % 2 == 1
        other = lax.ppermute(block, axis, [(i, i ^ mask) for i in range(count)])
        block = jnp.concatenate(
            [jnp.where(upper, other, block), jnp.where(upper, block, other)], axis=dim
        )
    return block


def plane_shift(field, tap_row, tap_col):
    lead = field.shape[:-1]
    grid = field.reshape(lead + (PLANE_ROWS, ROW_CELLS))
    padded = jnp.pad(grid, [(0, 0)] * len(lead) + [(1, 1), (1, 1)])
    window = padded[..., tap_row : tap_row + PLANE_ROWS, tap_col : tap_col + ROW_CELLS]
    return window.reshape(lead + (PLANE_ROWS * ROW_CELLS,))


def stack_at(padded, tap_row, tap_col):
    planes = padded.shape[0] - 2
    moved = plane_shift(padded, tap_row, tap_col)
    return jnp.concatenate(
        [moved[tap_depth : tap_depth + planes] for tap_depth in range(3)], axis=1
    )


def tap_weights(taps, tap_row, tap_col):
    return jnp.concatenate(
        [taps[tap_depth * 9 + tap_row * 3 + tap_col] for tap_depth in range(3)], axis=0
    )


def convolve(padded, taps):
    total = None
    for tap_row in range(3):
        for tap_col in range(3):
            term = jnp.einsum(
                "dcp,co->dop",
                stack_at(padded, tap_row, tap_col),
                tap_weights(taps, tap_row, tap_col),
                preferred_element_type=jnp.float32,
            )
            total = term if total is None else total + term
    return total


def weight_terms(padded, cot_whole, channels):
    pieces = [None] * 27
    for tap_row in range(3):
        for tap_col in range(3):
            block = jnp.einsum(
                "dcp,dop->co",
                stack_at(padded, tap_row, tap_col),
                cot_whole,
                preferred_element_type=jnp.float32,
            )
            block = block.reshape(3, channels, cot_whole.shape[1])
            for tap_depth in range(3):
                pieces[tap_depth * 9 + tap_row * 3 + tap_col] = block[tap_depth]
    return jnp.stack(pieces, axis=0)


def conv_forward(padded, taps):
    planes, channels, cells = padded.shape
    lhs = padded.reshape(1, planes, channels, PLANE_ROWS, ROW_CELLS)
    rhs = taps.reshape(3, 3, 3, channels, taps.shape[-1])
    out = lax.conv_general_dilated(
        lhs, rhs, (1, 1, 1), [(0, 0), (1, 1), (1, 1)],
        dimension_numbers=("NDCHW", "DHWIO", "NDCHW"),
        preferred_element_type=jnp.float32,
    )
    return out.reshape(planes - 2, taps.shape[-1], cells)


def conv_backward(cot_padded, taps):
    planes, channels, cells = cot_padded.shape
    lhs = cot_padded.reshape(1, planes, channels, PLANE_ROWS, ROW_CELLS)
    rhs = taps.reshape(3, 3, 3, taps.shape[1], channels)[::-1, ::-1, ::-1]
    out = lax.conv_general_dilated(
        lhs, rhs, (1, 1, 1), [(0, 0), (1, 1), (1, 1)],
        dimension_numbers=("NDCHW", "DHWOI", "NDCHW"),
        preferred_element_type=jnp.float32,
    )
    return out.reshape(planes - 2, taps.shape[1], cells)


FLAT_EDGE = 128


def filter_kernel(x_ref, c_ref, o_ref):
    cells = c_ref.shape[0]
    width = x_ref.shape[-1]
    column = lax.broadcasted_iota(jnp.int32, (x_ref.shape[1], cells), 1) % ROW_CELLS
    cot = c_ref[...]
    for tap_depth in range(3):
        plane = x_ref[tap_depth].astype(jnp.float32)
        for tap_row in range(3):
            for tap_col in range(3):
                offset = FLAT_EDGE + (tap_row - 1) * ROW_CELLS + (tap_col - 1)
                moved = pltpu.roll(plane, (width - offset) % width, 1)[:, :cells]
                if tap_col == 0:
                    moved = jnp.where(column >= 1, moved, 0.0)
                if tap_col == 2:
                    moved = jnp.where(column < ROW_CELLS - 1, moved, 0.0)
                o_ref[tap_depth * 9 + tap_row * 3 + tap_col] = jnp.dot(
                    moved.astype(jnp.bfloat16), cot, preferred_element_type=jnp.float32
                )


def conv_filter(padded, cot_whole):
    planes, channels, cells = padded.shape
    flat = jnp.pad(padded, ((0, 0), (0, 0), (FLAT_EDGE, FLAT_EDGE)))
    cot_t = cot_whole[0].T
    return pl.pallas_call(
        filter_kernel,
        out_shape=jax.ShapeDtypeStruct((27, channels, cot_t.shape[1]), jnp.float32),
    )(flat, cot_t)


def scatter_sum(block, axis, dim):
    count = lax.axis_size(axis)
    shape = block.shape
    parts = block.reshape(shape[:dim] + (count, shape[dim] // count) + shape[dim + 1 :])
    parts = jnp.moveaxis(parts, dim, 0)
    parts = lax.all_to_all(parts, axis, 0, 0, tiled=True)
    return parts.sum(axis=0)


def spread_gather(block, axis, dim):
    count = lax.axis_size(axis)
    copies = jnp.broadcast_to(block[None], (count,) + block.shape)
    copies = lax.all_to_all(copies, axis, 0, 0, tiled=True)
    copies = jnp.moveaxis(copies, 0, dim)
    shape = block.shape
    return copies.reshape(shape[:dim] + (count * shape[dim],) + shape[dim + 1 :])


def local(inputs, weights, cotangent):
    padded = extended(inputs, (("space", 0),), 1)
    partial_out = conv_forward(padded, weights)
    output = scatter_sum(partial_out, "chan", 1).astype(jnp.bfloat16)
    gathered = spread_gather(cotangent, "chan", 1)
    cot_padded = extended(gathered, (("space", 0),), 1)
    cot_whole = cot_padded[1:-1]
    input_grad = conv_backward(cot_padded, weights).astype(jnp.bfloat16)
    local_terms = conv_filter(padded, cot_whole)
    flat = local_terms.reshape(-1, local_terms.shape[-1])
    flat = spread_gather(scatter_sum(flat, "space", 0), "space", 0)
    weight_grad = flat.reshape(local_terms.shape)
    return (output, input_grad, weight_grad)


def solution(mesh):
    placed = (P("space", "chan", None), P(None, "chan", None), P("space", "chan", None))
    return jax.shard_map(
        local,
        mesh=mesh,
        in_specs=placed,
        out_specs=(P("space", "chan", None), P("space", "chan", None), P(None, "chan", None)),
        check_vma=False,
    )
```

profile of v0, /device:TPU:1, one launch (start us, length us, event | category | flops | bytes accessed | tf_op | source)
XLA Modules:
  0.0 152.7 jit_solution(13854848334532215519)
XLA Ops:
  0.6 0.0 copy-start
  0.7 2.1 %broadcast_in_dim.7 = bf16[8,1,32,2048]{3,2,1,0:T(8,128)(2,1)} broadcast(bf16[32,2048]{1,0:T(8,128)(2,1)} %bitcast.54), dimensions={2,3} | broadcast | bytes 1179648 | tf_op jit(solution)/shard_map/broadcast_in_dim | solution.py:176
  2.7 7.5 %all-to-all-start.1 = ((bf16[8,1,32,2048]{3,2,1,0:T(8,128)(2,1)}), bf16[8,1,32,2048]{3,2,1,0:T(8,128)(2,1)S(1)}, u32[]{:S(2)}, u32[]{:S(2)}) async-start(bf16[8,1,32,2048]{3,2,1,0:T(8,128)(2,1)} %broadcast_in_dim.7), calls=%async_computation.1 | async-start | bytes 2097152 | tf_op jit(solution)/shard_map/all_to_all | solution.py:177
  10.2 4.4 %collective-permute-start = (bf16[1,32,2048]{2,1,0:T(8,128)(2,1)S(1)}, bf16[1,32,2048]{2,1,0:T(8,128)(2,1)S(1)}, u32[]{:S(2)}, u32[]{:S(2)}) collective-permute-start(bf16[1,32,2048]{2,1,0:T(8,128)(2,1)S(1)} %copy-done.1), channel_id=1, source_target_pairs={{0,8},{8,16},{16,24},{24,32},{32,40},{40,48},{48,56},{56,64},{64,7... | collective-permute-start | bytes 393224 | tf_op jit(solution)/shard_map/ppermute | solution.py:17
  14.6 1.9 %collective-permute-start.1 = (bf16[1,32,2048]{2,1,0:T(8,128)(2,1)S(1)}, bf16[1,32,2048]{2,1,0:T(8,128)(2,1)S(1)}, u32[]{:S(2)}, u32[]{:S(2)}) collective-permute-start(bf16[1,32,2048]{2,1,0:T(8,128)(2,1)S(1)} %copy-done.1), channel_id=1, source_target_pairs={{8,0},{16,8},{24,16},{32,24},{40,32},{48,40},{56,48},{64,56},{72,6... | collective-permute-start | bytes 393224 | tf_op jit(solution)/shard_map/ppermute | solution.py:20
  16.5 0.0 collective-permute-done
  16.6 4.6 %collective-permute-done.1 = bf16[1,32,2048]{2,1,0:T(8,128)(2,1)S(1)} collective-permute-done((bf16[1,32,2048]{2,1,0:T(8,128)(2,1)S(1)}, bf16[1,32,2048]{2,1,0:T(8,128)(2,1)S(1)}, u32[]{:S(2)}, u32[]{:S(2)}) %collective-permute-start.1) | collective-permute-done | bytes 131104 | tf_op jit(solution)/shard_map/ppermute | solution.py:20
  21.2 0.8 pad.4.x_ref
  22.0 4.8 %all-to-all-done.1 = bf16[8,1,32,2048]{3,2,1,0:T(8,128)(2,1)S(1)} async-done(((bf16[8,1,32,2048]{3,2,1,0:T(8,128)(2,1)}), bf16[8,1,32,2048]{3,2,1,0:T(8,128)(2,1)S(1)}, u32[]{:S(2)}, u32[]{:S(2)}) %all-to-all-start.1) | async-done | bytes 1048608 | tf_op jit(solution)/shard_map/all_to_all | solution.py:177
  26.8 1.3 copy.45
  28.1 7.3 %shard_map.58 = f32[27,32,256]{2,1,0:T(8,128)} custom-call(bf16[3,32,2304]{2,1,0:T(8,128)(2,1)} %pad.4.x_ref, bf16[2048,256]{1,0:T(8,128)(2,1)} %bitcast.50), custom_call_target="tpu_custom_call" | custom-call | tf_op jit(solution)/shard_map/pallas_call | solution.py:159
  35.4 2.3 %reshape_reshape.6 = f32[32,27,256]{2,1,0:T(8,128)} reshape(f32[27,32,256]{2,1,0:T(8,128)} %shard_map.58) | data formatting | bytes 1769472 | tf_op jit(solution)/shard_map/reshape;reshape | solution.py:168
  37.7 9.0 %all-to-all-start.2 = ((f32[32,27,256]{2,1,0:T(8,128)}), f32[32,27,256]{2,1,0:T(8,128)}, u32[]{:S(2)}, u32[]{:S(2)}) async-start(f32[32,27,256]{2,1,0:T(8,128)} %reshape_reshape.6), calls=%async_computation.2 | async-start | bytes 2097152 | tf_op jit(solution)/shard_map/all_to_all | solution.py:170
  46.7 0.8 reshape.62
  47.5 2.1 %copy.31 = bf16[3,32,32,1,64]{2,1,4,0,3:T(8,128)(2,1)} copy(bf16[3,32,32,1,64]{4,2,1,0,3:T(8,128)(2,1)S(1)} %reshape.62) | data formatting | bytes 786432 | tf_op jit(solution)/shard_map/reshape | solution.py:110
  49.6 1.8 %pad.5 = bf16[3,32,32,1,72]{2,1,4,0,3:T(8,128)(2,1)S(1)} pad(bf16[3,32,32,1,64]{2,1,4,0,3:T(8,128)(2,1)} %copy.31, bf16[]{:T(256)} %constant.4.clone.1), padding=0_0x0_0x0_0x0_0x1_7 | pad | bytes 835586 | tf_op jit(solution)/shard_map/reshape | solution.py:110
  51.4 2.4 %copy.33 = bf16[3,32,32,1,8,9]{1,4,5,2,0,3:T(8,128)(2,1)} copy(bf16[3,32,32,1,8,9]{2,1,5,4,0,3:T(8,128)(2,1)S(1)} %bitcast.49) | data formatting | bytes 884736 | tf_op jit(solution)/shard_map/conv_general_dilated | solution.py:112
  53.8 1.1 slice.4
  54.9 3.9 %fusion.17 = f32[1,32,8,9,256]{4,2,3,1,0:T(8,128)S(1)} fusion(bf16[3,3,3,32,256]{4,3,2,1,0:T(8,128)(2,1)S(1)} %bitcast.41, bf16[3,32,32,1,7,2]{1,4,5,2,0,3:T(8,128)(2,1)S(1)} %slice.4, bf16[3,32,32,1,8,9]{1,4,5,2,0,3:T(8,128)(2,1)} %copy.33, pred[8,9]{0,1:T(8,128)(4,1)S(1)} %copy-done.2), kind=kOutput, calls=%fused_computation.19 | convolution fusion | flops 1000194048 | bytes 3330120 | tf_op jit(solution)/shard_map/conv_general_dilated | solution.py:112
  58.8 0.8 copy.34
  59.6 1.5 slice_bitcast_fusion
  61.0 5.6 %copy.35 = f32[1,1,256,32,64]{4,3,2,1,0:T(8,128)} copy(f32[1,1,256,32,64]{2,3,4,0,1:T(8,128)} %slice_bitcast_fusion) | data formatting | bytes 4194304 | tf_op jit(solution)/shard_map/conv_general_dilated | solution.py:112
  66.6 5.0 %transpose_reshape_reshape.3 = f32[8,1,32,2048]{3,2,0,1:T(8,128)} reshape(f32[1,1,256,32,64]{4,3,2,1,0:T(8,128)} %copy.35) | data formatting | bytes 4194304 | tf_op jit(solution)/shard_map/transpose;reshape;reshape | solution.py:169
  71.5 1.6 %all-to-all-done.2 = f32[32,27,256]{2,1,0:T(8,128)} async-done(((f32[32,27,256]{2,1,0:T(8,128)}), f32[32,27,256]{2,1,0:T(8,128)}, u32[]{:S(2)}, u32[]{:S(2)}) %all-to-all-start.2) | async-done | bytes 884768 | tf_op jit(solution)/shard_map/all_to_all | solution.py:170
  73.1 4.4 %all-to-all-start = ((f32[8,1,32,2048]{3,2,1,0:T(8,128)}), f32[8,1,32,2048]{3,2,1,0:T(8,128)}, u32[]{:S(2)}, u32[]{:S(2)}) async-start(f32[8,1,32,2048]{3,2,1,0:T(8,128)} %bitcast.48), calls=%async_computation | async-start | bytes 4194304 | tf_op jit(solution)/shard_map/all_to_all | solution.py:170
  77.5 4.5 %collective-permute-start.3 = (bf16[1,256,2048]{2,1,0:T(8,128)(2,1)S(1)}, bf16[1,256,2048]{2,1,0:T(8,128)(2,1)}, u32[]{:S(2)}, u32[]{:S(2)}) collective-permute-start(bf16[1,256,2048]{2,1,0:T(8,128)(2,1)S(1)} %bitcast.45), channel_id=1, source_target_pairs={{8,0},{16,8},{24,16},{32,24},{40,32},{48,40},{56,48},{64,56},{72,6... | collective-permute-start | bytes 3145736 | tf_op jit(solution)/shard_map/ppermute | solution.py:20
  82.0 3.8 %collective-permute-start.2 = (bf16[1,256,2048]{2,1,0:T(8,128)(2,1)S(1)}, bf16[1,256,2048]{2,1,0:T(8,128)(2,1)}, u32[]{:S(2)}, u32[]{:S(2)}) collective-permute-start(bf16[1,256,2048]{2,1,0:T(8,128)(2,1)S(1)} %bitcast.46), channel_id=1, source_target_pairs={{0,8},{8,16},{16,24},{24,32},{32,40},{40,48},{48,56},{56,64},{64,7... | collective-permute-start | bytes 3145736 | tf_op jit(solution)/shard_map/ppermute | solution.py:17
  85.9 1.3 reduce_sum.19
  87.2 23.6 %all-to-all-done = f32[8,1,32,2048]{3,2,1,0:T(8,128)} async-done(((f32[8,1,32,2048]{3,2,1,0:T(8,128)}), f32[8,1,32,2048]{3,2,1,0:T(8,128)}, u32[]{:S(2)}, u32[]{:S(2)}) %all-to-all-start) | async-done | bytes 2097184 | tf_op jit(solution)/shard_map/all_to_all | solution.py:170
  110.8 1.1 broadcast_in_dim.16
  111.9 9.6 %all-to-all-start.3 = ((f32[32,27,256]{2,1,0:T(8,128)}), f32[32,27,256]{2,1,0:T(8,128)}, u32[]{:S(2)}, u32[]{:S(2)}) async-start(f32[32,27,256]{2,1,0:T(8,128)} %broadcast_in_dim.16), calls=%async_computation.3 | async-start | bytes 2097152 | tf_op jit(solution)/shard_map/all_to_all | solution.py:177
  121.5 3.2 %concatenate.15 = bf16[1,1,256,32,64]{4,3,2,1,0:T(8,128)(2,1)} reshape(bf16[8,1,32,2048]{3,2,1,0:T(8,128)(2,1)S(1)} %all-to-all-done.1) | data formatting | bytes 2097152 | tf_op jit(solution)/shard_map/concatenate | solution.py:21
  124.7 2.8 %copy.39 = bf16[1,1,256,32,64]{2,4,3,1,0:T(8,128)(2,1)S(1)} copy(bf16[1,1,256,32,64]{4,3,2,1,0:T(8,128)(2,1)} %concatenate.15) | data formatting | bytes 2097152 | tf_op jit(solution)/shard_map/concatenate | solution.py:21
  127.5 0.0 collective-permute-done.3
  127.5 2.3 %copy.38 = bf16[1,256,2048]{1,2,0:T(8,128)(2,1)} copy(bf16[1,256,2048]{2,1,0:T(8,128)(2,1)} %collective-permute-done.3) | data formatting | bytes 2097152 | tf_op jit(solution)/shard_map/ppermute | solution.py:20
  129.8 0.0 collective-permute-done.2
  129.8 1.7 %copy.37 = bf16[1,256,2048]{1,2,0:T(8,128)(2,1)S(1)} copy(bf16[1,256,2048]{2,1,0:T(8,128)(2,1)} %collective-permute-done.2) | data formatting | bytes 2097152 | tf_op jit(solution)/shard_map/ppermute | solution.py:17
  131.5 1.6 %maximum_bitcast_fusion = bf16[3,256,32,1,64]{1,4,2,0,3:T(8,128)(2,1)S(1)} fusion(bf16[1,1,256,32,64]{2,4,3,1,0:T(8,128)(2,1)} %bitcast.51, bf16[1,1,256,32,64]{2,4,3,1,0:T(8,128)(2,1)S(1)} %copy.39, bf16[1,1,256,32,64]{2,4,3,1,0:T(8,128)(2,1)S(1)} %bitcast.52), kind=kLoop, calls=%fused_computation.10 | loop fusion | flops 3145728 | bytes 6291456 | tf_op jit(solution)/shard_map/concatenate | solution.py:21
  133.0 1.8 %copy.46 = bf16[3,256,32,1,64]{1,2,4,0,3:T(8,128)(2,1)S(1)} copy(bf16[3,256,32,1,64]{1,4,2,0,3:T(8,128)(2,1)S(1)} %maximum_bitcast_fusion) | data formatting | bytes 6291456
  134.8 0.4 pad.7.clone
  135.2 2.1 %copy.42 = bf16[3,256,32,1,8,9]{1,4,5,2,0,3:T(8,128)(2,1)S(1)} copy(bf16[3,256,32,1,8,9]{1,2,5,4,0,3:T(8,128)(2,1)S(1)} %bitcast.43) | data formatting | bytes 7077888 | tf_op jit(solution)/shard_map/conv_general_dilated | solution.py:124
  137.2 0.2 slice.6
  137.4 8.8 %fusion.23 = bf16[1,32,8,9,32]{4,2,3,1,0:T(8,128)(2,1)S(1)} fusion(bf16[3,3,3,32,256]{4,3,2,1,0:T(8,128)(2,1)S(1)} %bitcast.42, bf16[3,256,32,1,7,2]{1,4,5,2,0,3:T(8,128)(2,1)S(1)} %slice.6, bf16[3,256,32,1,8,9]{1,4,5,2,0,3:T(8,128)(2,1)S(1)} %copy.42, pred[8,9]{0,1:T(8,128)(4,1)S(1)} %copy-done.2), kind=kOutput, calls=%fused_computation.21 | convolution fusion | flops 1011105792 | bytes 4816968 | tf_op jit(solution)/shard_map/conv_general_dilated | solution.py:124
  146.2 0.1 copy.43
  146.3 0.8 copy.44
  147.1 0.9 convert_element_type.33
  148.1 2.4 %reduce_sum.18 = bf16[32,2048]{1,0:T(8,128)(2,1)} reduce(f32[8,1,32,2048]{3,2,1,0:T(8,128)} %all-to-all-done, f32[]{:T(128)} %constant.1.clone.1), dimensions={0,1}, to_apply=%region_0.0 | reduce | flops 458752 | bytes 2228228 | tf_op jit(solution)/shard_map/reduce_sum | solution.py:171
  150.5 2.3 %reshape_reshape.7 = f32[27,32,256]{2,1,0:T(8,128)} reshape(f32[32,27,256]{2,1,0:T(8,128)} %all-to-all-done.3) | data formatting | bytes 1769472 | tf_op jit(solution)/shard_map/reshape;reshape | solution.py:194
  (10 shorter events, 0.1 us)
Async XLA Ops:
  0.6 54.3 %copy-start = (bf16[27,32,256]{2,1,0:T(8,128)(2,1)S(1)}, bf16[27,32,256]{2,1,0:T(8,128)(2,1)}, u32[]{:S(2)}) copy-start(bf16[27,32,256]{2,1,0:T(8,128)(2,1)} %param.4) | copy-start | bytes 1327108
  0.6 9.5 %copy-start.1 = (bf16[1,32,2048]{2,1,0:T(8,128)(2,1)S(1)}, bf16[1,32,2048]{2,1,0:T(8,128)(2,1)}, u32[]{:S(2)}) copy-start(bf16[1,32,2048]{2,1,0:T(8,128)(2,1)} %param.3) | copy-start | bytes 393220
  2.7 24.1 %all-to-all-start.1 = ((bf16[8,1,32,2048]{3,2,1,0:T(8,128)(2,1)}), bf16[8,1,32,2048]{3,2,1,0:T(8,128)(2,1)S(1)}, u32[]{:S(2)}, u32[]{:S(2)}) async-start(bf16[8,1,32,2048]{3,2,1,0:T(8,128)(2,1)} %broadcast_in_dim.7), calls=%async_computation.1 | async-start | bytes 2097152 | tf_op jit(solution)/shard_map/all_to_all | solution.py:177
  10.2 6.3 %collective-permute-start = (bf16[1,32,2048]{2,1,0:T(8,128)(2,1)S(1)}, bf16[1,32,2048]{2,1,0:T(8,128)(2,1)S(1)}, u32[]{:S(2)}, u32[]{:S(2)}) collective-permute-start(bf16[1,32,2048]{2,1,0:T(8,128)(2,1)S(1)} %copy-done.1), channel_id=1, source_target_pairs={{0,8},{8,16},{16,24},{24,32},{32,40},{40,48},{48,56},{56,64},{64,7... | collective-permute-start | bytes 393224 | tf_op jit(solution)/shard_map/ppermute | solution.py:17
  14.6 6.6 %collective-permute-start.1 = (bf16[1,32,2048]{2,1,0:T(8,128)(2,1)S(1)}, bf16[1,32,2048]{2,1,0:T(8,128)(2,1)S(1)}, u32[]{:S(2)}, u32[]{:S(2)}) collective-permute-start(bf16[1,32,2048]{2,1,0:T(8,128)(2,1)S(1)} %copy-done.1), channel_id=1, source_target_pairs={{8,0},{16,8},{24,16},{32,24},{40,32},{48,40},{56,48},{64,56},{72,6... | collective-permute-start | bytes 393224 | tf_op jit(solution)/shard_map/ppermute | solution.py:20
  37.7 35.4 %all-to-all-start.2 = ((f32[32,27,256]{2,1,0:T(8,128)}), f32[32,27,256]{2,1,0:T(8,128)}, u32[]{:S(2)}, u32[]{:S(2)}) async-start(f32[32,27,256]{2,1,0:T(8,128)} %reshape_reshape.6), calls=%async_computation.2 | async-start | bytes 2097152 | tf_op jit(solution)/shard_map/all_to_all | solution.py:170
  49.6 5.3 %copy-start.2 = (pred[8,9]{0,1:T(8,128)(4,1)S(1)}, pred[8,9]{0,1:T(8,128)(4,1)}, u32[]{:S(2)}) copy-start(pred[8,9]{0,1:T(8,128)(4,1)} %constant.17) | copy-start | bytes 220
  73.1 37.7 %all-to-all-start = ((f32[8,1,32,2048]{3,2,1,0:T(8,128)}), f32[8,1,32,2048]{3,2,1,0:T(8,128)}, u32[]{:S(2)}, u32[]{:S(2)}) async-start(f32[8,1,32,2048]{3,2,1,0:T(8,128)} %bitcast.48), calls=%async_computation | async-start | bytes 4194304 | tf_op jit(solution)/shard_map/all_to_all | solution.py:170
  77.5 50.0 %collective-permute-start.3 = (bf16[1,256,2048]{2,1,0:T(8,128)(2,1)S(1)}, bf16[1,256,2048]{2,1,0:T(8,128)(2,1)}, u32[]{:S(2)}, u32[]{:S(2)}) collective-permute-start(bf16[1,256,2048]{2,1,0:T(8,128)(2,1)S(1)} %bitcast.45), channel_id=1, source_target_pairs={{8,0},{16,8},{24,16},{32,24},{40,32},{48,40},{56,48},{64,56},{72,6... | collective-permute-start | bytes 3145736 | tf_op jit(solution)/shard_map/ppermute | solution.py:20
  82.0 47.7 %collective-permute-start.2 = (bf16[1,256,2048]{2,1,0:T(8,128)(2,1)S(1)}, bf16[1,256,2048]{2,1,0:T(8,128)(2,1)}, u32[]{:S(2)}, u32[]{:S(2)}) collective-permute-start(bf16[1,256,2048]{2,1,0:T(8,128)(2,1)S(1)} %bitcast.46), channel_id=1, source_target_pairs={{0,8},{8,16},{16,24},{24,32},{32,40},{40,48},{48,56},{56,64},{64,7... | collective-permute-start | bytes 3145736 | tf_op jit(solution)/shard_map/ppermute | solution.py:17
  111.9 38.6 %all-to-all-start.3 = ((f32[32,27,256]{2,1,0:T(8,128)}), f32[32,27,256]{2,1,0:T(8,128)}, u32[]{:S(2)}, u32[]{:S(2)}) async-start(f32[32,27,256]{2,1,0:T(8,128)} %broadcast_in_dim.16), calls=%async_computation.3 | async-start | bytes 2097152 | tf_op jit(solution)/shard_map/all_to_all | solution.py:177
where the time goes:
time: 154 us; the launch traced here: 153 us
  local copies, waits for them, and re-layouts  46.9 us (30%)
  starting transfers between devices  45.1 us (29%)
  waiting for transfers between devices  34.6 us (22%)
  matrix products  12.6 us (8%)
  Pallas kernels  7.28 us (5%)
  other arithmetic  5.25 us (3%)
    all_to_all x2, waiting for transfers between devices, scatter_sum(): parts = lax.all_to_all(parts, axis, 0, 0, tiled=True)  25.2 us
    all_to_all x2, starting transfers between devices, spread_gather(): copies = lax.all_to_all(copies, axis, 0, 0, tiled=True)  17.1 us
    all_to_all x2, starting transfers between devices, scatter_sum(): parts = lax.all_to_all(parts, axis, 0, 0, tiled=True)  13.4 us
    conv_general_dilated x5, local copies, waits for them, and re-layouts, conv_forward(): lax.conv_general_dilated(lhs, rhs, (1, 1, 1), [(0, 0), (1, 1), (1, 1)], d...  11.3 us
    conv_general_dilated x1, matrix products, conv_backward(): lax.conv_general_dilated(lhs, rhs, (1, 1, 1), [(0, 0), (1, 1), (1, 1)], d...  8.76 us
    ppermute x2, starting transfers between devices, extended(): lax.ppermute(lax.slice_in_dim(block, block.shape[dim] - width, None, axis...  8.19 us
    pallas_call x1, Pallas kernels, conv_filter(): pl.pallas_call(filter_kernel, out_shape=jax.ShapeDtypeStruct((27, channel...  7.28 us
    ppermute x2, starting transfers between devices, extended(): lax.ppermute(lax.slice_in_dim(block, 0, width, axis=dim), axis, backward)  6.45 us
  transfers between devices with their start and end apart: 8, of which 4 were waited for; matrix products, arithmetic and copies ran while one was open for 37% of the time, Pallas kernels for 0%

commit v1 on v0

--- a/solution.py
+++ b/solution.py
@@ -117,16 +117,25 @@
     return out.reshape(planes - 2, taps.shape[-1], cells)
 
 
-def conv_backward(cot_padded, taps):
-    planes, channels, cells = cot_padded.shape
-    lhs = cot_padded.reshape(1, planes, channels, PLANE_ROWS, ROW_CELLS)
+def conv_backward(cot_plane, taps):
+    planes, channels, cells = cot_plane.shape
+    lhs = cot_plane.reshape(1, planes, channels, PLANE_ROWS, ROW_CELLS)
     rhs = taps.reshape(3, 3, 3, taps.shape[1], channels)[::-1, ::-1, ::-1]
     out = lax.conv_general_dilated(
-        lhs, rhs, (1, 1, 1), [(0, 0), (1, 1), (1, 1)],
+        lhs, rhs, (1, 1, 1), [(2, 2), (1, 1), (1, 1)],
         dimension_numbers=("NDCHW", "DHWOI", "NDCHW"),
         preferred_element_type=jnp.float32,
     )
-    return out.reshape(planes - 2, taps.shape[1], cells)
+    return out.reshape(planes + 2, taps.shape[1], cells)
+
+
+def spill_sum(parts, axis):
+    count = lax.axis_size(axis)
+    forward = [(i, i + 1) for i in range(count - 1)]
+    backward = [(target, source) for source, target in forward]
+    from_low = lax.ppermute(parts[-1:], axis, forward)
+    from_high = lax.ppermute(parts[:1], axis, backward)
+    return parts[1:-1] + from_low + from_high
 
 
 FLAT_EDGE = 128
@@ -185,10 +194,8 @@
     partial_out = conv_forward(padded, weights)
     output = scatter_sum(partial_out, "chan", 1).astype(jnp.bfloat16)
     gathered = spread_gather(cotangent, "chan", 1)
-    cot_padded = extended(gathered, (("space", 0),), 1)
-    cot_whole = cot_padded[1:-1]
-    input_grad = conv_backward(cot_padded, weights).astype(jnp.bfloat16)
-    local_terms = conv_filter(padded, cot_whole)
+    input_grad = spill_sum(conv_backward(gathered, weights), "space").astype(jnp.bfloat16)
+    local_terms = conv_filter(padded, gathered)
     flat = local_terms.reshape(-1, local_terms.shape[-1])
     flat = spread_gather(scatter_sum(flat, "space", 0), "space", 0)
     weight_grad = flat.reshape(local_terms.shape)

time: 154 us -> 152 us (0.987)
  waiting for transfers between devices: 34.6 us -> 40.3 us
  matrix products: 12.6 us -> 9.65 us
  starting transfers between devices: 45.1 us -> 42.6 us
    ppermute x0 -> x2, waiting for transfers between devices: none -> 9.89 us  [the longest x1 7.81 us: spill_sum(): from_low = lax.ppermute(parts[-1:], axis, forward)]
    concatenate x4 -> x1, local copies, waits for them, and re-layouts: 6.33 us -> 0.01 us  [extended(): block = jnp.concatenate([low, block, high], axis=dim)]
    slice x0 -> x9, local copies, waits for them, and re-layouts: none -> 5.9 us  [the longest x3 3.85 us: spill_sum(): from_low = lax.ppermute(parts[-1:], axis, forward)]
    ppermute x0 -> x2, starting transfers between devices: none -> 5.44 us  [the longest x1 3.52 us: spill_sum(): from_low = lax.ppermute(parts[-1:], axis, forward)]
    ppermute x2 -> x1, starting transfers between devices: 6.45 us -> 1.92 us  [extended(): lax.ppermute(lax.slice_in_dim(block, 0, width, axis=dim), axis, backward)]
    all_to_all x2, waiting for transfers between devices: 25.2 us -> 21 us  [scatter_sum(): parts = lax.all_to_all(parts, axis, 0, 0, tiled=True)]
    ppermute x2 -> x0, local copies, waits for them, and re-layouts: 3.97 us -> none  [the longest x1 2.27 us: extended(): lax.ppermute(lax.slice_in_dim(block, 0, width, axis=dim), axis, backward)]
    ppermute x2 -> x1, starting transfers between devices: 8.19 us -> 4.39 us  [extended(): lax.ppermute(lax.slice_in_dim(block, block.shape[dim] - width, None, axis...]
  transfers between devices with their start and end apart: 8 -> 8, of which waited for: 4 -> 6; matrix products, arithmetic and copies ran while one was open for 37% -> 34% of each run, Pallas kernels for 0% -> 0%
where the time goes in v1:
time: 152 us; the launch traced here: 151 us
  local copies, waits for them, and re-layouts  45.7 us (30%)
  starting transfers between devices  42.6 us (28%)
  waiting for transfers between devices  40.3 us (27%)
  matrix products  9.65 us (6%)
  Pallas kernels  7.28 us (5%)
  other arithmetic  4.38 us (3%)
    all_to_all x2, waiting for transfers between devices, scatter_sum(): parts = lax.all_to_all(parts, axis, 0, 0, tiled=True)  21 us
    all_to_all x2, starting transfers between devices, spread_gather(): copies = lax.all_to_all(copies, axis, 0, 0, tiled=True)  17.4 us
    all_to_all x2, starting transfers between devices, scatter_sum(): parts = lax.all_to_all(parts, axis, 0, 0, tiled=True)  13.4 us
    conv_general_dilated x5, local copies, waits for them, and re-layouts, conv_forward(): lax.conv_general_dilated(lhs, rhs, (1, 1, 1), [(0, 0), (1, 1), (1, 1)], d...  11.3 us
    ppermute x1, waiting for transfers between devices, spill_sum(): from_low = lax.ppermute(parts[-1:], axis, forward)  7.81 us
    pallas_call x1, Pallas kernels, conv_filter(): pl.pallas_call(filter_kernel, out_shape=jax.ShapeDtypeStruct((27, channel...  7.28 us
    conv_general_dilated x1, matrix products, conv_backward(): lax.conv_general_dilated(lhs, rhs, (1, 1, 1), [(2, 2), (1, 1), (1, 1)], d...  5.76 us
    another operation x1, local copies, waits for them, and re-layouts, scatter_sum(): parts = jnp.moveaxis(parts, dim, 0)  4.96 us
  transfers between devices with their start and end apart: 8, of which 6 were waited for; matrix products, arithmetic and copies ran while one was open for 34% of the time, Pallas kernels for 0%

profile of v1, /device:TPU:1, one launch (start us, length us, event | category | flops | bytes accessed | tf_op | source)
XLA Modules:
  0.0 150.8 jit_solution(9756276531584134728)
XLA Ops:
  0.7 2.1 %broadcast_in_dim.7 = bf16[8,1,32,2048]{3,2,1,0:T(8,128)(2,1)} broadcast(bf16[32,2048]{1,0:T(8,128)(2,1)} %bitcast.53), dimensions={2,3} | broadcast | bytes 1179648 | tf_op jit(solution)/shard_map/broadcast_in_dim | solution.py:185
  2.7 7.5 %all-to-all-start.1 = ((bf16[8,1,32,2048]{3,2,1,0:T(8,128)(2,1)}), bf16[8,1,32,2048]{3,2,1,0:T(8,128)(2,1)S(1)}, u32[]{:S(2)}, u32[]{:S(2)}) async-start(bf16[8,1,32,2048]{3,2,1,0:T(8,128)(2,1)} %broadcast_in_dim.7), calls=%async_computation.1 | async-start | bytes 2097152 | tf_op jit(solution)/shard_map/all_to_all | solution.py:186
  10.2 4.4 %collective-permute-start = (bf16[1,32,2048]{2,1,0:T(8,128)(2,1)S(1)}, bf16[1,32,2048]{2,1,0:T(8,128)(2,1)S(1)}, u32[]{:S(2)}, u32[]{:S(2)}) collective-permute-start(bf16[1,32,2048]{2,1,0:T(8,128)(2,1)S(1)} %copy-done.1), channel_id=1, source_target_pairs={{0,8},{8,16},{16,24},{24,32},{32,40},{40,48},{48,56},{56,64},{64,7... | collective-permute-start | bytes 393224 | tf_op jit(solution)/shard_map/ppermute | solution.py:17
  14.6 1.9 %collective-permute-start.1 = (bf16[1,32,2048]{2,1,0:T(8,128)(2,1)S(1)}, bf16[1,32,2048]{2,1,0:T(8,128)(2,1)S(1)}, u32[]{:S(2)}, u32[]{:S(2)}) collective-permute-start(bf16[1,32,2048]{2,1,0:T(8,128)(2,1)S(1)} %copy-done.1), channel_id=1, source_target_pairs={{8,0},{16,8},{24,16},{32,24},{40,32},{48,40},{56,48},{64,56},{72,6... | collective-permute-start | bytes 393224 | tf_op jit(solution)/shard_map/ppermute | solution.py:20
  16.6 4.6 %collective-permute-done.1 = bf16[1,32,2048]{2,1,0:T(8,128)(2,1)S(1)} collective-permute-done((bf16[1,32,2048]{2,1,0:T(8,128)(2,1)S(1)}, bf16[1,32,2048]{2,1,0:T(8,128)(2,1)S(1)}, u32[]{:S(2)}, u32[]{:S(2)}) %collective-permute-start.1) | collective-permute-done | bytes 131104 | tf_op jit(solution)/shard_map/ppermute | solution.py:20
  21.2 0.8 pad.4.x_ref
  22.0 4.8 %all-to-all-done.1 = bf16[8,1,32,2048]{3,2,1,0:T(8,128)(2,1)S(1)} async-done(((bf16[8,1,32,2048]{3,2,1,0:T(8,128)(2,1)}), bf16[8,1,32,2048]{3,2,1,0:T(8,128)(2,1)S(1)}, u32[]{:S(2)}, u32[]{:S(2)}) %all-to-all-start.1) | async-done | bytes 1048608 | tf_op jit(solution)/shard_map/all_to_all | solution.py:186
  26.8 1.3 copy.49
  28.1 7.3 %shard_map.58 = f32[27,32,256]{2,1,0:T(8,128)} custom-call(bf16[3,32,2304]{2,1,0:T(8,128)(2,1)} %pad.4.x_ref, bf16[2048,256]{1,0:T(8,128)(2,1)} %bitcast.52), custom_call_target="tpu_custom_call" | custom-call | tf_op jit(solution)/shard_map/pallas_call | solution.py:168
  35.4 2.3 %reshape_reshape.6 = f32[32,27,256]{2,1,0:T(8,128)} reshape(f32[27,32,256]{2,1,0:T(8,128)} %shard_map.58) | data formatting | bytes 1769472 | tf_op jit(solution)/shard_map/reshape;reshape | solution.py:177
  37.7 9.0 %all-to-all-start.2 = ((f32[32,27,256]{2,1,0:T(8,128)}), f32[32,27,256]{2,1,0:T(8,128)}, u32[]{:S(2)}, u32[]{:S(2)}) async-start(f32[32,27,256]{2,1,0:T(8,128)} %reshape_reshape.6), calls=%async_computation.2 | async-start | bytes 2097152 | tf_op jit(solution)/shard_map/all_to_all | solution.py:179
  46.7 0.8 reshape.51
  47.5 2.1 %copy.34 = bf16[3,32,32,1,64]{2,1,4,0,3:T(8,128)(2,1)} copy(bf16[3,32,32,1,64]{4,2,1,0,3:T(8,128)(2,1)S(1)} %reshape.51) | data formatting | bytes 786432 | tf_op jit(solution)/shard_map/reshape | solution.py:110
  49.7 1.8 %pad.5 = bf16[3,32,32,1,72]{2,1,4,0,3:T(8,128)(2,1)S(1)} pad(bf16[3,32,32,1,64]{2,1,4,0,3:T(8,128)(2,1)} %copy.34, bf16[]{:T(256)} %constant.4.clone.1), padding=0_0x0_0x0_0x0_0x1_7 | pad | bytes 835586 | tf_op jit(solution)/shard_map/reshape | solution.py:110
  51.4 2.4 %copy.36 = bf16[3,32,32,1,8,9]{1,4,5,2,0,3:T(8,128)(2,1)} copy(bf16[3,32,32,1,8,9]{2,1,5,4,0,3:T(8,128)(2,1)S(1)} %bitcast.47) | data formatting | bytes 884736 | tf_op jit(solution)/shard_map/conv_general_dilated | solution.py:112
  53.8 1.1 slice.33
  54.9 3.9 %fusion.9 = f32[1,32,8,9,256]{4,2,3,1,0:T(8,128)S(1)} fusion(bf16[3,3,3,32,256]{4,3,2,1,0:T(8,128)(2,1)S(1)} %bitcast.42, bf16[3,32,32,1,7,2]{1,4,5,2,0,3:T(8,128)(2,1)S(1)} %slice.33, bf16[3,32,32,1,8,9]{1,4,5,2,0,3:T(8,128)(2,1)} %copy.36, pred[8,9]{0,1:T(8,128)(4,1)S(1)} %copy-done.2), kind=kOutput, calls=%fused_computation.12 | convolution fusion | flops 1000194048 | bytes 3330120 | tf_op jit(solution)/shard_map/conv_general_dilated | solution.py:112
  58.8 0.8 copy.37
  59.6 1.5 slice_bitcast_fusion
  61.1 5.6 %copy.38 = f32[1,1,256,32,64]{4,3,2,1,0:T(8,128)} copy(f32[1,1,256,32,64]{2,3,4,0,1:T(8,128)} %slice_bitcast_fusion) | data formatting | bytes 4194304 | tf_op jit(solution)/shard_map/conv_general_dilated | solution.py:112
  66.6 5.0 %transpose_reshape_reshape.3 = f32[8,1,32,2048]{3,2,0,1:T(8,128)} reshape(f32[1,1,256,32,64]{4,3,2,1,0:T(8,128)} %copy.38) | data formatting | bytes 4194304 | tf_op jit(solution)/shard_map/transpose;reshape;reshape | solution.py:178
  71.6 1.5 %all-to-all-done.2 = f32[32,27,256]{2,1,0:T(8,128)} async-done(((f32[32,27,256]{2,1,0:T(8,128)}), f32[32,27,256]{2,1,0:T(8,128)}, u32[]{:S(2)}, u32[]{:S(2)}) %all-to-all-start.2) | async-done | bytes 884768 | tf_op jit(solution)/shard_map/all_to_all | solution.py:179
  73.1 4.4 %all-to-all-start = ((f32[8,1,32,2048]{3,2,1,0:T(8,128)}), f32[8,1,32,2048]{3,2,1,0:T(8,128)}, u32[]{:S(2)}, u32[]{:S(2)}) async-start(f32[8,1,32,2048]{3,2,1,0:T(8,128)} %bitcast.46), calls=%async_computation | async-start | bytes 4194304 | tf_op jit(solution)/shard_map/all_to_all | solution.py:179
  77.5 3.2 %reshape.55 = bf16[1,256,32,1,64]{4,2,1,3,0:T(8,128)(2,1)} reshape(bf16[8,1,32,2048]{3,2,1,0:T(8,128)(2,1)S(1)} %all-to-all-done.1) | data formatting | bytes 2097152 | tf_op jit(solution)/shard_map/reshape;reshape;transpose | solution.py:122
  80.7 4.1 %copy.50 = bf16[1,256,32,1,64]{1,2,4,3,0:T(8,128)(2,1)S(1)} copy(bf16[1,256,32,1,64]{4,2,1,3,0:T(8,128)(2,1)} %reshape.55) | data formatting | bytes 2097152
  84.9 0.7 copy.42
  85.7 1.3 reduce_sum.19
  87.0 19.4 %all-to-all-done = f32[8,1,32,2048]{3,2,1,0:T(8,128)} async-done(((f32[8,1,32,2048]{3,2,1,0:T(8,128)}), f32[8,1,32,2048]{3,2,1,0:T(8,128)}, u32[]{:S(2)}, u32[]{:S(2)}) %all-to-all-start) | async-done | bytes 2097184 | tf_op jit(solution)/shard_map/all_to_all | solution.py:179
  106.4 1.1 broadcast_in_dim.16
  107.5 10.0 %all-to-all-start.3 = ((f32[32,27,256]{2,1,0:T(8,128)}), f32[32,27,256]{2,1,0:T(8,128)}, u32[]{:S(2)}, u32[]{:S(2)}) async-start(f32[32,27,256]{2,1,0:T(8,128)} %broadcast_in_dim.16), calls=%async_computation.3 | async-start | bytes 2097152 | tf_op jit(solution)/shard_map/all_to_all | solution.py:186
  117.5 5.8 %convolution_select_fusion = f32[3,32,8,9,32]{4,2,3,1,0:T(8,128)S(1)} fusion(bf16[3,3,3,32,256]{4,3,2,1,0:T(8,128)(2,1)S(1)} %bitcast.43, pred[8,9]{0,1:T(8,128)(4,1)S(1)} %copy-done.2, bf16[1,256,32,1,7,2]{1,4,5,2,3,0:T(8,128)(2,1)S(1)} %slice.35, bf16[1,256,32,1,8,9]{1,4,5,2,3,0:T(8,128)(2,1)S(1)} %copy.42), kind=kOutput, calls=%fused_computation.11 | convolution fusion | flops 1002528768 | bytes 2736200 | tf_op jit(solution)/shard_map/conv_general_dilated | solution.py:124
  123.2 0.2 fusion.26
  123.5 0.2 copy.45
  123.7 1.0 slice_bitcast_fusion.2
  124.7 1.9 %copy.46 = f32[1,1,32,32,64]{4,3,2,1,0:T(8,128)S(1)} copy(f32[1,1,32,32,64]{2,3,4,0,1:T(8,128)} %slice_bitcast_fusion.2) | data formatting | bytes 524288 | tf_op jit(solution)/shard_map/slice | solution.py:136
  126.7 0.9 slice.21
  127.6 3.5 %collective-permute-start.2 = (f32[1,32,2048]{2,1,0:T(8,128)}, f32[1,32,2048]{2,1,0:T(8,128)S(1)}, u32[]{:S(2)}, u32[]{:S(2)}) collective-permute-start(f32[1,32,2048]{2,1,0:T(8,128)} %slice.21), channel_id=1, source_target_pairs={{0,8},{8,16},{16,24},{24,32},{32,40},{40,48},{48,56},{56,64},{64,7... | collective-permute-start | bytes 786440 | tf_op jit(solution)/shard_map/ppermute | solution.py:136
  131.1 0.2 copy.47
  131.4 0.8 copy.48
  132.2 0.2 slice.23
  132.4 1.9 %collective-permute-start.3 = (f32[1,32,2048]{2,1,0:T(8,128)S(1)}, f32[1,32,2048]{2,1,0:T(8,128)S(1)}, u32[]{:S(2)}, u32[]{:S(2)}) collective-permute-start(f32[1,32,2048]{2,1,0:T(8,128)S(1)} %slice.23), channel_id=1, source_target_pairs={{8,0},{16,8},{24,16},{32,24},{40,32},{48,40},{56,48},{64,56},{72,6... | collective-permute-start | bytes 786440 | tf_op jit(solution)/shard_map/ppermute | solution.py:137
  134.3 0.2 copy.43
  134.6 0.8 copy.44
  135.6 7.8 %collective-permute-done.2 = f32[1,32,2048]{2,1,0:T(8,128)S(1)} collective-permute-done((f32[1,32,2048]{2,1,0:T(8,128)}, f32[1,32,2048]{2,1,0:T(8,128)S(1)}, u32[]{:S(2)}, u32[]{:S(2)}) %collective-permute-start.2) | collective-permute-done | bytes 262176 | tf_op jit(solution)/shard_map/ppermute | solution.py:136
  143.4 2.1 %collective-permute-done.3 = f32[1,32,2048]{2,1,0:T(8,128)S(1)} collective-permute-done((f32[1,32,2048]{2,1,0:T(8,128)S(1)}, f32[1,32,2048]{2,1,0:T(8,128)S(1)}, u32[]{:S(2)}, u32[]{:S(2)}) %collective-permute-start.3) | collective-permute-done | bytes 262176 | tf_op jit(solution)/shard_map/ppermute | solution.py:137
  145.5 0.7 add_convert_fusion
  146.2 2.4 %reduce_sum.18 = bf16[32,2048]{1,0:T(8,128)(2,1)} reduce(f32[8,1,32,2048]{3,2,1,0:T(8,128)} %all-to-all-done, f32[]{:T(128)} %constant.1.clone.1), dimensions={0,1}, to_apply=%region_0.0 | reduce | flops 458752 | bytes 2228228 | tf_op jit(solution)/shard_map/reduce_sum | solution.py:180
  148.6 2.3 %reshape_reshape.7 = f32[27,32,256]{2,1,0:T(8,128)} reshape(f32[32,27,256]{2,1,0:T(8,128)} %all-to-all-done.3) | data formatting | bytes 1769472 | tf_op jit(solution)/shard_map/reshape;reshape | solution.py:201
  (16 shorter events, 0.6 us)
Async XLA Ops:
  0.6 54.3 %copy-start = (bf16[27,32,256]{2,1,0:T(8,128)(2,1)S(1)}, bf16[27,32,256]{2,1,0:T(8,128)(2,1)}, u32[]{:S(2)}) copy-start(bf16[27,32,256]{2,1,0:T(8,128)(2,1)} %param.4) | copy-start | bytes 1327108
  0.6 9.6 %copy-start.1 = (bf16[1,32,2048]{2,1,0:T(8,128)(2,1)S(1)}, bf16[1,32,2048]{2,1,0:T(8,128)(2,1)}, u32[]{:S(2)}) copy-start(bf16[1,32,2048]{2,1,0:T(8,128)(2,1)} %param.3) | copy-start | bytes 393220
  2.7 24.1 %all-to-all-start.1 = ((bf16[8,1,32,2048]{3,2,1,0:T(8,128)(2,1)}), bf16[8,1,32,2048]{3,2,1,0:T(8,128)(2,1)S(1)}, u32[]{:S(2)}, u32[]{:S(2)}) async-start(bf16[8,1,32,2048]{3,2,1,0:T(8,128)(2,1)} %broadcast_in_dim.7), calls=%async_computation.1 | async-start | bytes 2097152 | tf_op jit(solution)/shard_map/all_to_all | solution.py:186
  10.2 6.3 %collective-permute-start = (bf16[1,32,2048]{2,1,0:T(8,128)(2,1)S(1)}, bf16[1,32,2048]{2,1,0:T(8,128)(2,1)S(1)}, u32[]{:S(2)}, u32[]{:S(2)}) collective-permute-start(bf16[1,32,2048]{2,1,0:T(8,128)(2,1)S(1)} %copy-done.1), channel_id=1, source_target_pairs={{0,8},{8,16},{16,24},{24,32},{32,40},{40,48},{48,56},{56,64},{64,7... | collective-permute-start | bytes 393224 | tf_op jit(solution)/shard_map/ppermute | solution.py:17
  14.6 6.6 %collective-permute-start.1 = (bf16[1,32,2048]{2,1,0:T(8,128)(2,1)S(1)}, bf16[1,32,2048]{2,1,0:T(8,128)(2,1)S(1)}, u32[]{:S(2)}, u32[]{:S(2)}) collective-permute-start(bf16[1,32,2048]{2,1,0:T(8,128)(2,1)S(1)} %copy-done.1), channel_id=1, source_target_pairs={{8,0},{16,8},{24,16},{32,24},{40,32},{48,40},{56,48},{64,56},{72,6... | collective-permute-start | bytes 393224 | tf_op jit(solution)/shard_map/ppermute | solution.py:20
  37.7 35.4 %all-to-all-start.2 = ((f32[32,27,256]{2,1,0:T(8,128)}), f32[32,27,256]{2,1,0:T(8,128)}, u32[]{:S(2)}, u32[]{:S(2)}) async-start(f32[32,27,256]{2,1,0:T(8,128)} %reshape_reshape.6), calls=%async_computation.2 | async-start | bytes 2097152 | tf_op jit(solution)/shard_map/all_to_all | solution.py:179
  51.4 3.5 %copy-start.2 = (pred[8,9]{0,1:T(8,128)(4,1)S(1)}, pred[8,9]{0,1:T(8,128)(4,1)}, u32[]{:S(2)}) copy-start(pred[8,9]{0,1:T(8,128)(4,1)} %constant.17) | copy-start | bytes 220
  73.1 33.2 %all-to-all-start = ((f32[8,1,32,2048]{3,2,1,0:T(8,128)}), f32[8,1,32,2048]{3,2,1,0:T(8,128)}, u32[]{:S(2)}, u32[]{:S(2)}) async-start(f32[8,1,32,2048]{3,2,1,0:T(8,128)} %bitcast.46), calls=%async_computation | async-start | bytes 4194304 | tf_op jit(solution)/shard_map/all_to_all | solution.py:179
  107.5 41.1 %all-to-all-start.3 = ((f32[32,27,256]{2,1,0:T(8,128)}), f32[32,27,256]{2,1,0:T(8,128)}, u32[]{:S(2)}, u32[]{:S(2)}) async-start(f32[32,27,256]{2,1,0:T(8,128)} %broadcast_in_dim.16), calls=%async_computation.3 | async-start | bytes 2097152 | tf_op jit(solution)/shard_map/all_to_all | solution.py:186
  127.6 15.8 %collective-permute-start.2 = (f32[1,32,2048]{2,1,0:T(8,128)}, f32[1,32,2048]{2,1,0:T(8,128)S(1)}, u32[]{:S(2)}, u32[]{:S(2)}) collective-permute-start(f32[1,32,2048]{2,1,0:T(8,128)} %slice.21), channel_id=1, source_target_pairs={{0,8},{8,16},{16,24},{24,32},{32,40},{40,48},{48,56},{56,64},{64,7... | collective-permute-start | bytes 786440 | tf_op jit(solution)/shard_map/ppermute | solution.py:136
  132.4 13.1 %collective-permute-start.3 = (f32[1,32,2048]{2,1,0:T(8,128)S(1)}, f32[1,32,2048]{2,1,0:T(8,128)S(1)}, u32[]{:S(2)}, u32[]{:S(2)}) collective-permute-start(f32[1,32,2048]{2,1,0:T(8,128)S(1)} %slice.23), channel_id=1, source_target_pairs={{8,0},{16,8},{24,16},{32,24},{40,32},{48,40},{56,48},{64,56},{72,6... | collective-permute-start | bytes 786440 | tf_op jit(solution)/shard_map/ppermute | solution.py:137

commit v2 on v1

--- a/solution.py
+++ b/solution.py
@@ -192,7 +192,8 @@
 def local(inputs, weights, cotangent):
     padded = extended(inputs, (("space", 0),), 1)
     partial_out = conv_forward(padded, weights)
-    output = scatter_sum(partial_out, "chan", 1).astype(jnp.bfloat16)
+    chan_masks = partner_masks(lax.axis_size("chan"), 1)[::-1]
+    output = halving_sum(partial_out, "chan", chan_masks, 1).astype(jnp.bfloat16)
     gathered = spread_gather(cotangent, "chan", 1)
     input_grad = spill_sum(conv_backward(gathered, weights), "space").astype(jnp.bfloat16)
     local_terms = conv_filter(padded, gathered)

time: 152 us -> 146 us (0.961); the launches traced: 151 us -> 143 us
  waiting for transfers between devices: 40.3 us -> 23.4 us
  other arithmetic: 4.38 us -> 9.76 us
  local copies, waits for them, and re-layouts: 45.7 us -> 47.9 us
    all_to_all x2 -> x1, waiting for transfers between devices: 21 us -> 0.01 us  [scatter_sum(): parts = lax.all_to_all(parts, axis, 0, 0, tiled=True)]
    ppermute x0 -> x3, waiting for transfers between devices: none -> 14.7 us  [halving_sum(): lax.ppermute(send, axis, [(i, i ^ mask) for i in range(count)])]
    ppermute x1, waiting for transfers between devices: 7.81 us -> 0.01 us  [spill_sum(): from_low = lax.ppermute(parts[-1:], axis, forward)]
    ppermute x0 -> x3, starting transfers between devices: none -> 6.61 us  [halving_sum(): lax.ppermute(send, axis, [(i, i ^ mask) for i in range(count)])]
    conv_general_dilated x5, local copies, waits for them, and re-layouts: 11.3 us -> 5.7 us  [conv_forward(): lax.conv_general_dilated(lhs, rhs, (1, 1, 1), [(0, 0), (1, 1), (1, 1)], d...]
    another operation x1 -> x0, local copies, waits for them, and re-layouts: 4.96 us -> none  [scatter_sum(): parts = jnp.moveaxis(parts, dim, 0)]
    ppermute x1, waiting for transfers between devices: 4.61 us -> 0.01 us  [extended(): lax.ppermute(lax.slice_in_dim(block, 0, width, axis=dim), axis, backward)]
    slice x3, local copies, waits for them, and re-layouts: 1.03 us -> 5.06 us  [spill_sum(): from_high = lax.ppermute(parts[:1], axis, backward)]
  transfers between devices with their start and end apart: 8 -> 10, of which waited for: 6 -> 3; matrix products, arithmetic and copies ran while one was open for 34% -> 45% of each run, Pallas kernels for 0% -> 5%
where the time goes in v2:
time: 146 us; the launch traced here: 143 us
  local copies, waits for them, and re-layouts  47.9 us (33%)
  starting transfers between devices  44.1 us (30%)
  waiting for transfers between devices  23.4 us (16%)
  other arithmetic  9.76 us (7%)
  matrix products  9.7 us (7%)
  Pallas kernels  7.28 us (5%)
    ppermute x3, waiting for transfers between devices, halving_sum(): lax.ppermute(send, axis, [(i, i ^ mask) for i in range(count)])  14.7 us
    all_to_all x2, starting transfers between devices, spread_gather(): copies = lax.all_to_all(copies, axis, 0, 0, tiled=True)  14 us
    all_to_all x1, starting transfers between devices, scatter_sum(): parts = lax.all_to_all(parts, axis, 0, 0, tiled=True)  11 us
    all_to_all x2, waiting for transfers between devices, spread_gather(): copies = lax.all_to_all(copies, axis, 0, 0, tiled=True)  8.67 us
    pallas_call x1, Pallas kernels, conv_filter(): pl.pallas_call(filter_kernel, out_shape=jax.ShapeDtypeStruct((27, channel...  7.28 us
    ppermute x3, starting transfers between devices, halving_sum(): lax.ppermute(send, axis, [(i, i ^ mask) for i in range(count)])  6.61 us
    unnamed x16, local copies, waits for them, and re-layouts  6.33 us
    conv_general_dilated x1, matrix products, conv_backward(): lax.conv_general_dilated(lhs, rhs, (1, 1, 1), [(2, 2), (1, 1), (1, 1)], d...  5.76 us
  transfers between devices with their start and end apart: 10, of which 3 were waited for; matrix products, arithmetic and copies ran while one was open for 45% of the time, Pallas kernels for 5%

profile of v2, /device:TPU:1, one launch (start us, length us, event | category | flops | bytes accessed | tf_op | source)
XLA Modules:
  0.0 143.1 jit_solution(4923628964056603721)
XLA Ops:
  0.7 5.1 %collective-permute-start = (bf16[1,32,2048]{2,1,0:T(8,128)(2,1)}, bf16[1,32,2048]{2,1,0:T(8,128)(2,1)S(1)}, u32[]{:S(2)}, u32[]{:S(2)}) collective-permute-start(bf16[1,32,2048]{2,1,0:T(8,128)(2,1)} %param.3), channel_id=1, source_target_pairs={{0,8},{8,16},{16,24},{24,32},{32,40},{40,48},{48,56},{56,64},{64,7... | collective-permute-start | bytes 393224 | tf_op jit(solution)/shard_map/ppermute | solution.py:17
  5.7 1.9 %collective-permute-start.1 = (bf16[1,32,2048]{2,1,0:T(8,128)(2,1)}, bf16[1,32,2048]{2,1,0:T(8,128)(2,1)S(1)}, u32[]{:S(2)}, u32[]{:S(2)}) collective-permute-start(bf16[1,32,2048]{2,1,0:T(8,128)(2,1)} %param.3), channel_id=1, source_target_pairs={{8,0},{16,8},{24,16},{32,24},{40,32},{48,40},{56,48},{64,56},{72,6... | collective-permute-start | bytes 393224 | tf_op jit(solution)/shard_map/ppermute | solution.py:20
  7.6 2.0 %broadcast_in_dim.7 = bf16[8,1,32,2048]{3,2,1,0:T(8,128)(2,1)} broadcast(bf16[32,2048]{1,0:T(8,128)(2,1)} %bitcast.49), dimensions={2,3} | broadcast | bytes 1179648 | tf_op jit(solution)/shard_map/broadcast_in_dim | solution.py:185
  9.6 6.7 %all-to-all-start = ((bf16[8,1,32,2048]{3,2,1,0:T(8,128)(2,1)}), bf16[8,1,32,2048]{3,2,1,0:T(8,128)(2,1)S(1)}, u32[]{:S(2)}, u32[]{:S(2)}) async-start(bf16[8,1,32,2048]{3,2,1,0:T(8,128)(2,1)} %broadcast_in_dim.7), calls=%async_computation | async-start | bytes 2097152 | tf_op jit(solution)/shard_map/all_to_all | solution.py:186
  16.4 0.8 reshape.45
  17.2 2.1 %copy.36 = bf16[3,32,32,1,64]{2,1,4,0,3:T(8,128)(2,1)} copy(bf16[3,32,32,1,64]{4,2,1,0,3:T(8,128)(2,1)S(1)} %reshape.45) | data formatting | bytes 786432 | tf_op jit(solution)/shard_map/reshape | solution.py:110
  19.3 1.8 %pad.5 = bf16[3,32,32,1,72]{2,1,4,0,3:T(8,128)(2,1)S(1)} pad(bf16[3,32,32,1,64]{2,1,4,0,3:T(8,128)(2,1)} %copy.36, bf16[]{:T(256)} %constant.58.clone.1), padding=0_0x0_0x0_0x0_0x1_7 | pad | bytes 835586 | tf_op jit(solution)/shard_map/reshape | solution.py:110
  21.1 2.4 %copy.38 = bf16[3,32,32,1,8,9]{1,4,5,2,0,3:T(8,128)(2,1)} copy(bf16[3,32,32,1,8,9]{2,1,5,4,0,3:T(8,128)(2,1)S(1)} %bitcast.43) | data formatting | bytes 884736 | tf_op jit(solution)/shard_map/conv_general_dilated | solution.py:112
  23.5 1.1 slice.57
  24.6 3.9 %fusion.9 = f32[1,32,8,9,256]{4,2,3,1,0:T(8,128)S(1)} fusion(bf16[3,3,3,32,256]{4,3,2,1,0:T(8,128)(2,1)S(1)} %bitcast.37, bf16[3,32,32,1,7,2]{1,4,5,2,0,3:T(8,128)(2,1)S(1)} %slice.57, bf16[3,32,32,1,8,9]{1,4,5,2,0,3:T(8,128)(2,1)} %copy.38, pred[8,9]{0,1:T(8,128)(4,1)S(1)} %copy-done.5), kind=kOutput, calls=%fused_computation.12 | convolution fusion | flops 1000194048 | bytes 3330120 | tf_op jit(solution)/shard_map/conv_general_dilated | solution.py:112
  28.6 0.8 pad.4.x_ref
  29.4 0.8 copy.39
  30.4 1.2 copy.40
  31.6 1.3 copy-done.1
  33.0 1.2 slice_select_fusion.2
  34.2 3.0 %collective-permute-start.2 = (f32[1,128,2048]{1,2,0:T(8,128)}, f32[1,128,2048]{1,2,0:T(8,128)}, u32[]{:S(2)}, u32[]{:S(2)}) collective-permute-start(f32[1,128,2048]{1,2,0:T(8,128)} %slice_select_fusion.2), channel_id=1, source_target_pairs={{0,4},{1,5},{2,6},{3,7},{4,0},{5,1},{6,2},{7,3},{8,12},{9,13},{10,... | collective-permute-start | bytes 3145736 | tf_op jit(solution)/shard_map/ppermute | solution.py:40
  37.1 1.3 copy.54
  38.4 7.3 %shard_map.58 = f32[27,32,256]{2,1,0:T(8,128)} custom-call(bf16[3,32,2304]{2,1,0:T(8,128)(2,1)} %pad.4.x_ref, bf16[2048,256]{1,0:T(8,128)(2,1)} %bitcast.48), custom_call_target="tpu_custom_call" | custom-call | tf_op jit(solution)/shard_map/pallas_call | solution.py:168
  45.7 2.3 %reshape_reshape.6 = f32[32,27,256]{2,1,0:T(8,128)} reshape(f32[27,32,256]{2,1,0:T(8,128)} %shard_map.58) | data formatting | bytes 1769472 | tf_op jit(solution)/shard_map/reshape;reshape | solution.py:177
  48.0 11.0 %all-to-all-start.1 = ((f32[32,27,256]{2,1,0:T(8,128)}), f32[32,27,256]{2,1,0:T(8,128)}, u32[]{:S(2)}, u32[]{:S(2)}) async-start(f32[32,27,256]{2,1,0:T(8,128)} %reshape_reshape.6), calls=%async_computation.1 | async-start | bytes 2097152 | tf_op jit(solution)/shard_map/all_to_all | solution.py:179
  59.0 3.2 %reshape.49 = bf16[1,256,32,1,64]{4,2,1,3,0:T(8,128)(2,1)} reshape(bf16[8,1,32,2048]{3,2,1,0:T(8,128)(2,1)S(1)} %all-to-all-done) | data formatting | bytes 2097152 | tf_op jit(solution)/shard_map/reshape;reshape;transpose | solution.py:122
  62.2 4.1 %copy.56 = bf16[1,256,32,1,64]{1,2,4,3,0:T(8,128)(2,1)S(1)} copy(bf16[1,256,32,1,64]{4,2,1,3,0:T(8,128)(2,1)} %reshape.49) | data formatting | bytes 2097152
  67.2 5.8 %convolution_select_fusion = f32[3,32,8,9,32]{4,2,3,1,0:T(8,128)S(1)} fusion(bf16[3,3,3,32,256]{4,3,2,1,0:T(8,128)(2,1)S(1)} %bitcast.38, pred[8,9]{0,1:T(8,128)(4,1)S(1)} %copy-done.5, bf16[1,256,32,1,7,2]{1,4,5,2,3,0:T(8,128)(2,1)S(1)} %slice.65, bf16[1,256,32,1,8,9]{1,4,5,2,3,0:T(8,128)(2,1)S(1)} %copy.47), kind=kOutput, calls=%fused_computation.11 | convolution fusion | flops 1002528768 | bytes 2736200 | tf_op jit(solution)/shard_map/conv_general_dilated | solution.py:124
  73.0 1.2 fusion.26
  74.5 0.8 copy.51
  75.3 0.9 slice.45
  76.2 3.5 %collective-permute-start.5 = (f32[1,32,2048]{2,1,0:T(8,128)}, f32[1,32,2048]{2,1,0:T(8,128)}, u32[]{:S(2)}, u32[]{:S(2)}) collective-permute-start(f32[1,32,2048]{2,1,0:T(8,128)} %slice.45), channel_id=1, source_target_pairs={{0,8},{8,16},{16,24},{24,32},{32,40},{40,48},{48,56},{56,64},{64,7... | collective-permute-start | bytes 786440 | tf_op jit(solution)/shard_map/ppermute | solution.py:136
  79.7 2.5 %copy.52 = f32[1,32,8,9,32]{4,1,3,2,0:T(8,128)} copy(f32[1,32,8,9,32]{4,2,3,1,0:T(8,128)} %get-tuple-element.13) | data formatting | bytes 589824 | tf_op jit(solution)/shard_map/conv_general_dilated | solution.py:124
  82.3 2.0 %select_add_fusion.1 = f32[1,128,2048]{1,2,0:T(8,128)S(1)} fusion(f32[1,128,2048]{1,2,0:T(8,128)} %collective-permute-done.2, f32[1,256,2048]{1,2,0:T(8,128)} %bitcast.40, pred[]{:T(512)S(6)} %eq.15), kind=kLoop, calls=%fused_computation.24 | loop fusion | flops 524288 | bytes 4194305 | tf_op jit(solution)/shard_map/add | solution.py:40
  84.3 1.3 slice_select_fusion.1
  85.6 2.3 %copy.41 = f32[1,64,2048]{2,1,0:T(8,128)} copy(f32[1,64,2048]{1,2,0:T(8,128)} %slice_select_fusion.1) | data formatting | bytes 1048576 | tf_op jit(solution)/shard_map/jit(_where)/select_n | solution.py:39
  88.2 2.3 %slice_bitcast_fusion.1 = f32[1,1,32,32,64]{2,3,4,0,1:T(8,128)} fusion(f32[1,32,1,72,32]{4,1,3,2,0:T(8,128)} %bitcast.45), kind=kLoop, calls=%fused_computation.19 | loop fusion | bytes 524288 | tf_op jit(solution)/shard_map/slice | solution.py:137
  90.4 1.9 %copy.53 = f32[1,1,32,32,64]{4,3,2,1,0:T(8,128)S(1)} copy(f32[1,1,32,32,64]{2,3,4,0,1:T(8,128)} %slice_bitcast_fusion.1) | data formatting | bytes 524288 | tf_op jit(solution)/shard_map/slice | solution.py:137
  92.4 0.9 slice.47
  93.3 1.9 %collective-permute-start.6 = (f32[1,32,2048]{2,1,0:T(8,128)}, f32[1,32,2048]{2,1,0:T(8,128)}, u32[]{:S(2)}, u32[]{:S(2)}) collective-permute-start(f32[1,32,2048]{2,1,0:T(8,128)} %slice.47), channel_id=1, source_target_pairs={{8,0},{16,8},{24,16},{32,24},{40,32},{48,40},{56,48},{64,56},{72,6... | collective-permute-start | bytes 786440 | tf_op jit(solution)/shard_map/ppermute | solution.py:137
  95.5 0.8 copy.49
  96.5 5.7 %collective-permute-done.3 = f32[1,64,2048]{2,1,0:T(8,128)} collective-permute-done((f32[1,64,2048]{2,1,0:T(8,128)}, f32[1,64,2048]{2,1,0:T(8,128)}, u32[]{:S(2)}, u32[]{:S(2)}) %collective-permute-start.3) | collective-permute-done | bytes 524320 | tf_op jit(solution)/shard_map/ppermute | solution.py:40
  102.1 2.3 %copy.42 = f32[1,64,2048]{1,2,0:T(8,128)} copy(f32[1,64,2048]{2,1,0:T(8,128)} %collective-permute-done.3) | data formatting | bytes 1048576 | tf_op jit(solution)/shard_map/ppermute | solution.py:40
  104.5 1.3 reduce_sum.9
  105.8 1.1 broadcast_in_dim.16
  106.9 7.4 %all-to-all-start.2 = ((f32[32,27,256]{2,1,0:T(8,128)}), f32[32,27,256]{2,1,0:T(8,128)}, u32[]{:S(2)}, u32[]{:S(2)}) async-start(f32[32,27,256]{2,1,0:T(8,128)} %broadcast_in_dim.16), calls=%async_computation.2 | async-start | bytes 2097152 | tf_op jit(solution)/shard_map/all_to_all | solution.py:186
  114.2 1.6 %select_add_fusion = f32[1,64,2048]{1,2,0:T(8,128)S(1)} fusion(f32[1,64,2048]{1,2,0:T(8,128)} %copy.42, f32[1,128,2048]{1,2,0:T(8,128)S(1)} %select_add_fusion.1, pred[]{:T(512)S(6)} %eq.14), kind=kLoop, calls=%fused_computation.23 | loop fusion | flops 262144 | bytes 2097153 | tf_op jit(solution)/shard_map/add | solution.py:40
  116.5 3.4 %collective-permute-start.4 = (f32[1,32,2048]{2,1,0:T(8,128)S(1)}, f32[1,32,2048]{2,1,0:T(8,128)S(1)}, u32[]{:S(2)}, u32[]{:S(2)}) collective-permute-start(f32[1,32,2048]{2,1,0:T(8,128)S(1)} %copy.43), channel_id=1, source_target_pairs={{0,1},{1,0},{2,3},{3,2},{4,5},{5,4},{6,7},{7,6},{8,9},{9,8},{10,11... | collective-permute-start | bytes 786440 | tf_op jit(solution)/shard_map/ppermute | solution.py:40
  119.8 1.7 %add_convert_fusion.1 = bf16[1,32,2048]{2,1,0:T(8,128)(2,1)} fusion(f32[1,32,2048]{2,1,0:T(8,128)} %collective-permute-done.6, f32[1,32,2048]{2,1,0:T(8,128)S(1)} %slice.43, f32[1,32,2048]{2,1,0:T(8,128)} %collective-permute-done.5), kind=kLoop, calls=%fused_computation.29 | loop fusion | flops 196608 | bytes 917504 | tf_op jit(solution)/shard_map/convert_element_type | solution.py:198
  121.6 9.1 %collective-permute-done.4 = f32[1,32,2048]{2,1,0:T(8,128)S(1)} collective-permute-done((f32[1,32,2048]{2,1,0:T(8,128)S(1)}, f32[1,32,2048]{2,1,0:T(8,128)S(1)}, u32[]{:S(2)}, u32[]{:S(2)}) %collective-permute-start.4) | collective-permute-done | bytes 262176 | tf_op jit(solution)/shard_map/ppermute | solution.py:40
  131.3 0.8 copy.55
  132.1 8.7 %all-to-all-done.2 = f32[32,27,256]{2,1,0:T(8,128)} async-done(((f32[32,27,256]{2,1,0:T(8,128)}), f32[32,27,256]{2,1,0:T(8,128)}, u32[]{:S(2)}, u32[]{:S(2)}) %all-to-all-start.2) | async-done | bytes 884768 | tf_op jit(solution)/shard_map/all_to_all | solution.py:186
  140.8 2.3 %reshape_reshape.7 = f32[27,32,256]{2,1,0:T(8,128)} reshape(f32[32,27,256]{2,1,0:T(8,128)} %all-to-all-done.2) | data formatting | bytes 1769472 | tf_op jit(solution)/shard_map/reshape;reshape | solution.py:202
  (35 shorter events, 3.5 us)
Async XLA Ops:
  0.6 23.9 %copy-start = (bf16[27,32,256]{2,1,0:T(8,128)(2,1)S(1)}, bf16[27,32,256]{2,1,0:T(8,128)(2,1)}, u32[]{:S(2)}) copy-start(bf16[27,32,256]{2,1,0:T(8,128)(2,1)} %param.4) | copy-start | bytes 1327108
  0.6 15.7 %copy-start.4 = (bf16[1,32,2048]{2,1,0:T(8,128)(2,1)S(1)}, bf16[1,32,2048]{2,1,0:T(8,128)(2,1)}, u32[]{:S(2)}) copy-start(bf16[1,32,2048]{2,1,0:T(8,128)(2,1)} %param.3) | copy-start | bytes 393220
  0.7 15.6 %collective-permute-start = (bf16[1,32,2048]{2,1,0:T(8,128)(2,1)}, bf16[1,32,2048]{2,1,0:T(8,128)(2,1)S(1)}, u32[]{:S(2)}, u32[]{:S(2)}) collective-permute-start(bf16[1,32,2048]{2,1,0:T(8,128)(2,1)} %param.3), channel_id=1, source_target_pairs={{0,8},{8,16},{16,24},{24,32},{32,40},{40,48},{48,56},{56,64},{64,7... | collective-permute-start | bytes 393224 | tf_op jit(solution)/shard_map/ppermute | solution.py:17
  5.7 10.6 %collective-permute-start.1 = (bf16[1,32,2048]{2,1,0:T(8,128)(2,1)}, bf16[1,32,2048]{2,1,0:T(8,128)(2,1)S(1)}, u32[]{:S(2)}, u32[]{:S(2)}) collective-permute-start(bf16[1,32,2048]{2,1,0:T(8,128)(2,1)} %param.3), channel_id=1, source_target_pairs={{8,0},{16,8},{24,16},{32,24},{40,32},{48,40},{56,48},{64,56},{72,6... | collective-permute-start | bytes 393224 | tf_op jit(solution)/shard_map/ppermute | solution.py:20
  9.6 27.5 %all-to-all-start = ((bf16[8,1,32,2048]{3,2,1,0:T(8,128)(2,1)}), bf16[8,1,32,2048]{3,2,1,0:T(8,128)(2,1)S(1)}, u32[]{:S(2)}, u32[]{:S(2)}) async-start(bf16[8,1,32,2048]{3,2,1,0:T(8,128)(2,1)} %broadcast_in_dim.7), calls=%async_computation | async-start | bytes 2097152 | tf_op jit(solution)/shard_map/all_to_all | solution.py:186
  16.4 0.8 copy-start.2
  21.1 3.5 %copy-start.5 = (pred[8,9]{0,1:T(8,128)(4,1)S(1)}, pred[8,9]{0,1:T(8,128)(4,1)}, u32[]{:S(2)}) copy-start(pred[8,9]{0,1:T(8,128)(4,1)} %constant.72) | copy-start | bytes 220
  24.6 4.0 %copy-start.3 = (bf16[3,32,2048]{2,1,0:T(8,128)(2,1)S(1)}, bf16[3,32,2048]{2,1,0:T(8,128)(2,1)}, u32[]{:S(2)}) copy-start(bf16[3,32,2048]{2,1,0:T(8,128)(2,1)} %copy-done.2) | copy-start | bytes 1179652
  31.6 1.3 copy-start.1
  34.2 48.1 %collective-permute-start.2 = (f32[1,128,2048]{1,2,0:T(8,128)}, f32[1,128,2048]{1,2,0:T(8,128)}, u32[]{:S(2)}, u32[]{:S(2)}) collective-permute-start(f32[1,128,2048]{1,2,0:T(8,128)} %slice_select_fusion.2), channel_id=1, source_target_pairs={{0,4},{1,5},{2,6},{3,7},{4,0},{5,1},{6,2},{7,3},{8,12},{9,13},{10,... | collective-permute-start | bytes 3145736 | tf_op jit(solution)/shard_map/ppermute | solution.py:40
  48.0 56.5 %all-to-all-start.1 = ((f32[32,27,256]{2,1,0:T(8,128)}), f32[32,27,256]{2,1,0:T(8,128)}, u32[]{:S(2)}, u32[]{:S(2)}) async-start(f32[32,27,256]{2,1,0:T(8,128)} %reshape_reshape.6), calls=%async_computation.1 | async-start | bytes 2097152 | tf_op jit(solution)/shard_map/all_to_all | solution.py:179
  76.2 43.6 %collective-permute-start.5 = (f32[1,32,2048]{2,1,0:T(8,128)}, f32[1,32,2048]{2,1,0:T(8,128)}, u32[]{:S(2)}, u32[]{:S(2)}) collective-permute-start(f32[1,32,2048]{2,1,0:T(8,128)} %slice.45), channel_id=1, source_target_pairs={{0,8},{8,16},{16,24},{24,32},{32,40},{40,48},{48,56},{56,64},{64,7... | collective-permute-start | bytes 786440 | tf_op jit(solution)/shard_map/ppermute | solution.py:136
  87.9 14.2 %collective-permute-start.3 = (f32[1,64,2048]{2,1,0:T(8,128)}, f32[1,64,2048]{2,1,0:T(8,128)}, u32[]{:S(2)}, u32[]{:S(2)}) collective-permute-start(f32[1,64,2048]{2,1,0:T(8,128)} %copy.41), channel_id=1, source_target_pairs={{0,2},{1,3},{2,0},{3,1},{4,6},{5,7},{6,4},{7,5},{8,10},{9,11},{10,... | collective-permute-start | bytes 1572872 | tf_op jit(solution)/shard_map/ppermute | solution.py:40
  93.3 26.6 %collective-permute-start.6 = (f32[1,32,2048]{2,1,0:T(8,128)}, f32[1,32,2048]{2,1,0:T(8,128)}, u32[]{:S(2)}, u32[]{:S(2)}) collective-permute-start(f32[1,32,2048]{2,1,0:T(8,128)} %slice.47), channel_id=1, source_target_pairs={{8,0},{16,8},{24,16},{32,24},{40,32},{48,40},{56,48},{64,56},{72,6... | collective-permute-start | bytes 786440 | tf_op jit(solution)/shard_map/ppermute | solution.py:137
  106.9 33.9 %all-to-all-start.2 = ((f32[32,27,256]{2,1,0:T(8,128)}), f32[32,27,256]{2,1,0:T(8,128)}, u32[]{:S(2)}, u32[]{:S(2)}) async-start(f32[32,27,256]{2,1,0:T(8,128)} %broadcast_in_dim.16), calls=%async_computation.2 | async-start | bytes 2097152 | tf_op jit(solution)/shard_map/all_to_all | solution.py:186
  116.5 14.2 %collective-permute-start.4 = (f32[1,32,2048]{2,1,0:T(8,128)S(1)}, f32[1,32,2048]{2,1,0:T(8,128)S(1)}, u32[]{:S(2)}, u32[]{:S(2)}) collective-permute-start(f32[1,32,2048]{2,1,0:T(8,128)S(1)} %copy.43), channel_id=1, source_target_pairs={{0,1},{1,0},{2,3},{3,2},{4,5},{5,4},{6,7},{7,6},{8,9},{9,8},{10,11... | collective-permute-start | bytes 786440 | tf_op jit(solution)/shard_map/ppermute | solution.py:40

commit v3 on v2

--- a/solution.py
+++ b/solution.py
@@ -189,26 +189,33 @@
     return copies.reshape(shape[:dim] + (count * shape[dim],) + shape[dim + 1 :])
 
 
+SPACE = ("srest", "core")
+
+
 def local(inputs, weights, cotangent):
-    padded = extended(inputs, (("space", 0),), 1)
+    padded = extended(inputs, ((SPACE, 0),), 1)
     partial_out = conv_forward(padded, weights)
     chan_masks = partner_masks(lax.axis_size("chan"), 1)[::-1]
     output = halving_sum(partial_out, "chan", chan_masks, 1).astype(jnp.bfloat16)
     gathered = spread_gather(cotangent, "chan", 1)
-    input_grad = spill_sum(conv_backward(gathered, weights), "space").astype(jnp.bfloat16)
+    input_grad = spill_sum(conv_backward(gathered, weights), SPACE).astype(jnp.bfloat16)
     local_terms = conv_filter(padded, gathered)
     flat = local_terms.reshape(-1, local_terms.shape[-1])
-    flat = spread_gather(scatter_sum(flat, "space", 0), "space", 0)
+    flat = halving_sum(flat, "core", [1], 0)
+    flat = spread_gather(scatter_sum(flat, "srest", 0), "srest", 0)
+    flat = doubling_gather(flat, "core", [1], 0)
     weight_grad = flat.reshape(local_terms.shape)
     return (output, input_grad, weight_grad)
 
 
 def solution(mesh):
-    placed = (P("space", "chan", None), P(None, "chan", None), P("space", "chan", None))
+    space, chan = mesh.devices.shape
+    split = jax.sharding.Mesh(mesh.devices.reshape(space // 2, 2, chan), SPACE + ("chan",))
+    placed = (P(SPACE, "chan", None), P(None, "chan", None), P(SPACE, "chan", None))
     return jax.shard_map(
         local,
-        mesh=mesh,
+        mesh=split,
         in_specs=placed,
-        out_specs=(P("space", "chan", None), P("space", "chan", None), P(None, "chan", None)),
+        out_specs=(P(SPACE, "chan", None), P(SPACE, "chan", None), P(None, "chan", None)),
         check_vma=False,
     )

time: 146 us -> 135 us (0.925); the launches traced: 143 us -> 134 us
  waiting for transfers between devices: 23.4 us -> 9.81 us
  other arithmetic: 9.76 us -> 15.3 us
    all_to_all x2, waiting for transfers between devices: 8.67 us -> 0.01 us  [spread_gather(): copies = lax.all_to_all(copies, axis, 0, 0, tiled=True)]
    ppermute x3 -> x4, waiting for transfers between devices: 14.7 us -> 8.5 us  [halving_sum(): lax.ppermute(send, axis, [(i, i ^ mask) for i in range(count)])]
    another operation x2 -> x0, local copies, waits for them, and re-layouts: 4.53 us -> none  [the longest x1 2.28 us: scatter_sum(): block.reshape(shape[:dim] + (count, shape[dim] // count) + shape[dim + 1:])]
    all_to_all x1, starting transfers between devices: 11 us -> 8.31 us  [scatter_sum(): parts = lax.all_to_all(parts, axis, 0, 0, tiled=True)]
    reshape x0 -> x2, local copies, waits for them, and re-layouts: none -> 1.92 us  [the longest x1 1.86 us: scatter_sum(): block.reshape(shape[:dim] + (count, shape[dim] // count) + shape[dim + 1:])]
    select_n x3 -> x4, other arithmetic: 2.83 us -> 4.72 us  [halving_sum(): send = jnp.where(upper, low, high)]
    add x2 -> x3, other arithmetic: 3.57 us -> 5.43 us  [halving_sum(): keep + lax.ppermute(send, axis, [(i, i ^ mask) for i in range(count)])]
    ppermute x0 -> x1, starting transfers between devices: none -> 1.81 us  [doubling_gather(): other = lax.ppermute(block, axis, [(i, i ^ mask) for i in range(count)])]
  transfers between devices with their start and end apart: 10 -> 12, of which waited for: 3 -> 3; matrix products, arithmetic and copies ran while one was open for 45% -> 51% of each run, Pallas kernels for 5% -> 5%
where the time goes in v3:
time: 135 us; the launch traced here: 134 us
  local copies, waits for them, and re-layouts  46.6 us (35%)
  starting transfers between devices  44.4 us (33%)
  other arithmetic  15.3 us (11%)
  waiting for transfers between devices  9.81 us (7%)
  matrix products  9.7 us (7%)
  Pallas kernels  7.28 us (5%)
    all_to_all x2, starting transfers between devices, spread_gather(): copies = lax.all_to_all(copies, axis, 0, 0, tiled=True)  13.5 us
    ppermute x4, waiting for transfers between devices, halving_sum(): lax.ppermute(send, axis, [(i, i ^ mask) for i in range(count)])  8.5 us
    all_to_all x1, starting transfers between devices, scatter_sum(): parts = lax.all_to_all(parts, axis, 0, 0, tiled=True)  8.31 us
    pallas_call x1, Pallas kernels, conv_filter(): pl.pallas_call(filter_kernel, out_shape=jax.ShapeDtypeStruct((27, channel...  7.28 us
    ppermute x4, starting transfers between devices, halving_sum(): lax.ppermute(send, axis, [(i, i ^ mask) for i in range(count)])  6.54 us
    unnamed x18, local copies, waits for them, and re-layouts  6.33 us
    conv_general_dilated x1, matrix products, conv_backward(): lax.conv_general_dilated(lhs, rhs, (1, 1, 1), [(2, 2), (1, 1), (1, 1)], d...  5.76 us
    conv_general_dilated x5, local copies, waits for them, and re-layouts, conv_forward(): lax.conv_general_dilated(lhs, rhs, (1, 1, 1), [(0, 0), (1, 1), (1, 1)], d...  5.68 us
  transfers between devices with their start and end apart: 12, of which 3 were waited for; matrix products, arithmetic and copies ran while one was open for 51% of the time, Pallas kernels for 5%

profile of v3, /device:TPU:1, one launch (start us, length us, event | category | flops | bytes accessed | tf_op | source)
XLA Modules:
  0.0 134.2 jit_solution(7886623044007342991)
XLA Ops:
  0.7 5.1 %collective-permute-start = (bf16[1,32,2048]{2,1,0:T(8,128)(2,1)}, bf16[1,32,2048]{2,1,0:T(8,128)(2,1)S(1)}, u32[]{:S(2)}, u32[]{:S(2)}) collective-permute-start(bf16[1,32,2048]{2,1,0:T(8,128)(2,1)} %param.3), channel_id=1, source_target_pairs={{0,8},{8,16},{16,24},{24,32},{32,40},{40,48},{48,56},{56,64},{64,7... | collective-permute-start | bytes 393224 | tf_op jit(solution)/shard_map/ppermute | solution.py:17
  5.7 1.9 %collective-permute-start.1 = (bf16[1,32,2048]{2,1,0:T(8,128)(2,1)}, bf16[1,32,2048]{2,1,0:T(8,128)(2,1)S(1)}, u32[]{:S(2)}, u32[]{:S(2)}) collective-permute-start(bf16[1,32,2048]{2,1,0:T(8,128)(2,1)} %param.3), channel_id=1, source_target_pairs={{8,0},{16,8},{24,16},{32,24},{40,32},{48,40},{56,48},{64,56},{72,6... | collective-permute-start | bytes 393224 | tf_op jit(solution)/shard_map/ppermute | solution.py:20
  7.6 2.0 %broadcast_in_dim.7 = bf16[8,1,32,2048]{3,2,1,0:T(8,128)(2,1)} broadcast(bf16[32,2048]{1,0:T(8,128)(2,1)} %bitcast.54), dimensions={2,3} | broadcast | bytes 1179648 | tf_op jit(solution)/shard_map/broadcast_in_dim | solution.py:185
  9.6 6.7 %all-to-all-start = ((bf16[8,1,32,2048]{3,2,1,0:T(8,128)(2,1)}), bf16[8,1,32,2048]{3,2,1,0:T(8,128)(2,1)S(1)}, u32[]{:S(2)}, u32[]{:S(2)}) async-start(bf16[8,1,32,2048]{3,2,1,0:T(8,128)(2,1)} %broadcast_in_dim.7), calls=%async_computation | async-start | bytes 2097152 | tf_op jit(solution)/shard_map/all_to_all | solution.py:186
  17.2 2.1 %copy.36 = bf16[3,32,32,1,64]{2,1,4,0,3:T(8,128)(2,1)} copy(bf16[3,32,32,1,64]{4,2,1,0,3:T(8,128)(2,1)S(1)} %reshape.61) | data formatting | bytes 786432 | tf_op jit(solution)/shard_map/reshape | solution.py:110
  19.3 1.8 %pad.5 = bf16[3,32,32,1,72]{2,1,4,0,3:T(8,128)(2,1)S(1)} pad(bf16[3,32,32,1,64]{2,1,4,0,3:T(8,128)(2,1)} %copy.36, bf16[]{:T(256)} %constant.78.clone.1), padding=0_0x0_0x0_0x0_0x1_7 | pad | bytes 835586 | tf_op jit(solution)/shard_map/reshape | solution.py:110
  21.1 2.4 %copy.38 = bf16[3,32,32,1,8,9]{1,4,5,2,0,3:T(8,128)(2,1)} copy(bf16[3,32,32,1,8,9]{2,1,5,4,0,3:T(8,128)(2,1)S(1)} %bitcast.47) | data formatting | bytes 884736 | tf_op jit(solution)/shard_map/conv_general_dilated | solution.py:112
  23.4 1.1 slice.65
  24.6 3.9 %fusion.9 = f32[1,32,8,9,256]{4,2,3,1,0:T(8,128)S(1)} fusion(bf16[3,3,3,32,256]{4,3,2,1,0:T(8,128)(2,1)S(1)} %bitcast.39, bf16[3,32,32,1,7,2]{1,4,5,2,0,3:T(8,128)(2,1)S(1)} %slice.65, bf16[3,32,32,1,8,9]{1,4,5,2,0,3:T(8,128)(2,1)} %copy.38, pred[8,9]{0,1:T(8,128)(4,1)S(1)} %copy-done.6), kind=kOutput, calls=%fused_computation.12 | convolution fusion | flops 1000194048 | bytes 3330120 | tf_op jit(solution)/shard_map/conv_general_dilated | solution.py:112
  30.3 1.2 copy.40
  31.6 1.3 copy-done.1
  32.9 1.1 slice_select_fusion.2
  34.0 3.0 %collective-permute-start.2 = (f32[1,128,2048]{1,2,0:T(8,128)}, f32[1,128,2048]{1,2,0:T(8,128)}, u32[]{:S(2)}, u32[]{:S(2)}) collective-permute-start(f32[1,128,2048]{1,2,0:T(8,128)} %slice_select_fusion.2), channel_id=1, source_target_pairs={{0,4},{1,5},{2,6},{3,7},{4,0},{5,1},{6,2},{7,3},{8,12},{9,13},{10,... | collective-permute-start | bytes 3145736 | tf_op jit(solution)/shard_map/ppermute | solution.py:40
  37.0 1.3 copy.54
  38.3 7.3 %shard_map.58 = f32[27,32,256]{2,1,0:T(8,128)} custom-call(bf16[3,32,2304]{2,1,0:T(8,128)(2,1)} %pad.4.x_ref, bf16[2048,256]{1,0:T(8,128)(2,1)} %bitcast.52), custom_call_target="tpu_custom_call" | custom-call | tf_op jit(solution)/shard_map/pallas_call | solution.py:168
  45.6 1.9 %slice_select_fusion.3 = f32[432,256]{1,0:T(8,128)} fusion(f32[864,256]{1,0:T(8,128)} %bitcast.45, pred[]{:T(512)S(6)} %eq.22), kind=kLoop, calls=%fused_computation.31 | loop fusion | flops 110592 | bytes 1327105 | tf_op jit(solution)/shard_map/jit(_where)/select_n | solution.py:39
  47.5 3.1 %reshape.65 = bf16[1,256,32,1,64]{4,2,1,3,0:T(8,128)(2,1)} reshape(bf16[8,1,32,2048]{3,2,1,0:T(8,128)(2,1)S(1)} %all-to-all-done) | data formatting | bytes 2097152 | tf_op jit(solution)/shard_map/reshape;reshape;transpose | solution.py:122
  50.6 4.1 %copy.56 = bf16[1,256,32,1,64]{1,2,4,3,0:T(8,128)(2,1)S(1)} copy(bf16[1,256,32,1,64]{4,2,1,3,0:T(8,128)(2,1)} %reshape.65) | data formatting | bytes 2097152
  55.6 5.8 %convolution_select_fusion = f32[3,32,8,9,32]{4,2,3,1,0:T(8,128)S(1)} fusion(bf16[3,3,3,32,256]{4,3,2,1,0:T(8,128)(2,1)S(1)} %bitcast.40, pred[8,9]{0,1:T(8,128)(4,1)S(1)} %copy-done.6, bf16[1,256,32,1,7,2]{1,4,5,2,3,0:T(8,128)(2,1)S(1)} %slice.73, bf16[1,256,32,1,8,9]{1,4,5,2,3,0:T(8,128)(2,1)S(1)} %copy.47), kind=kOutput, calls=%fused_computation.11 | convolution fusion | flops 1002528768 | bytes 2736200 | tf_op jit(solution)/shard_map/conv_general_dilated | solution.py:124
  61.4 1.3 fusion.26
  63.7 0.9 slice.51
  64.6 4.5 %collective-permute-start.5 = (f32[1,32,2048]{2,1,0:T(8,128)}, f32[1,32,2048]{2,1,0:T(8,128)}, u32[]{:S(2)}, u32[]{:S(2)}) collective-permute-start(f32[1,32,2048]{2,1,0:T(8,128)} %slice.51), channel_id=1, source_target_pairs={{0,8},{8,16},{16,24},{24,32},{32,40},{40,48},{48,56},{56,64},{64,7... | collective-permute-start | bytes 786440 | tf_op jit(solution)/shard_map/ppermute | solution.py:136
  69.1 2.5 %copy.52 = f32[1,32,8,9,32]{4,1,3,2,0:T(8,128)} copy(f32[1,32,8,9,32]{4,2,3,1,0:T(8,128)} %get-tuple-element.13) | data formatting | bytes 589824 | tf_op jit(solution)/shard_map/conv_general_dilated | solution.py:124
  71.6 2.0 %select_add_fusion.1 = f32[1,128,2048]{1,2,0:T(8,128)S(1)} fusion(f32[1,128,2048]{1,2,0:T(8,128)} %collective-permute-done.2, f32[1,256,2048]{1,2,0:T(8,128)} %bitcast.42, pred[]{:T(512)S(6)} %eq.21), kind=kLoop, calls=%fused_computation.24 | loop fusion | flops 524288 | bytes 4194305 | tf_op jit(solution)/shard_map/add | solution.py:40
  73.6 1.3 slice_select_fusion.1
  75.0 2.3 %copy.41 = f32[1,64,2048]{2,1,0:T(8,128)} copy(f32[1,64,2048]{1,2,0:T(8,128)} %slice_select_fusion.1) | data formatting | bytes 1048576 | tf_op jit(solution)/shard_map/jit(_where)/select_n | solution.py:39
  77.6 1.9 %select_add_fusion.2 = f32[432,256]{1,0:T(8,128)} fusion(f32[432,256]{1,0:T(8,128)} %collective-permute-done.7, f32[864,256]{1,0:T(8,128)S(1)} %bitcast.46, pred[]{:T(512)S(6)} %eq.22), kind=kLoop, calls=%fused_computation.30 | loop fusion | flops 221184 | bytes 1769473 | tf_op jit(solution)/shard_map/add | solution.py:40
  79.5 1.9 %reshape.40 = f32[16,27,256]{2,1,0:T(8,128)} reshape(f32[432,256]{1,0:T(8,128)} %select_add_fusion.2) | data formatting | bytes 884736 | tf_op jit(solution)/shard_map/reshape | solution.py:177
  81.3 8.3 %all-to-all-start.1 = ((f32[16,27,256]{2,1,0:T(8,128)}), f32[16,27,256]{2,1,0:T(8,128)}, u32[]{:S(2)}, u32[]{:S(2)}) async-start(f32[16,27,256]{2,1,0:T(8,128)} %reshape.40), calls=%async_computation.1 | async-start | bytes 1048576 | tf_op jit(solution)/shard_map/all_to_all | solution.py:179
  89.6 2.3 %slice_bitcast_fusion.1 = f32[1,1,32,32,64]{2,3,4,0,1:T(8,128)} fusion(f32[1,32,1,72,32]{4,1,3,2,0:T(8,128)} %bitcast.49), kind=kLoop, calls=%fused_computation.19 | loop fusion | bytes 524288 | tf_op jit(solution)/shard_map/slice | solution.py:137
  91.9 1.9 %copy.53 = f32[1,1,32,32,64]{4,3,2,1,0:T(8,128)S(1)} copy(f32[1,1,32,32,64]{2,3,4,0,1:T(8,128)} %slice_bitcast_fusion.1) | data formatting | bytes 524288 | tf_op jit(solution)/shard_map/slice | solution.py:137
  93.9 0.9 slice.53
  94.7 2.8 %collective-permute-start.6 = (f32[1,32,2048]{2,1,0:T(8,128)}, f32[1,32,2048]{2,1,0:T(8,128)}, u32[]{:S(2)}, u32[]{:S(2)}) collective-permute-start(f32[1,32,2048]{2,1,0:T(8,128)} %slice.53), channel_id=1, source_target_pairs={{8,0},{16,8},{24,16},{32,24},{40,32},{48,40},{56,48},{64,56},{72,6... | collective-permute-start | bytes 786440 | tf_op jit(solution)/shard_map/ppermute | solution.py:137
  98.8 2.4 %copy.42 = f32[1,64,2048]{1,2,0:T(8,128)} copy(f32[1,64,2048]{2,1,0:T(8,128)} %collective-permute-done.3) | data formatting | bytes 1048576 | tf_op jit(solution)/shard_map/ppermute | solution.py:40
  101.2 1.6 %select_add_fusion = f32[1,64,2048]{1,2,0:T(8,128)S(1)} fusion(f32[1,64,2048]{1,2,0:T(8,128)} %copy.42, f32[1,128,2048]{1,2,0:T(8,128)S(1)} %select_add_fusion.1, pred[]{:T(512)S(6)} %eq.20), kind=kLoop, calls=%fused_computation.23 | loop fusion | flops 262144 | bytes 2097153 | tf_op jit(solution)/shard_map/add | solution.py:40
  102.8 0.9 all-to-all-done.1
  103.7 1.1 reduce_sum.9
  104.8 0.8 broadcast_in_dim.16
  105.6 6.9 %all-to-all-start.2 = ((f32[16,27,256]{2,1,0:T(8,128)}), f32[16,27,256]{2,1,0:T(8,128)S(1)}, u32[]{:S(2)}, u32[]{:S(2)}) async-start(f32[16,27,256]{2,1,0:T(8,128)} %broadcast_in_dim.16), calls=%async_computation.2 | async-start | bytes 1048576 | tf_op jit(solution)/shard_map/all_to_all | solution.py:186
  112.8 1.0 copy.43
  113.9 3.3 %collective-permute-start.4 = (f32[1,32,2048]{2,1,0:T(8,128)}, f32[1,32,2048]{2,1,0:T(8,128)}, u32[]{:S(2)}, u32[]{:S(2)}) collective-permute-start(f32[1,32,2048]{2,1,0:T(8,128)} %copy.43), channel_id=1, source_target_pairs={{0,1},{1,0},{2,3},{3,2},{4,5},{5,4},{6,7},{7,6},{8,9},{9,8},{10,11... | collective-permute-start | bytes 786440 | tf_op jit(solution)/shard_map/ppermute | solution.py:40
  117.2 1.7 %add_convert_fusion.1 = bf16[1,32,2048]{2,1,0:T(8,128)(2,1)} fusion(f32[1,32,2048]{2,1,0:T(8,128)} %collective-permute-done.6, f32[1,32,2048]{2,1,0:T(8,128)S(1)} %slice.49, f32[1,32,2048]{2,1,0:T(8,128)} %collective-permute-done.5), kind=kLoop, calls=%fused_computation.32 | loop fusion | flops 196608 | bytes 917504 | tf_op jit(solution)/shard_map/convert_element_type | solution.py:201
  118.9 8.5 %collective-permute-done.4 = f32[1,32,2048]{2,1,0:T(8,128)} collective-permute-done((f32[1,32,2048]{2,1,0:T(8,128)}, f32[1,32,2048]{2,1,0:T(8,128)}, u32[]{:S(2)}, u32[]{:S(2)}) %collective-permute-start.4) | collective-permute-done | bytes 262176 | tf_op jit(solution)/shard_map/ppermute | solution.py:40
  127.4 1.3 copy.44
  128.7 1.8 %collective-permute-start.8 = (f32[432,256]{1,0:T(8,128)S(1)}, f32[432,256]{1,0:T(8,128)}, u32[]{:S(2)}, u32[]{:S(2)}) collective-permute-start(f32[432,256]{1,0:T(8,128)S(1)} %reshape.41), channel_id=1, source_target_pairs={{0,8},{8,0},{1,9},{9,1},{2,10},{10,2},{3,11},{11,3},{4,12},{12,4},... | collective-permute-start | bytes 1327112 | tf_op jit(solution)/shard_map/ppermute | solution.py:49
  130.9 0.8 copy.55
  132.1 1.1 broadcast_select_fusion.1
  133.2 1.0 pad_maximum_fusion
  (45 shorter events, 7.2 us)
Async XLA Ops:
  0.6 23.9 %copy-start = (bf16[27,32,256]{2,1,0:T(8,128)(2,1)S(1)}, bf16[27,32,256]{2,1,0:T(8,128)(2,1)}, u32[]{:S(2)}) copy-start(bf16[27,32,256]{2,1,0:T(8,128)(2,1)} %param.4) | copy-start | bytes 1327108
  0.6 15.7 %copy-start.5 = (bf16[1,32,2048]{2,1,0:T(8,128)(2,1)S(1)}, bf16[1,32,2048]{2,1,0:T(8,128)(2,1)}, u32[]{:S(2)}) copy-start(bf16[1,32,2048]{2,1,0:T(8,128)(2,1)} %param.3) | copy-start | bytes 393220
  0.7 15.6 %collective-permute-start = (bf16[1,32,2048]{2,1,0:T(8,128)(2,1)}, bf16[1,32,2048]{2,1,0:T(8,128)(2,1)S(1)}, u32[]{:S(2)}, u32[]{:S(2)}) collective-permute-start(bf16[1,32,2048]{2,1,0:T(8,128)(2,1)} %param.3), channel_id=1, source_target_pairs={{0,8},{8,16},{16,24},{24,32},{32,40},{40,48},{48,56},{56,64},{64,7... | collective-permute-start | bytes 393224 | tf_op jit(solution)/shard_map/ppermute | solution.py:17
  5.7 10.6 %collective-permute-start.1 = (bf16[1,32,2048]{2,1,0:T(8,128)(2,1)}, bf16[1,32,2048]{2,1,0:T(8,128)(2,1)S(1)}, u32[]{:S(2)}, u32[]{:S(2)}) collective-permute-start(bf16[1,32,2048]{2,1,0:T(8,128)(2,1)} %param.3), channel_id=1, source_target_pairs={{8,0},{16,8},{24,16},{32,24},{40,32},{48,40},{56,48},{64,56},{72,6... | collective-permute-start | bytes 393224 | tf_op jit(solution)/shard_map/ppermute | solution.py:20
  9.6 27.3 %all-to-all-start = ((bf16[8,1,32,2048]{3,2,1,0:T(8,128)(2,1)}), bf16[8,1,32,2048]{3,2,1,0:T(8,128)(2,1)S(1)}, u32[]{:S(2)}, u32[]{:S(2)}) async-start(bf16[8,1,32,2048]{3,2,1,0:T(8,128)(2,1)} %broadcast_in_dim.7), calls=%async_computation | async-start | bytes 2097152 | tf_op jit(solution)/shard_map/all_to_all | solution.py:186
  16.4 0.8 copy-start.3
  21.1 3.5 %copy-start.6 = (pred[8,9]{0,1:T(8,128)(4,1)S(1)}, pred[8,9]{0,1:T(8,128)(4,1)}, u32[]{:S(2)}) copy-start(pred[8,9]{0,1:T(8,128)(4,1)} %constant.92) | copy-start | bytes 220
  24.6 4.0 %copy-start.4 = (bf16[3,32,2048]{2,1,0:T(8,128)(2,1)S(1)}, bf16[3,32,2048]{2,1,0:T(8,128)(2,1)}, u32[]{:S(2)}) copy-start(bf16[3,32,2048]{2,1,0:T(8,128)(2,1)} %copy-done.3) | copy-start | bytes 1179652
  31.6 1.3 copy-start.1
  34.0 37.6 %collective-permute-start.2 = (f32[1,128,2048]{1,2,0:T(8,128)}, f32[1,128,2048]{1,2,0:T(8,128)}, u32[]{:S(2)}, u32[]{:S(2)}) collective-permute-start(f32[1,128,2048]{1,2,0:T(8,128)} %slice_select_fusion.2), channel_id=1, source_target_pairs={{0,4},{1,5},{2,6},{3,7},{4,0},{5,1},{6,2},{7,3},{8,12},{9,13},{10,... | collective-permute-start | bytes 3145736 | tf_op jit(solution)/shard_map/ppermute | solution.py:40
  47.5 30.1 %collective-permute-start.7 = (f32[432,256]{1,0:T(8,128)}, f32[432,256]{1,0:T(8,128)}, u32[]{:S(2)}, u32[]{:S(2)}) collective-permute-start(f32[432,256]{1,0:T(8,128)} %slice_select_fusion.3), channel_id=1, source_target_pairs={{0,8},{8,0},{1,9},{9,1},{2,10},{10,2},{3,11},{11,3},{4,12},{12,4},... | collective-permute-start | bytes 1327112 | tf_op jit(solution)/shard_map/ppermute | solution.py:40
  64.6 52.6 %collective-permute-start.5 = (f32[1,32,2048]{2,1,0:T(8,128)}, f32[1,32,2048]{2,1,0:T(8,128)}, u32[]{:S(2)}, u32[]{:S(2)}) collective-permute-start(f32[1,32,2048]{2,1,0:T(8,128)} %slice.51), channel_id=1, source_target_pairs={{0,8},{8,16},{16,24},{24,32},{32,40},{40,48},{48,56},{56,64},{64,7... | collective-permute-start | bytes 786440 | tf_op jit(solution)/shard_map/ppermute | solution.py:136
  73.6 4.0 %copy-start.2 = (f32[27,32,256]{2,1,0:T(8,128)S(1)}, f32[27,32,256]{2,1,0:T(8,128)}, u32[]{:S(2)}) copy-start(f32[27,32,256]{2,1,0:T(8,128)} %shard_map.58) | copy-start | bytes 2654212
  77.3 21.5 %collective-permute-start.3 = (f32[1,64,2048]{2,1,0:T(8,128)}, f32[1,64,2048]{2,1,0:T(8,128)}, u32[]{:S(2)}, u32[]{:S(2)}) collective-permute-start(f32[1,64,2048]{2,1,0:T(8,128)} %copy.41), channel_id=1, source_target_pairs={{0,2},{1,3},{2,0},{3,1},{4,6},{5,7},{6,4},{7,5},{8,10},{9,11},{10,... | collective-permute-start | bytes 1572872 | tf_op jit(solution)/shard_map/ppermute | solution.py:40
  81.3 22.4 %all-to-all-start.1 = ((f32[16,27,256]{2,1,0:T(8,128)}), f32[16,27,256]{2,1,0:T(8,128)}, u32[]{:S(2)}, u32[]{:S(2)}) async-start(f32[16,27,256]{2,1,0:T(8,128)} %reshape.40), calls=%async_computation.1 | async-start | bytes 1048576 | tf_op jit(solution)/shard_map/all_to_all | solution.py:179
  94.7 22.4 %collective-permute-start.6 = (f32[1,32,2048]{2,1,0:T(8,128)}, f32[1,32,2048]{2,1,0:T(8,128)}, u32[]{:S(2)}, u32[]{:S(2)}) collective-permute-start(f32[1,32,2048]{2,1,0:T(8,128)} %slice.53), channel_id=1, source_target_pairs={{8,0},{16,8},{24,16},{32,24},{40,32},{48,40},{56,48},{64,56},{72,6... | collective-permute-start | bytes 786440 | tf_op jit(solution)/shard_map/ppermute | solution.py:137
  105.6 23.0 %all-to-all-start.2 = ((f32[16,27,256]{2,1,0:T(8,128)}), f32[16,27,256]{2,1,0:T(8,128)S(1)}, u32[]{:S(2)}, u32[]{:S(2)}) async-start(f32[16,27,256]{2,1,0:T(8,128)} %broadcast_in_dim.16), calls=%async_computation.2 | async-start | bytes 1048576 | tf_op jit(solution)/shard_map/all_to_all | solution.py:186
  113.9 13.5 %collective-permute-start.4 = (f32[1,32,2048]{2,1,0:T(8,128)}, f32[1,32,2048]{2,1,0:T(8,128)}, u32[]{:S(2)}, u32[]{:S(2)}) collective-permute-start(f32[1,32,2048]{2,1,0:T(8,128)} %copy.43), channel_id=1, source_target_pairs={{0,1},{1,0},{2,3},{3,2},{4,5},{5,4},{6,7},{7,6},{8,9},{9,8},{10,11... | collective-permute-start | bytes 786440 | tf_op jit(solution)/shard_map/ppermute | solution.py:40
  128.7 3.4 %collective-permute-start.8 = (f32[432,256]{1,0:T(8,128)S(1)}, f32[432,256]{1,0:T(8,128)}, u32[]{:S(2)}, u32[]{:S(2)}) collective-permute-start(f32[432,256]{1,0:T(8,128)S(1)} %reshape.41), channel_id=1, source_target_pairs={{0,8},{8,0},{1,9},{9,1},{2,10},{10,2},{3,11},{11,3},{4,12},{12,4},... | collective-permute-start | bytes 1327112 | tf_op jit(solution)/shard_map/ppermute | solution.py:49

commit v4 on v3

--- a/solution.py
+++ b/solution.py
@@ -39,6 +39,17 @@
         send = jnp.where(upper, low, high)
         block = keep + lax.ppermute(send, axis, [(i, i ^ mask) for i in range(count)])
     return block
+
+
+def direct_sum(block, axis, dim):
+    count = lax.axis_size(axis)
+    index = lax.axis_index(axis)
+    width = block.shape[dim] // count
+    total = lax.dynamic_slice_in_dim(block, index * width, width, axis=dim)
+    for step in range(1, count):
+        send = lax.dynamic_slice_in_dim(block, (index ^ step) * width, width, axis=dim)
+        total = total + lax.ppermute(send, axis, [(i, i ^ step) for i in range(count)])
+    return total
 
 
 def doubling_gather(block, axis, masks, dim):
@@ -195,8 +206,7 @@
 def local(inputs, weights, cotangent):
     padded = extended(inputs, ((SPACE, 0),), 1)
     partial_out = conv_forward(padded, weights)
-    chan_masks = partner_masks(lax.axis_size("chan"), 1)[::-1]
-    output = halving_sum(partial_out, "chan", chan_masks, 1).astype(jnp.bfloat16)
+    output = direct_sum(partial_out, "chan", 1).astype(jnp.bfloat16)
     gathered = spread_gather(cotangent, "chan", 1)
     input_grad = spill_sum(conv_backward(gathered, weights), SPACE).astype(jnp.bfloat16)
     local_terms = conv_filter(padded, gathered)

time: 135 us -> 146 us (1.081)
  the two profiles are of different devices: /device:TPU:1 before, /device:TPU:24 now
where the time goes in v4:
time: 146 us; the launch traced here: 145 us
  local copies, waits for them, and re-layouts  58.3 us (40%)
  starting transfers between devices  49 us (34%)
  waiting for transfers between devices  13.5 us (9%)
  matrix products  9.65 us (7%)
  Pallas kernels  7.33 us (5%)
  other arithmetic  6.14 us (4%)
    dynamic_slice x8, local copies, waits for them, and re-layouts, direct_sum(): lax.dynamic_slice_in_dim(block, (index ^ step) * width, width, axis=dim)  20.8 us
    ppermute x7, starting transfers between devices, direct_sum(): lax.ppermute(send, axis, [(i, i ^ step) for i in range(count)])  13.3 us
    all_to_all x2, starting transfers between devices, spread_gather(): copies = lax.all_to_all(copies, axis, 0, 0, tiled=True)  13.1 us
    all_to_all x1, starting transfers between devices, scatter_sum(): parts = lax.all_to_all(parts, axis, 0, 0, tiled=True)  7.42 us
    ppermute x1, starting transfers between devices, extended(): lax.ppermute(lax.slice_in_dim(block, 0, width, axis=dim), axis, backward)  7.38 us
    pallas_call x1, Pallas kernels, conv_filter(): pl.pallas_call(filter_kernel, out_shape=jax.ShapeDtypeStruct((27, channel...  7.33 us
    all_to_all x1, waiting for transfers between devices, scatter_sum(): parts = lax.all_to_all(parts, axis, 0, 0, tiled=True)  6.76 us
    conv_general_dilated x6, local copies, waits for them, and re-layouts, conv_backward(): lax.conv_general_dilated(lhs, rhs, (1, 1, 1), [(2, 2), (1, 1), (1, 1)], d...  6.69 us
  transfers between devices with their start and end apart: 16, of which 4 were waited for; matrix products, arithmetic and copies ran while one was open for 48% of the time, Pallas kernels for 5%

profile of v4, /device:TPU:24, one launch (start us, length us, event | category | flops | bytes accessed | tf_op | source)
XLA Modules:
  0.0 144.9 jit_solution(16701890472073572983)
XLA Ops:
  0.7 2.1 %collective-permute-start = (bf16[1,32,2048]{2,1,0:T(8,128)(2,1)}, bf16[1,32,2048]{2,1,0:T(8,128)(2,1)S(1)}, u32[]{:S(2)}, u32[]{:S(2)}) collective-permute-start(bf16[1,32,2048]{2,1,0:T(8,128)(2,1)} %param.3), channel_id=1, source_target_pairs={{0,8},{8,16},{16,24},{24,32},{32,40},{40,48},{48,56},{56,64},{64,7... | collective-permute-start | bytes 393224 | tf_op jit(solution)/shard_map/ppermute | solution.py:17
  2.7 7.4 %collective-permute-start.1 = (bf16[1,32,2048]{2,1,0:T(8,128)(2,1)}, bf16[1,32,2048]{2,1,0:T(8,128)(2,1)S(1)}, u32[]{:S(2)}, u32[]{:S(2)}) collective-permute-start(bf16[1,32,2048]{2,1,0:T(8,128)(2,1)} %param.3), channel_id=1, source_target_pairs={{8,0},{16,8},{24,16},{32,24},{40,32},{48,40},{56,48},{64,56},{72,6... | collective-permute-start | bytes 393224 | tf_op jit(solution)/shard_map/ppermute | solution.py:20
  10.1 2.0 %broadcast_in_dim.7 = bf16[8,1,32,2048]{3,2,1,0:T(8,128)(2,1)} broadcast(bf16[32,2048]{1,0:T(8,128)(2,1)} %bitcast.53), dimensions={2,3} | broadcast | bytes 1179648 | tf_op jit(solution)/shard_map/broadcast_in_dim | solution.py:196
  12.1 7.3 %all-to-all-start = ((bf16[8,1,32,2048]{3,2,1,0:T(8,128)(2,1)}), bf16[8,1,32,2048]{3,2,1,0:T(8,128)(2,1)S(1)}, u32[]{:S(2)}, u32[]{:S(2)}) async-start(bf16[8,1,32,2048]{3,2,1,0:T(8,128)(2,1)} %broadcast_in_dim.7), calls=%async_computation | async-start | bytes 2097152 | tf_op jit(solution)/shard_map/all_to_all | solution.py:197
  20.3 2.1 %copy.66 = bf16[3,32,32,1,64]{2,1,4,0,3:T(8,128)(2,1)} copy(bf16[3,32,32,1,64]{4,2,1,0,3:T(8,128)(2,1)S(1)} %reshape.61) | data formatting | bytes 786432 | tf_op jit(solution)/shard_map/reshape | solution.py:121
  22.4 1.8 %pad.5 = bf16[3,32,32,1,72]{2,1,4,0,3:T(8,128)(2,1)S(1)} pad(bf16[3,32,32,1,64]{2,1,4,0,3:T(8,128)(2,1)} %copy.66, bf16[]{:T(256)} %constant.54.clone.1), padding=0_0x0_0x0_0x0_0x1_7 | pad | bytes 835586 | tf_op jit(solution)/shard_map/reshape | solution.py:121
  24.2 2.4 %copy.68 = bf16[3,32,32,1,8,9]{1,4,5,2,0,3:T(8,128)(2,1)} copy(bf16[3,32,32,1,8,9]{2,1,5,4,0,3:T(8,128)(2,1)S(1)} %bitcast.46) | data formatting | bytes 884736 | tf_op jit(solution)/shard_map/conv_general_dilated | solution.py:123
  26.5 1.1 slice.41
  27.7 3.9 %fusion.9 = f32[1,32,8,9,256]{4,2,3,1,0:T(8,128)S(1)} fusion(bf16[3,3,3,32,256]{4,3,2,1,0:T(8,128)(2,1)S(1)} %bitcast.39, bf16[3,32,32,1,7,2]{1,4,5,2,0,3:T(8,128)(2,1)S(1)} %slice.41, bf16[3,32,32,1,8,9]{1,4,5,2,0,3:T(8,128)(2,1)} %copy.68, pred[8,9]{0,1:T(8,128)(4,1)S(1)} %copy-done.11), kind=kOutput, calls=%fused_computation.12 | convolution fusion | flops 1000194048 | bytes 3330120 | tf_op jit(solution)/shard_map/conv_general_dilated | solution.py:123
  32.6 1.2 copy.70
  33.8 5.2 %constant_dynamic-slice_fusion.6 = (f32[1,32,2048]{1,2,0:T(8,128)}, f32[1,32,2048]{1,2,0:T(8,128)}, f32[1,32,2048]{1,2,0:T(8,128)}, f32[1,32,2048]{1,2,0:T(8,128...) fusion(f32[1,256,2048]{1,2,0:T(8,128)S(1)} %bitcast.41, ...), kind=kLoop, calls=%fused_computation.39 | loop fusion | bytes 4194336 | tf_op jit(solution)/shard_map/dynamic_slice | solution.py:50
  39.0 2.2 %copy.78 = f32[1,32,2048]{2,1,0:T(8,128)} copy(f32[1,32,2048]{1,2,0:T(8,128)} %get-tuple-element.16) | data formatting | bytes 524288 | tf_op jit(solution)/shard_map/dynamic_slice | solution.py:50
  41.2 2.7 %collective-permute-start.8 = (f32[1,32,2048]{2,1,0:T(8,128)}, f32[1,32,2048]{2,1,0:T(8,128)S(1)}, u32[]{:S(2)}, u32[]{:S(2)}) collective-permute-start(f32[1,32,2048]{2,1,0:T(8,128)} %copy.78), channel_id=1, source_target_pairs={{0,7},{1,6},{2,5},{3,4},{4,3},{5,2},{6,1},{7,0},{8,15},{9,14},{10,... | collective-permute-start | bytes 786440 | tf_op jit(solution)/shard_map/ppermute | solution.py:51
  43.9 2.2 %copy.77 = f32[1,32,2048]{2,1,0:T(8,128)} copy(f32[1,32,2048]{1,2,0:T(8,128)} %get-tuple-element.17) | data formatting | bytes 524288 | tf_op jit(solution)/shard_map/dynamic_slice | solution.py:50
  46.1 2.2 %copy.76 = f32[1,32,2048]{2,1,0:T(8,128)} copy(f32[1,32,2048]{1,2,0:T(8,128)} %get-tuple-element.18) | data formatting | bytes 524288 | tf_op jit(solution)/shard_map/dynamic_slice | solution.py:50
  48.4 4.7 %collective-permute-start.6 = (f32[1,32,2048]{2,1,0:T(8,128)}, f32[1,32,2048]{2,1,0:T(8,128)}, u32[]{:S(2)}, u32[]{:S(2)}) collective-permute-start(f32[1,32,2048]{2,1,0:T(8,128)} %copy.76), channel_id=1, source_target_pairs={{0,5},{1,4},{2,7},{3,6},{4,1},{5,0},{6,3},{7,2},{8,13},{9,12},{10,... | collective-permute-start | bytes 786440 | tf_op jit(solution)/shard_map/ppermute | solution.py:51
  53.1 2.2 %copy.75 = f32[1,32,2048]{2,1,0:T(8,128)} copy(f32[1,32,2048]{1,2,0:T(8,128)} %get-tuple-element.19) | data formatting | bytes 524288 | tf_op jit(solution)/shard_map/dynamic_slice | solution.py:50
  55.3 1.8 %collective-permute-start.5 = (f32[1,32,2048]{2,1,0:T(8,128)}, f32[1,32,2048]{2,1,0:T(8,128)}, u32[]{:S(2)}, u32[]{:S(2)}) collective-permute-start(f32[1,32,2048]{2,1,0:T(8,128)} %copy.75), channel_id=1, source_target_pairs={{0,4},{1,5},{2,6},{3,7},{4,0},{5,1},{6,2},{7,3},{8,12},{9,13},{10,... | collective-permute-start | bytes 786440 | tf_op jit(solution)/shard_map/ppermute | solution.py:51
  57.1 2.3 %copy.74 = f32[1,32,2048]{2,1,0:T(8,128)} copy(f32[1,32,2048]{1,2,0:T(8,128)} %get-tuple-element.20) | data formatting | bytes 524288 | tf_op jit(solution)/shard_map/dynamic_slice | solution.py:50
  59.6 2.2 %copy.73 = f32[1,32,2048]{2,1,0:T(8,128)} copy(f32[1,32,2048]{1,2,0:T(8,128)} %get-tuple-element.21) | data formatting | bytes 524288 | tf_op jit(solution)/shard_map/dynamic_slice | solution.py:50
  61.8 2.2 %copy.72 = f32[1,32,2048]{2,1,0:T(8,128)} copy(f32[1,32,2048]{1,2,0:T(8,128)} %get-tuple-element.15) | data formatting | bytes 524288 | tf_op jit(solution)/shard_map/dynamic_slice | solution.py:50
  64.1 0.9 collective-permute-done.8
  65.3 3.5 %collective-permute-start.2 = (f32[1,32,2048]{2,1,0:T(8,128)}, f32[1,32,2048]{2,1,0:T(8,128)}, u32[]{:S(2)}, u32[]{:S(2)}) collective-permute-start(f32[1,32,2048]{2,1,0:T(8,128)} %copy.72), channel_id=1, source_target_pairs={{0,1},{1,0},{2,3},{3,2},{4,5},{5,4},{6,7},{7,6},{8,9},{9,8},{10,11... | collective-permute-start | bytes 786440 | tf_op jit(solution)/shard_map/ppermute | solution.py:51
  68.8 0.8 pad.4.x_ref
  69.9 1.3 copy.88
  71.3 7.3 %shard_map.58 = f32[27,32,256]{2,1,0:T(8,128)} custom-call(bf16[3,32,2304]{2,1,0:T(8,128)(2,1)} %pad.4.x_ref, bf16[2048,256]{1,0:T(8,128)(2,1)} %bitcast.51), custom_call_target="tpu_custom_call" | custom-call | tf_op jit(solution)/shard_map/pallas_call | solution.py:179
  78.6 1.2 slice_select_fusion
  80.0 2.0 %add_convert_fusion.1 = bf16[1,32,2048]{2,1,0:T(8,128)(2,1)} fusion(f32[1,32,2048]{2,1,0:T(8,128)S(1)} %copy-done.6, f32[1,32,2048]{2,1,0:T(8,128)S(1)} %copy-done.8, f32[1,32,2048]{2,1,0:T(8,128)} %collective-permute-done.6, f32[1,32,2048]{2,1,0:T(8,128)} %collective-permute-done.5, f32[1,32,2048]{2,1,0:T(8,128)} %collective-permute-done.4, ...), kind=kLoop, calls=%fused_computation.27 | loop fusion | flops 524288 | bytes 2228224 | tf_op jit(solution)/shard_map/convert_element_type | solution.py:209
  82.0 3.1 %reshape.65 = bf16[1,256,32,1,64]{4,2,1,3,0:T(8,128)(2,1)} reshape(bf16[8,1,32,2048]{3,2,1,0:T(8,128)(2,1)S(1)} %all-to-all-done) | data formatting | bytes 2097152 | tf_op jit(solution)/shard_map/reshape;reshape;transpose | solution.py:133
  85.2 4.1 %copy.90 = bf16[1,256,32,1,64]{1,2,4,3,0:T(8,128)(2,1)S(1)} copy(bf16[1,256,32,1,64]{4,2,1,3,0:T(8,128)(2,1)} %reshape.65) | data formatting | bytes 2097152
  90.8 1.1 select_add_fusion
  92.0 0.9 reshape.40
  92.8 7.4 %all-to-all-start.1 = ((f32[16,27,256]{2,1,0:T(8,128)}), f32[16,27,256]{2,1,0:T(8,128)S(1)}, u32[]{:S(2)}, u32[]{:S(2)}) async-start(f32[16,27,256]{2,1,0:T(8,128)} %reshape.40), calls=%async_computation.1 | async-start | bytes 1048576 | tf_op jit(solution)/shard_map/all_to_all | solution.py:190
  100.3 5.8 %convolution_select_fusion = f32[3,32,8,9,32]{4,2,3,1,0:T(8,128)S(1)} fusion(bf16[3,3,3,32,256]{4,3,2,1,0:T(8,128)(2,1)S(1)} %bitcast.40, pred[8,9]{0,1:T(8,128)(4,1)S(1)} %copy-done.12, bf16[1,256,32,1,7,2]{1,4,5,2,3,0:T(8,128)(2,1)S(1)} %copy-done.9, bf16[1,256,32,1,8,9]{1,4,5,2,3,0:T(8,128)(2,1)S(1)} %copy.81), kind=kOutput, calls=%fused_computation.11 | convolution fusion | flops 1002528768 | bytes 2736200 | tf_op jit(solution)/shard_map/conv_general_dilated | solution.py:135
  106.0 1.2 fusion.26
  107.3 1.3 copy.86
  108.5 6.8 %all-to-all-done.1 = f32[16,27,256]{2,1,0:T(8,128)S(1)} async-done(((f32[16,27,256]{2,1,0:T(8,128)}), f32[16,27,256]{2,1,0:T(8,128)S(1)}, u32[]{:S(2)}, u32[]{:S(2)}) %all-to-all-start.1) | async-done | bytes 442400 | tf_op jit(solution)/shard_map/all_to_all | solution.py:190
  115.3 0.8 broadcast_in_dim.16
  116.2 5.8 %all-to-all-start.2 = ((f32[16,27,256]{2,1,0:T(8,128)}), f32[16,27,256]{2,1,0:T(8,128)}, u32[]{:S(2)}, u32[]{:S(2)}) async-start(f32[16,27,256]{2,1,0:T(8,128)} %broadcast_in_dim.16), calls=%async_computation.2 | async-start | bytes 1048576 | tf_op jit(solution)/shard_map/all_to_all | solution.py:197
  122.0 1.3 slice_bitcast_fusion.1
  124.1 0.9 slice.29
  125.0 3.6 %collective-permute-start.10 = (f32[1,32,2048]{2,1,0:T(8,128)}, f32[1,32,2048]{2,1,0:T(8,128)S(1)}, u32[]{:S(2)}, u32[]{:S(2)}) collective-permute-start(f32[1,32,2048]{2,1,0:T(8,128)} %slice.29), channel_id=1, source_target_pairs={{8,0},{16,8},{24,16},{32,24},{40,32},{48,40},{56,48},{64,56},{72,6... | collective-permute-start | bytes 786440 | tf_op jit(solution)/shard_map/ppermute | solution.py:148
  128.6 2.5 %copy.82 = f32[1,32,8,9,32]{4,1,3,2,0:T(8,128)} copy(f32[1,32,8,9,32]{4,2,3,1,0:T(8,128)} %get-tuple-element.14) | data formatting | bytes 589824 | tf_op jit(solution)/shard_map/conv_general_dilated | solution.py:135
  132.3 0.9 slice.27
  133.2 1.9 %collective-permute-start.9 = (f32[1,32,2048]{2,1,0:T(8,128)}, f32[1,32,2048]{2,1,0:T(8,128)S(1)}, u32[]{:S(2)}, u32[]{:S(2)}) collective-permute-start(f32[1,32,2048]{2,1,0:T(8,128)} %slice.27), channel_id=1, source_target_pairs={{0,8},{8,16},{16,24},{24,32},{32,40},{40,48},{48,56},{56,64},{64,7... | collective-permute-start | bytes 786440 | tf_op jit(solution)/shard_map/ppermute | solution.py:147
  136.9 1.1 reshape.41
  138.1 5.1 %collective-permute-done.9 = f32[1,32,2048]{2,1,0:T(8,128)S(1)} collective-permute-done((f32[1,32,2048]{2,1,0:T(8,128)}, f32[1,32,2048]{2,1,0:T(8,128)S(1)}, u32[]{:S(2)}, u32[]{:S(2)}) %collective-permute-start.9) | collective-permute-done | bytes 262176 | tf_op jit(solution)/shard_map/ppermute | solution.py:147
  143.9 1.0 pad_maximum_fusion
  (64 shorter events, 8.9 us)
Async XLA Ops:
  0.6 27.0 %copy-start = (bf16[27,32,256]{2,1,0:T(8,128)(2,1)S(1)}, bf16[27,32,256]{2,1,0:T(8,128)(2,1)}, u32[]{:S(2)}) copy-start(bf16[27,32,256]{2,1,0:T(8,128)(2,1)} %param.4) | copy-start | bytes 1327108
  0.6 18.7 %copy-start.10 = (bf16[1,32,2048]{2,1,0:T(8,128)(2,1)S(1)}, bf16[1,32,2048]{2,1,0:T(8,128)(2,1)}, u32[]{:S(2)}) copy-start(bf16[1,32,2048]{2,1,0:T(8,128)(2,1)} %param.3) | copy-start | bytes 393220
  0.7 18.7 %collective-permute-start = (bf16[1,32,2048]{2,1,0:T(8,128)(2,1)}, bf16[1,32,2048]{2,1,0:T(8,128)(2,1)S(1)}, u32[]{:S(2)}, u32[]{:S(2)}) collective-permute-start(bf16[1,32,2048]{2,1,0:T(8,128)(2,1)} %param.3), channel_id=1, source_target_pairs={{0,8},{8,16},{16,24},{24,32},{32,40},{40,48},{48,56},{56,64},{64,7... | collective-permute-start | bytes 393224 | tf_op jit(solution)/shard_map/ppermute | solution.py:17
  2.7 16.7 %collective-permute-start.1 = (bf16[1,32,2048]{2,1,0:T(8,128)(2,1)}, bf16[1,32,2048]{2,1,0:T(8,128)(2,1)S(1)}, u32[]{:S(2)}, u32[]{:S(2)}) collective-permute-start(bf16[1,32,2048]{2,1,0:T(8,128)(2,1)} %param.3), channel_id=1, source_target_pairs={{8,0},{16,8},{24,16},{32,24},{40,32},{48,40},{56,48},{64,56},{72,6... | collective-permute-start | bytes 393224 | tf_op jit(solution)/shard_map/ppermute | solution.py:20
  12.1 57.8 %all-to-all-start = ((bf16[8,1,32,2048]{3,2,1,0:T(8,128)(2,1)}), bf16[8,1,32,2048]{3,2,1,0:T(8,128)(2,1)S(1)}, u32[]{:S(2)}, u32[]{:S(2)}) async-start(bf16[8,1,32,2048]{3,2,1,0:T(8,128)(2,1)} %broadcast_in_dim.7), calls=%async_computation | async-start | bytes 2097152 | tf_op jit(solution)/shard_map/all_to_all | solution.py:197
  19.4 0.8 copy-start.3
  24.1 3.5 %copy-start.11 = (pred[8,9]{0,1:T(8,128)(4,1)S(1)}, pred[8,9]{0,1:T(8,128)(4,1)}, u32[]{:S(2)}) copy-start(pred[8,9]{0,1:T(8,128)(4,1)} %constant.68) | copy-start | bytes 220
  41.2 23.8 %collective-permute-start.8 = (f32[1,32,2048]{2,1,0:T(8,128)}, f32[1,32,2048]{2,1,0:T(8,128)S(1)}, u32[]{:S(2)}, u32[]{:S(2)}) collective-permute-start(f32[1,32,2048]{2,1,0:T(8,128)} %copy.78), channel_id=1, source_target_pairs={{0,7},{1,6},{2,5},{3,4},{4,3},{5,2},{6,1},{7,0},{8,15},{9,14},{10,... | collective-permute-start | bytes 786440 | tf_op jit(solution)/shard_map/ppermute | solution.py:51
  46.1 19.2 %collective-permute-start.7 = (f32[1,32,2048]{2,1,0:T(8,128)}, f32[1,32,2048]{2,1,0:T(8,128)S(1)}, u32[]{:S(2)}, u32[]{:S(2)}) collective-permute-start(f32[1,32,2048]{2,1,0:T(8,128)} %copy.77), channel_id=1, source_target_pairs={{0,6},{1,7},{2,4},{3,5},{4,2},{5,3},{6,0},{7,1},{8,14},{9,15},{10,... | collective-permute-start | bytes 786440 | tf_op jit(solution)/shard_map/ppermute | solution.py:51
  48.4 31.5 %collective-permute-start.6 = (f32[1,32,2048]{2,1,0:T(8,128)}, f32[1,32,2048]{2,1,0:T(8,128)}, u32[]{:S(2)}, u32[]{:S(2)}) collective-permute-start(f32[1,32,2048]{2,1,0:T(8,128)} %copy.76), channel_id=1, source_target_pairs={{0,5},{1,4},{2,7},{3,6},{4,1},{5,0},{6,3},{7,2},{8,13},{9,12},{10,... | collective-permute-start | bytes 786440 | tf_op jit(solution)/shard_map/ppermute | solution.py:51
  55.3 13.5 %copy-start.4 = (bf16[3,32,2048]{2,1,0:T(8,128)(2,1)S(1)}, bf16[3,32,2048]{2,1,0:T(8,128)(2,1)}, u32[]{:S(2)}) copy-start(bf16[3,32,2048]{2,1,0:T(8,128)(2,1)} %copy-done.3) | copy-start | bytes 1179652
  55.3 24.6 %collective-permute-start.5 = (f32[1,32,2048]{2,1,0:T(8,128)}, f32[1,32,2048]{2,1,0:T(8,128)}, u32[]{:S(2)}, u32[]{:S(2)}) collective-permute-start(f32[1,32,2048]{2,1,0:T(8,128)} %copy.75), channel_id=1, source_target_pairs={{0,4},{1,5},{2,6},{3,7},{4,0},{5,1},{6,2},{7,3},{8,12},{9,13},{10,... | collective-permute-start | bytes 786440 | tf_op jit(solution)/shard_map/ppermute | solution.py:51
  59.3 20.6 %collective-permute-start.4 = (f32[1,32,2048]{2,1,0:T(8,128)}, f32[1,32,2048]{2,1,0:T(8,128)}, u32[]{:S(2)}, u32[]{:S(2)}) collective-permute-start(f32[1,32,2048]{2,1,0:T(8,128)} %copy.74), channel_id=1, source_target_pairs={{0,3},{1,2},{2,1},{3,0},{4,7},{5,6},{6,5},{7,4},{8,11},{9,10},{10,... | collective-permute-start | bytes 786440 | tf_op jit(solution)/shard_map/ppermute | solution.py:51
  65.0 6.3 %copy-start.5 = (f32[1,32,2048]{2,1,0:T(8,128)}, f32[1,32,2048]{2,1,0:T(8,128)S(1)}, u32[]{:S(2)}) copy-start(f32[1,32,2048]{2,1,0:T(8,128)S(1)} %collective-permute-done.8) | copy-start | bytes 786436
  65.0 15.0 %collective-permute-start.3 = (f32[1,32,2048]{2,1,0:T(8,128)}, f32[1,32,2048]{2,1,0:T(8,128)}, u32[]{:S(2)}, u32[]{:S(2)}) collective-permute-start(f32[1,32,2048]{2,1,0:T(8,128)} %copy.73), channel_id=1, source_target_pairs={{0,2},{1,3},{2,0},{3,1},{4,6},{5,7},{6,4},{7,5},{8,10},{9,11},{10,... | collective-permute-start | bytes 786440 | tf_op jit(solution)/shard_map/ppermute | solution.py:51
  65.3 6.0 %copy-start.7 = (f32[1,32,2048]{2,1,0:T(8,128)}, f32[1,32,2048]{2,1,0:T(8,128)S(1)}, u32[]{:S(2)}) copy-start(f32[1,32,2048]{2,1,0:T(8,128)S(1)} %collective-permute-done.7) | copy-start | bytes 786436
  65.3 14.7 %collective-permute-start.2 = (f32[1,32,2048]{2,1,0:T(8,128)}, f32[1,32,2048]{2,1,0:T(8,128)}, u32[]{:S(2)}, u32[]{:S(2)}) collective-permute-start(f32[1,32,2048]{2,1,0:T(8,128)} %copy.72), channel_id=1, source_target_pairs={{0,1},{1,0},{2,3},{3,2},{4,5},{5,4},{6,7},{7,6},{8,9},{9,8},{10,11... | collective-permute-start | bytes 786440 | tf_op jit(solution)/shard_map/ppermute | solution.py:51
  71.3 8.7 %copy-start.6 = (f32[1,32,2048]{2,1,0:T(8,128)S(1)}, f32[1,32,2048]{2,1,0:T(8,128)}, u32[]{:S(2)}) copy-start(f32[1,32,2048]{2,1,0:T(8,128)} %copy-done.5) | copy-start | bytes 786436
  71.3 8.7 %copy-start.8 = (f32[1,32,2048]{2,1,0:T(8,128)S(1)}, f32[1,32,2048]{2,1,0:T(8,128)}, u32[]{:S(2)}) copy-start(f32[1,32,2048]{2,1,0:T(8,128)} %copy-done.7) | copy-start | bytes 786436
  79.8 11.0 %collective-permute-start.11 = (f32[432,256]{1,0:T(8,128)S(1)}, f32[432,256]{1,0:T(8,128)}, u32[]{:S(2)}, u32[]{:S(2)}) collective-permute-start(f32[432,256]{1,0:T(8,128)S(1)} %slice_select_fusion), channel_id=1, source_target_pairs={{0,8},{8,0},{1,9},{9,1},{2,10},{10,2},{3,11},{11,3},{4,12},{12,4},... | collective-permute-start | bytes 1327112 | tf_op jit(solution)/shard_map/ppermute | solution.py:40
  89.3 1.6 %copy-start.1 = (f32[27,32,256]{2,1,0:T(8,128)S(1)}, f32[27,32,256]{2,1,0:T(8,128)}, u32[]{:S(2)}) copy-start(f32[27,32,256]{2,1,0:T(8,128)} %shard_map.58) | copy-start | bytes 2654212
  90.1 10.2 %copy-start.12 = (pred[8,9]{0,1:T(8,128)(4,1)S(1)}, pred[8,9]{0,1:T(8,128)(4,1)}, u32[]{:S(2)}) copy-start(pred[8,9]{0,1:T(8,128)(4,1)} %constant.68) | copy-start | bytes 220
  90.8 9.4 %copy-start.9 = (bf16[1,256,32,1,7,2]{1,4,5,2,3,0:T(8,128)(2,1)S(1)}, bf16[1,256,32,1,7,2]{1,4,5,2,3,0:T(8,128)(2,1)}, u32[]{:S(2)}) copy-start(bf16[1,256,32,1,7,2]{1,4,5,2,3,0:T(8,128)(2,1)} %slice.43) | copy-start | bytes 688132
  92.8 22.5 %all-to-all-start.1 = ((f32[16,27,256]{2,1,0:T(8,128)}), f32[16,27,256]{2,1,0:T(8,128)S(1)}, u32[]{:S(2)}, u32[]{:S(2)}) async-start(f32[16,27,256]{2,1,0:T(8,128)} %reshape.40), calls=%async_computation.1 | async-start | bytes 1048576 | tf_op jit(solution)/shard_map/all_to_all | solution.py:190
  116.2 20.7 %all-to-all-start.2 = ((f32[16,27,256]{2,1,0:T(8,128)}), f32[16,27,256]{2,1,0:T(8,128)}, u32[]{:S(2)}, u32[]{:S(2)}) async-start(f32[16,27,256]{2,1,0:T(8,128)} %broadcast_in_dim.16), calls=%async_computation.2 | async-start | bytes 1048576 | tf_op jit(solution)/shard_map/all_to_all | solution.py:197
  125.0 13.1 %collective-permute-start.10 = (f32[1,32,2048]{2,1,0:T(8,128)}, f32[1,32,2048]{2,1,0:T(8,128)S(1)}, u32[]{:S(2)}, u32[]{:S(2)}) collective-permute-start(f32[1,32,2048]{2,1,0:T(8,128)} %slice.29), channel_id=1, source_target_pairs={{8,0},{16,8},{24,16},{32,24},{40,32},{48,40},{56,48},{64,56},{72,6... | collective-permute-start | bytes 786440 | tf_op jit(solution)/shard_map/ppermute | solution.py:148
  131.4 3.7 %copy-start.2 = (f32[1,32,8,9,32]{4,1,3,2,0:T(8,128)S(1)}, f32[1,32,8,9,32]{4,1,3,2,0:T(8,128)}, u32[]{:S(2)}) copy-start(f32[1,32,8,9,32]{4,1,3,2,0:T(8,128)} %copy.82) | copy-start | bytes 884740
  133.2 10.0 %collective-permute-start.9 = (f32[1,32,2048]{2,1,0:T(8,128)}, f32[1,32,2048]{2,1,0:T(8,128)S(1)}, u32[]{:S(2)}, u32[]{:S(2)}) collective-permute-start(f32[1,32,2048]{2,1,0:T(8,128)} %slice.27), channel_id=1, source_target_pairs={{0,8},{8,16},{16,24},{24,32},{32,40},{40,48},{48,56},{56,64},{64,7... | collective-permute-start | bytes 786440 | tf_op jit(solution)/shard_map/ppermute | solution.py:147
  138.0 5.9 %collective-permute-start.12 = (f32[432,256]{1,0:T(8,128)S(1)}, f32[432,256]{1,0:T(8,128)S(1)}, u32[]{:S(2)}, u32[]{:S(2)}) collective-permute-start(f32[432,256]{1,0:T(8,128)S(1)} %reshape.41), channel_id=1, source_target_pairs={{0,8},{8,0},{1,9},{9,1},{2,10},{10,2},{3,11},{11,3},{4,12},{12,4},... | collective-permute-start | bytes 1327112 | tf_op jit(solution)/shard_map/ppermute | solution.py:60

commit v5 on v3

--- a/solution.py
+++ b/solution.py
@@ -189,7 +189,7 @@
     return copies.reshape(shape[:dim] + (count * shape[dim],) + shape[dim + 1 :])
 
 
-SPACE = ("srest", "core")
+SPACE = ("ylo", "z", "core")
 
 
 def local(inputs, weights, cotangent):
@@ -201,16 +201,16 @@
     input_grad = spill_sum(conv_backward(gathered, weights), SPACE).astype(jnp.bfloat16)
     local_terms = conv_filter(padded, gathered)
     flat = local_terms.reshape(-1, local_terms.shape[-1])
-    flat = halving_sum(flat, "core", [1], 0)
-    flat = spread_gather(scatter_sum(flat, "srest", 0), "srest", 0)
-    flat = doubling_gather(flat, "core", [1], 0)
+    flat = halving_sum(halving_sum(flat, "core", [1], 0), "ylo", [1], 0)
+    flat = spread_gather(scatter_sum(flat, "z", 0), "z", 0)
+    flat = doubling_gather(doubling_gather(flat, "ylo", [1], 0), "core", [1], 0)
     weight_grad = flat.reshape(local_terms.shape)
     return (output, input_grad, weight_grad)
 
 
 def solution(mesh):
     space, chan = mesh.devices.shape
-    split = jax.sharding.Mesh(mesh.devices.reshape(space // 2, 2, chan), SPACE + ("chan",))
+    split = jax.sharding.Mesh(mesh.devices.reshape(2, space // 4, 2, chan), SPACE + ("chan",))
     placed = (P(SPACE, "chan", None), P(None, "chan", None), P(SPACE, "chan", None))
     return jax.shard_map(
         local,

time: 135 us -> 141 us (1.044)
  waiting for transfers between devices: 9.81 us -> 15.5 us
  local copies, waits for them, and re-layouts: 46.6 us -> 42 us
  starting transfers between devices: 44.4 us -> 47 us
  other arithmetic: 15.3 us -> 17.1 us
    ppermute x4 -> x5, waiting for transfers between devices: 8.5 us -> 2.19 us  [halving_sum(): lax.ppermute(send, axis, [(i, i ^ mask) for i in range(count)])]
    all_to_all x2, waiting for transfers between devices: 0.01 us -> 5.94 us  [spread_gather(): copies = lax.all_to_all(copies, axis, 0, 0, tiled=True)]
    ppermute x1 -> x2, starting transfers between devices: 1.81 us -> 6.37 us  [doubling_gather(): other = lax.ppermute(block, axis, [(i, i ^ mask) for i in range(count)])]
    all_to_all x1, waiting for transfers between devices: 0.93 us -> 5.44 us  [scatter_sum(): parts = lax.all_to_all(parts, axis, 0, 0, tiled=True)]
    all_to_all x2, starting transfers between devices: 13.5 us -> 10.1 us  [spread_gather(): copies = lax.all_to_all(copies, axis, 0, 0, tiled=True)]
    slice x3, local copies, waits for them, and re-layouts: 5.1 us -> 1.73 us  [spill_sum(): from_high = lax.ppermute(parts[:1], axis, backward)]
    ppermute x4 -> x5, starting transfers between devices: 6.54 us -> 9.11 us  [halving_sum(): lax.ppermute(send, axis, [(i, i ^ mask) for i in range(count)])]
    ppermute x1 -> x2, waiting for transfers between devices: 0.36 us -> 1.92 us  [doubling_gather(): other = lax.ppermute(block, axis, [(i, i ^ mask) for i in range(count)])]
  transfers between devices with their start and end apart: 12 -> 14, of which waited for: 3 -> 5; matrix products, arithmetic and copies ran while one was open for 51% -> 46% of each run, Pallas kernels for 5% -> 5%
where the time goes in v5:
time: 141 us; the launch traced here: 140 us
  starting transfers between devices  47 us (33%)
  local copies, waits for them, and re-layouts  42 us (30%)
  other arithmetic  17.1 us (12%)
  waiting for transfers between devices  15.5 us (11%)
  matrix products  9.7 us (7%)
  Pallas kernels  7.28 us (5%)
    all_to_all x2, starting transfers between devices, spread_gather(): copies = lax.all_to_all(copies, axis, 0, 0, tiled=True)  10.1 us
    ppermute x5, starting transfers between devices, halving_sum(): lax.ppermute(send, axis, [(i, i ^ mask) for i in range(count)])  9.11 us
    all_to_all x1, starting transfers between devices, scatter_sum(): parts = lax.all_to_all(parts, axis, 0, 0, tiled=True)  7.91 us
    pallas_call x1, Pallas kernels, conv_filter(): pl.pallas_call(filter_kernel, out_shape=jax.ShapeDtypeStruct((27, channel...  7.28 us
    ppermute x2, starting transfers between devices, doubling_gather(): other = lax.ppermute(block, axis, [(i, i ^ mask) for i in range(count)])  6.37 us
    unnamed x24, local copies, waits for them, and re-layouts  6.34 us
    all_to_all x2, waiting for transfers between devices, spread_gather(): copies = lax.all_to_all(copies, axis, 0, 0, tiled=True)  5.94 us
    conv_general_dilated x1, matrix products, conv_backward(): lax.conv_general_dilated(lhs, rhs, (1, 1, 1), [(2, 2), (1, 1), (1, 1)], d...  5.76 us
  transfers between devices with their start and end apart: 14, of which 5 were waited for; matrix products, arithmetic and copies ran while one was open for 46% of the time, Pallas kernels for 5%

profile of v5, /device:TPU:1, one launch (start us, length us, event | category | flops | bytes accessed | tf_op | source)
XLA Modules:
  0.0 139.6 jit_solution(1185441698158092322)
XLA Ops:
  0.7 5.1 %collective-permute-start = (bf16[1,32,2048]{2,1,0:T(8,128)(2,1)}, bf16[1,32,2048]{2,1,0:T(8,128)(2,1)S(1)}, u32[]{:S(2)}, u32[]{:S(2)}) collective-permute-start(bf16[1,32,2048]{2,1,0:T(8,128)(2,1)} %param.3), channel_id=1, source_target_pairs={{0,8},{8,16},{16,24},{24,32},{32,40},{40,48},{48,56},{56,64},{64,7... | collective-permute-start | bytes 393224 | tf_op jit(solution)/shard_map/ppermute | solution.py:17
  5.7 1.9 %collective-permute-start.1 = (bf16[1,32,2048]{2,1,0:T(8,128)(2,1)}, bf16[1,32,2048]{2,1,0:T(8,128)(2,1)S(1)}, u32[]{:S(2)}, u32[]{:S(2)}) collective-permute-start(bf16[1,32,2048]{2,1,0:T(8,128)(2,1)} %param.3), channel_id=1, source_target_pairs={{8,0},{16,8},{24,16},{32,24},{40,32},{48,40},{56,48},{64,56},{72,6... | collective-permute-start | bytes 393224 | tf_op jit(solution)/shard_map/ppermute | solution.py:20
  7.6 2.0 %broadcast_in_dim.7 = bf16[8,1,32,2048]{3,2,1,0:T(8,128)(2,1)} broadcast(bf16[32,2048]{1,0:T(8,128)(2,1)} %bitcast.54), dimensions={2,3} | broadcast | bytes 1179648 | tf_op jit(solution)/shard_map/broadcast_in_dim | solution.py:185
  9.7 6.7 %all-to-all-start = ((bf16[8,1,32,2048]{3,2,1,0:T(8,128)(2,1)}), bf16[8,1,32,2048]{3,2,1,0:T(8,128)(2,1)S(1)}, u32[]{:S(2)}, u32[]{:S(2)}) async-start(bf16[8,1,32,2048]{3,2,1,0:T(8,128)(2,1)} %broadcast_in_dim.7), calls=%async_computation | async-start | bytes 2097152 | tf_op jit(solution)/shard_map/all_to_all | solution.py:186
  17.2 2.1 %copy.36 = bf16[3,32,32,1,64]{2,1,4,0,3:T(8,128)(2,1)} copy(bf16[3,32,32,1,64]{4,2,1,0,3:T(8,128)(2,1)S(1)} %reshape.61) | data formatting | bytes 786432 | tf_op jit(solution)/shard_map/reshape | solution.py:110
  19.3 1.8 %pad.5 = bf16[3,32,32,1,72]{2,1,4,0,3:T(8,128)(2,1)S(1)} pad(bf16[3,32,32,1,64]{2,1,4,0,3:T(8,128)(2,1)} %copy.36, bf16[]{:T(256)} %constant.96.clone.1), padding=0_0x0_0x0_0x0_0x1_7 | pad | bytes 835586 | tf_op jit(solution)/shard_map/reshape | solution.py:110
  21.1 2.4 %copy.38 = bf16[3,32,32,1,8,9]{1,4,5,2,0,3:T(8,128)(2,1)} copy(bf16[3,32,32,1,8,9]{2,1,5,4,0,3:T(8,128)(2,1)S(1)} %bitcast.47) | data formatting | bytes 884736 | tf_op jit(solution)/shard_map/conv_general_dilated | solution.py:112
  23.5 1.1 slice.73
  24.7 3.9 %fusion.9 = f32[1,32,8,9,256]{4,2,3,1,0:T(8,128)S(1)} fusion(bf16[3,3,3,32,256]{4,3,2,1,0:T(8,128)(2,1)S(1)} %bitcast.39, bf16[3,32,32,1,7,2]{1,4,5,2,0,3:T(8,128)(2,1)S(1)} %slice.73, bf16[3,32,32,1,8,9]{1,4,5,2,0,3:T(8,128)(2,1)} %copy.38, pred[8,9]{0,1:T(8,128)(4,1)S(1)} %copy-done.9), kind=kOutput, calls=%fused_computation.12 | convolution fusion | flops 1000194048 | bytes 3330120 | tf_op jit(solution)/shard_map/conv_general_dilated | solution.py:112
  30.4 1.2 copy.40
  31.6 1.3 copy-done.1
  33.0 1.1 slice_select_fusion.2
  34.0 3.0 %collective-permute-start.2 = (f32[1,128,2048]{1,2,0:T(8,128)}, f32[1,128,2048]{1,2,0:T(8,128)}, u32[]{:S(2)}, u32[]{:S(2)}) collective-permute-start(f32[1,128,2048]{1,2,0:T(8,128)} %slice_select_fusion.2), channel_id=1, source_target_pairs={{0,4},{1,5},{2,6},{3,7},{4,0},{5,1},{6,2},{7,3},{8,12},{9,13},{10,... | collective-permute-start | bytes 3145736 | tf_op jit(solution)/shard_map/ppermute | solution.py:40
  37.0 1.3 copy.54
  38.3 7.3 %shard_map.58 = f32[27,32,256]{2,1,0:T(8,128)} custom-call(bf16[3,32,2304]{2,1,0:T(8,128)(2,1)} %pad.4.x_ref, bf16[2048,256]{1,0:T(8,128)(2,1)} %bitcast.52), custom_call_target="tpu_custom_call" | custom-call | tf_op jit(solution)/shard_map/pallas_call | solution.py:168
  45.6 2.0 %slice_select_fusion.3 = f32[432,256]{1,0:T(8,128)} fusion(f32[864,256]{1,0:T(8,128)} %bitcast.45, pred[]{:T(512)S(6)} %eq.28), kind=kLoop, calls=%fused_computation.32 | loop fusion | flops 110592 | bytes 1327105 | tf_op jit(solution)/shard_map/jit(_where)/select_n | solution.py:39
  47.6 3.1 %reshape.65 = bf16[1,256,32,1,64]{4,2,1,3,0:T(8,128)(2,1)} reshape(bf16[8,1,32,2048]{3,2,1,0:T(8,128)(2,1)S(1)} %all-to-all-done) | data formatting | bytes 2097152 | tf_op jit(solution)/shard_map/reshape;reshape;transpose | solution.py:122
  50.7 4.1 %copy.56 = bf16[1,256,32,1,64]{1,2,4,3,0:T(8,128)(2,1)S(1)} copy(bf16[1,256,32,1,64]{4,2,1,3,0:T(8,128)(2,1)} %reshape.65) | data formatting | bytes 2097152
  55.6 5.8 %convolution_select_fusion = f32[3,32,8,9,32]{4,2,3,1,0:T(8,128)S(1)} fusion(bf16[3,3,3,32,256]{4,3,2,1,0:T(8,128)(2,1)S(1)} %bitcast.40, pred[8,9]{0,1:T(8,128)(4,1)S(1)} %copy-done.9, bf16[1,256,32,1,7,2]{1,4,5,2,3,0:T(8,128)(2,1)S(1)} %slice.81, bf16[1,256,32,1,8,9]{1,4,5,2,3,0:T(8,128)(2,1)S(1)} %copy.47), kind=kOutput, calls=%fused_computation.11 | convolution fusion | flops 1002528768 | bytes 2736200 | tf_op jit(solution)/shard_map/conv_general_dilated | solution.py:124
  61.4 1.3 fusion.26
  63.7 0.9 slice.57
  64.6 4.5 %collective-permute-start.5 = (f32[1,32,2048]{2,1,0:T(8,128)}, f32[1,32,2048]{2,1,0:T(8,128)}, u32[]{:S(2)}, u32[]{:S(2)}) collective-permute-start(f32[1,32,2048]{2,1,0:T(8,128)} %slice.57), channel_id=1, source_target_pairs={{0,8},{8,16},{16,24},{24,32},{32,40},{40,48},{48,56},{56,64},{64,7... | collective-permute-start | bytes 786440 | tf_op jit(solution)/shard_map/ppermute | solution.py:136
  69.1 1.5 %copy.52 = f32[1,32,8,9,32]{4,1,3,2,0:T(8,128)S(1)} copy(f32[1,32,8,9,32]{4,2,3,1,0:T(8,128)} %get-tuple-element.13) | data formatting | bytes 589824 | tf_op jit(solution)/shard_map/conv_general_dilated | solution.py:124
  71.5 0.9 slice.59
  72.4 2.1 %collective-permute-start.6 = (f32[1,32,2048]{2,1,0:T(8,128)}, f32[1,32,2048]{2,1,0:T(8,128)}, u32[]{:S(2)}, u32[]{:S(2)}) collective-permute-start(f32[1,32,2048]{2,1,0:T(8,128)} %slice.59), channel_id=1, source_target_pairs={{8,0},{16,8},{24,16},{32,24},{40,32},{48,40},{56,48},{64,56},{72,6... | collective-permute-start | bytes 786440 | tf_op jit(solution)/shard_map/ppermute | solution.py:137
  74.5 1.2 copy.48
  75.8 2.0 %select_add_fusion.1 = f32[1,128,2048]{1,2,0:T(8,128)S(1)} fusion(f32[1,128,2048]{1,2,0:T(8,128)} %collective-permute-done.2, f32[1,256,2048]{1,2,0:T(8,128)} %bitcast.42, pred[]{:T(512)S(6)} %eq.27), kind=kLoop, calls=%fused_computation.24 | loop fusion | flops 524288 | bytes 4194305 | tf_op jit(solution)/shard_map/add | solution.py:40
  77.8 1.4 slice_select_fusion.1
  79.1 2.3 %copy.41 = f32[1,64,2048]{2,1,0:T(8,128)} copy(f32[1,64,2048]{1,2,0:T(8,128)} %slice_select_fusion.1) | data formatting | bytes 1048576 | tf_op jit(solution)/shard_map/jit(_where)/select_n | solution.py:39
  81.8 1.2 select_add_fusion.2
  83.7 3.1 %collective-permute-start.8 = (f32[216,256]{1,0:T(8,128)}, f32[216,256]{1,0:T(8,128)}, u32[]{:S(2)}, u32[]{:S(2)}) collective-permute-start(f32[216,256]{1,0:T(8,128)} %slice_select_fusion.4), channel_id=1, source_target_pairs={{0,128},{128,0},{1,129},{129,1},{2,130},{130,2},{3,131},{131,3},{4... | collective-permute-start | bytes 663560 | tf_op jit(solution)/shard_map/ppermute | solution.py:40
  87.6 0.9 slice.55
  88.5 2.2 %collective-permute-done.8 = f32[216,256]{1,0:T(8,128)} collective-permute-done((f32[216,256]{1,0:T(8,128)}, f32[216,256]{1,0:T(8,128)}, u32[]{:S(2)}, u32[]{:S(2)}) %collective-permute-start.8) | collective-permute-done | bytes 221216 | tf_op jit(solution)/shard_map/ppermute | solution.py:40
  90.7 1.0 select_add_fusion.3
  92.4 7.9 %all-to-all-start.1 = ((f32[8,27,256]{2,1,0:T(8,128)}), f32[8,27,256]{2,1,0:T(8,128)S(1)}, u32[]{:S(2)}, u32[]{:S(2)}) async-start(f32[8,27,256]{2,1,0:T(8,128)} %reshape.40), calls=%async_computation.1 | async-start | bytes 524288 | tf_op jit(solution)/shard_map/all_to_all | solution.py:179
  100.3 2.4 %copy.42 = f32[1,64,2048]{1,2,0:T(8,128)} copy(f32[1,64,2048]{2,1,0:T(8,128)} %collective-permute-done.3) | data formatting | bytes 1048576 | tf_op jit(solution)/shard_map/ppermute | solution.py:40
  102.7 1.6 %select_add_fusion = f32[1,64,2048]{1,2,0:T(8,128)S(1)} fusion(f32[1,64,2048]{1,2,0:T(8,128)} %copy.42, f32[1,128,2048]{1,2,0:T(8,128)S(1)} %select_add_fusion.1, pred[]{:T(512)S(6)} %eq.26), kind=kLoop, calls=%fused_computation.23 | loop fusion | flops 262144 | bytes 2097153 | tf_op jit(solution)/shard_map/add | solution.py:40
  104.3 5.4 %all-to-all-done.1 = f32[8,27,256]{2,1,0:T(8,128)S(1)} async-done(((f32[8,27,256]{2,1,0:T(8,128)}), f32[8,27,256]{2,1,0:T(8,128)S(1)}, u32[]{:S(2)}, u32[]{:S(2)}) %all-to-all-start.1) | async-done | bytes 221216 | tf_op jit(solution)/shard_map/all_to_all | solution.py:179
  110.5 3.4 %all-to-all-start.2 = ((f32[8,27,256]{2,1,0:T(8,128)}), f32[8,27,256]{2,1,0:T(8,128)S(1)}, u32[]{:S(2)}, u32[]{:S(2)}) async-start(f32[8,27,256]{2,1,0:T(8,128)} %broadcast_in_dim.16), calls=%async_computation.2 | async-start | bytes 524288 | tf_op jit(solution)/shard_map/all_to_all | solution.py:186
  114.5 2.8 %collective-permute-start.4 = (f32[1,32,2048]{2,1,0:T(8,128)S(1)}, f32[1,32,2048]{2,1,0:T(8,128)}, u32[]{:S(2)}, u32[]{:S(2)}) collective-permute-start(f32[1,32,2048]{2,1,0:T(8,128)S(1)} %copy.43), channel_id=1, source_target_pairs={{0,1},{1,0},{2,3},{3,2},{4,5},{5,4},{6,7},{7,6},{8,9},{9,8},{10,11... | collective-permute-start | bytes 786440 | tf_op jit(solution)/shard_map/ppermute | solution.py:40
  117.3 5.9 %all-to-all-done.2 = f32[8,27,256]{2,1,0:T(8,128)S(1)} async-done(((f32[8,27,256]{2,1,0:T(8,128)}), f32[8,27,256]{2,1,0:T(8,128)S(1)}, u32[]{:S(2)}, u32[]{:S(2)}) %all-to-all-start.2) | async-done | bytes 221216 | tf_op jit(solution)/shard_map/all_to_all | solution.py:186
  123.8 1.7 %add_convert_fusion.1 = bf16[1,32,2048]{2,1,0:T(8,128)(2,1)} fusion(f32[1,32,2048]{2,1,0:T(8,128)} %collective-permute-done.6, f32[1,32,2048]{2,1,0:T(8,128)S(1)} %copy-done.6, f32[1,32,2048]{2,1,0:T(8,128)} %collective-permute-done.5), kind=kLoop, calls=%fused_computation.33 | loop fusion | flops 196608 | bytes 917504 | tf_op jit(solution)/shard_map/convert_element_type | solution.py:201
  125.5 1.3 copy.44
  126.8 1.3 collective-permute-done.9
  128.1 1.0 broadcast_select_fusion.3
  129.9 5.9 %collective-permute-start.10 = (f32[432,256]{1,0:T(8,128)}, f32[432,256]{1,0:T(8,128)}, u32[]{:S(2)}, u32[]{:S(2)}) collective-permute-start(f32[432,256]{1,0:T(8,128)} %pad_maximum_fusion.1), channel_id=1, source_target_pairs={{0,8},{8,0},{1,9},{9,1},{2,10},{10,2},{3,11},{11,3},{4,12},{12,4},... | collective-permute-start | bytes 1327112 | tf_op jit(solution)/shard_map/ppermute | solution.py:49
  137.6 1.1 broadcast_select_fusion.1
  138.7 1.0 pad_maximum_fusion
  (59 shorter events, 12.5 us)
Async XLA Ops:
  0.6 24.0 %copy-start = (bf16[27,32,256]{2,1,0:T(8,128)(2,1)S(1)}, bf16[27,32,256]{2,1,0:T(8,128)(2,1)}, u32[]{:S(2)}) copy-start(bf16[27,32,256]{2,1,0:T(8,128)(2,1)} %param.4) | copy-start | bytes 1327108
  0.6 15.7 %copy-start.8 = (bf16[1,32,2048]{2,1,0:T(8,128)(2,1)S(1)}, bf16[1,32,2048]{2,1,0:T(8,128)(2,1)}, u32[]{:S(2)}) copy-start(bf16[1,32,2048]{2,1,0:T(8,128)(2,1)} %param.3) | copy-start | bytes 393220
  0.7 15.7 %collective-permute-start = (bf16[1,32,2048]{2,1,0:T(8,128)(2,1)}, bf16[1,32,2048]{2,1,0:T(8,128)(2,1)S(1)}, u32[]{:S(2)}, u32[]{:S(2)}) collective-permute-start(bf16[1,32,2048]{2,1,0:T(8,128)(2,1)} %param.3), channel_id=1, source_target_pairs={{0,8},{8,16},{16,24},{24,32},{32,40},{40,48},{48,56},{56,64},{64,7... | collective-permute-start | bytes 393224 | tf_op jit(solution)/shard_map/ppermute | solution.py:17
  5.7 10.7 %collective-permute-start.1 = (bf16[1,32,2048]{2,1,0:T(8,128)(2,1)}, bf16[1,32,2048]{2,1,0:T(8,128)(2,1)S(1)}, u32[]{:S(2)}, u32[]{:S(2)}) collective-permute-start(bf16[1,32,2048]{2,1,0:T(8,128)(2,1)} %param.3), channel_id=1, source_target_pairs={{8,0},{16,8},{24,16},{32,24},{40,32},{48,40},{56,48},{64,56},{72,6... | collective-permute-start | bytes 393224 | tf_op jit(solution)/shard_map/ppermute | solution.py:20
  9.7 27.3 %all-to-all-start = ((bf16[8,1,32,2048]{3,2,1,0:T(8,128)(2,1)}), bf16[8,1,32,2048]{3,2,1,0:T(8,128)(2,1)S(1)}, u32[]{:S(2)}, u32[]{:S(2)}) async-start(bf16[8,1,32,2048]{3,2,1,0:T(8,128)(2,1)} %broadcast_in_dim.7), calls=%async_computation | async-start | bytes 2097152 | tf_op jit(solution)/shard_map/all_to_all | solution.py:186
  16.4 0.8 copy-start.4
  21.1 3.5 %copy-start.9 = (pred[8,9]{0,1:T(8,128)(4,1)S(1)}, pred[8,9]{0,1:T(8,128)(4,1)}, u32[]{:S(2)}) copy-start(pred[8,9]{0,1:T(8,128)(4,1)} %constant.110) | copy-start | bytes 220
  24.6 4.0 %copy-start.5 = (bf16[3,32,2048]{2,1,0:T(8,128)(2,1)S(1)}, bf16[3,32,2048]{2,1,0:T(8,128)(2,1)}, u32[]{:S(2)}) copy-start(bf16[3,32,2048]{2,1,0:T(8,128)(2,1)} %copy-done.4) | copy-start | bytes 1179652
  31.6 1.3 copy-start.1
  34.0 41.7 %collective-permute-start.2 = (f32[1,128,2048]{1,2,0:T(8,128)}, f32[1,128,2048]{1,2,0:T(8,128)}, u32[]{:S(2)}, u32[]{:S(2)}) collective-permute-start(f32[1,128,2048]{1,2,0:T(8,128)} %slice_select_fusion.2), channel_id=1, source_target_pairs={{0,4},{1,5},{2,6},{3,7},{4,0},{5,1},{6,2},{7,3},{8,12},{9,13},{10,... | collective-permute-start | bytes 3145736 | tf_op jit(solution)/shard_map/ppermute | solution.py:40
  47.6 34.2 %collective-permute-start.7 = (f32[432,256]{1,0:T(8,128)}, f32[432,256]{1,0:T(8,128)}, u32[]{:S(2)}, u32[]{:S(2)}) collective-permute-start(f32[432,256]{1,0:T(8,128)} %slice_select_fusion.3), channel_id=1, source_target_pairs={{0,8},{8,0},{1,9},{9,1},{2,10},{10,2},{3,11},{11,3},{4,12},{12,4},... | collective-permute-start | bytes 1327112 | tf_op jit(solution)/shard_map/ppermute | solution.py:40
  64.6 59.1 %collective-permute-start.5 = (f32[1,32,2048]{2,1,0:T(8,128)}, f32[1,32,2048]{2,1,0:T(8,128)}, u32[]{:S(2)}, u32[]{:S(2)}) collective-permute-start(f32[1,32,2048]{2,1,0:T(8,128)} %slice.57), channel_id=1, source_target_pairs={{0,8},{8,16},{16,24},{24,32},{32,40},{40,48},{48,56},{56,64},{64,7... | collective-permute-start | bytes 786440 | tf_op jit(solution)/shard_map/ppermute | solution.py:136
  72.4 51.4 %collective-permute-start.6 = (f32[1,32,2048]{2,1,0:T(8,128)}, f32[1,32,2048]{2,1,0:T(8,128)}, u32[]{:S(2)}, u32[]{:S(2)}) collective-permute-start(f32[1,32,2048]{2,1,0:T(8,128)} %slice.59), channel_id=1, source_target_pairs={{8,0},{16,8},{24,16},{32,24},{40,32},{48,40},{56,48},{64,56},{72,6... | collective-permute-start | bytes 786440 | tf_op jit(solution)/shard_map/ppermute | solution.py:137
  77.8 4.0 %copy-start.2 = (f32[27,32,256]{2,1,0:T(8,128)S(1)}, f32[27,32,256]{2,1,0:T(8,128)}, u32[]{:S(2)}) copy-start(f32[27,32,256]{2,1,0:T(8,128)} %shard_map.58) | copy-start | bytes 2654212
  81.5 5.3 %copy-start.3 = (f32[1,32,8,9,32]{4,1,3,2,0:T(8,128)S(1)}, f32[1,32,8,9,32]{4,1,3,2,0:T(8,128)}, u32[]{:S(2)}) copy-start(f32[1,32,8,9,32]{4,1,3,2,0:T(8,128)} %copy.48) | copy-start | bytes 884740
  81.5 18.8 %collective-permute-start.3 = (f32[1,64,2048]{2,1,0:T(8,128)}, f32[1,64,2048]{2,1,0:T(8,128)}, u32[]{:S(2)}, u32[]{:S(2)}) collective-permute-start(f32[1,64,2048]{2,1,0:T(8,128)} %copy.41), channel_id=1, source_target_pairs={{0,2},{1,3},{2,0},{3,1},{4,6},{5,7},{6,4},{7,5},{8,10},{9,11},{10,... | collective-permute-start | bytes 1572872 | tf_op jit(solution)/shard_map/ppermute | solution.py:40
  83.7 7.0 %collective-permute-start.8 = (f32[216,256]{1,0:T(8,128)}, f32[216,256]{1,0:T(8,128)}, u32[]{:S(2)}, u32[]{:S(2)}) collective-permute-start(f32[216,256]{1,0:T(8,128)} %slice_select_fusion.4), channel_id=1, source_target_pairs={{0,128},{128,0},{1,129},{129,1},{2,130},{130,2},{3,131},{131,3},{4... | collective-permute-start | bytes 663560 | tf_op jit(solution)/shard_map/ppermute | solution.py:40
  92.4 17.3 %all-to-all-start.1 = ((f32[8,27,256]{2,1,0:T(8,128)}), f32[8,27,256]{2,1,0:T(8,128)S(1)}, u32[]{:S(2)}, u32[]{:S(2)}) async-start(f32[8,27,256]{2,1,0:T(8,128)} %reshape.40), calls=%async_computation.1 | async-start | bytes 524288 | tf_op jit(solution)/shard_map/all_to_all | solution.py:179
  110.5 12.8 %all-to-all-start.2 = ((f32[8,27,256]{2,1,0:T(8,128)}), f32[8,27,256]{2,1,0:T(8,128)S(1)}, u32[]{:S(2)}, u32[]{:S(2)}) async-start(f32[8,27,256]{2,1,0:T(8,128)} %broadcast_in_dim.16), calls=%async_computation.2 | async-start | bytes 524288 | tf_op jit(solution)/shard_map/all_to_all | solution.py:186
  113.9 9.9 %copy-start.6 = (f32[1,32,2048]{2,1,0:T(8,128)S(1)}, f32[1,32,2048]{2,1,0:T(8,128)}, u32[]{:S(2)}) copy-start(f32[1,32,2048]{2,1,0:T(8,128)} %slice.55) | copy-start | bytes 786436
  114.5 11.0 %collective-permute-start.4 = (f32[1,32,2048]{2,1,0:T(8,128)S(1)}, f32[1,32,2048]{2,1,0:T(8,128)}, u32[]{:S(2)}, u32[]{:S(2)}) collective-permute-start(f32[1,32,2048]{2,1,0:T(8,128)S(1)} %copy.43), channel_id=1, source_target_pairs={{0,1},{1,0},{2,3},{3,2},{4,5},{5,4},{6,7},{7,6},{8,9},{9,8},{10,11... | collective-permute-start | bytes 786440 | tf_op jit(solution)/shard_map/ppermute | solution.py:40
  123.3 3.5 %copy-start.7 = (f32[216,256]{1,0:T(8,128)}, f32[216,256]{1,0:T(8,128)S(1)}, u32[]{:S(2)}) copy-start(f32[216,256]{1,0:T(8,128)S(1)} %reshape.41) | copy-start | bytes 663556
  123.3 4.9 %collective-permute-start.9 = (f32[216,256]{1,0:T(8,128)S(1)}, f32[216,256]{1,0:T(8,128)S(1)}, u32[]{:S(2)}, u32[]{:S(2)}) collective-permute-start(f32[216,256]{1,0:T(8,128)S(1)} %reshape.41), channel_id=1, source_target_pairs={{0,128},{128,0},{1,129},{129,1},{2,130},{130,2},{3,131},{131,3},{4... | collective-permute-start | bytes 663560 | tf_op jit(solution)/shard_map/ppermute | solution.py:49
  129.9 7.7 %collective-permute-start.10 = (f32[432,256]{1,0:T(8,128)}, f32[432,256]{1,0:T(8,128)}, u32[]{:S(2)}, u32[]{:S(2)}) collective-permute-start(f32[432,256]{1,0:T(8,128)} %pad_maximum_fusion.1), channel_id=1, source_target_pairs={{0,8},{8,0},{1,9},{9,1},{2,10},{10,2},{3,11},{11,3},{4,12},{12,4},... | collective-permute-start | bytes 1327112 | tf_op jit(solution)/shard_map/ppermute | solution.py:49

commit v6 on v3

--- a/solution.py
+++ b/solution.py
@@ -103,18 +103,6 @@
             for tap_depth in range(3):
                 pieces[tap_depth * 9 + tap_row * 3 + tap_col] = block[tap_depth]
     return jnp.stack(pieces, axis=0)
-
-
-def conv_forward(padded, taps):
-    planes, channels, cells = padded.shape
-    lhs = padded.reshape(1, planes, channels, PLANE_ROWS, ROW_CELLS)
-    rhs = taps.reshape(3, 3, 3, channels, taps.shape[-1])
-    out = lax.conv_general_dilated(
-        lhs, rhs, (1, 1, 1), [(0, 0), (1, 1), (1, 1)],
-        dimension_numbers=("NDCHW", "DHWIO", "NDCHW"),
-        preferred_element_type=jnp.float32,
-    )
-    return out.reshape(planes - 2, taps.shape[-1], cells)
 
 
 def conv_backward(cot_plane, taps):
@@ -161,6 +149,42 @@
                 )
 
 
+def forward_kernel(x_ref, w_ref, o_ref, col_ref):
+    cells = o_ref.shape[1]
+    width = x_ref.shape[-1]
+    channels = x_ref.shape[1]
+    column = lax.broadcasted_iota(jnp.int32, (channels, cells), 1) % ROW_CELLS
+    for tap_depth in range(3):
+        plane = x_ref[tap_depth].astype(jnp.float32)
+        for tap_row in range(3):
+            for tap_col in range(3):
+                offset = FLAT_EDGE + (tap_row - 1) * ROW_CELLS + (tap_col - 1)
+                moved = pltpu.roll(plane, (width - offset) % width, 1)[:, :cells]
+                if tap_col == 0:
+                    moved = jnp.where(column >= 1, moved, 0.0)
+                if tap_col == 2:
+                    moved = jnp.where(column < ROW_CELLS - 1, moved, 0.0)
+                tap = tap_depth * 9 + tap_row * 3 + tap_col
+                col_ref[pl.ds(tap * channels, channels), :] = moved.astype(jnp.bfloat16)
+    spare = col_ref.shape[0] - 27 * channels
+    col_ref[pl.ds(27 * channels, spare), :] = jnp.zeros((spare, cells), jnp.bfloat16)
+    o_ref[...] = jnp.dot(w_ref[...], col_ref[...], preferred_element_type=jnp.float32)
+
+
+def conv_forward(padded, taps):
+    planes, channels, cells = padded.shape
+    flat = jnp.pad(padded, ((0, 0), (0, 0), (FLAT_EDGE, FLAT_EDGE)))
+    rows = 27 * channels
+    depth = -(-rows // 128) * 128
+    lhs = jnp.pad(taps.reshape(rows, taps.shape[-1]), ((0, depth - rows), (0, 0))).T
+    out = pl.pallas_call(
+        forward_kernel,
+        out_shape=jax.ShapeDtypeStruct((taps.shape[-1], cells), jnp.float32),
+        scratch_shapes=[pltpu.VMEM((depth, cells), jnp.bfloat16)],
+    )(flat, lhs)
+    return out.reshape(planes - 2, taps.shape[-1], cells)
+
+
 def conv_filter(padded, cot_whole):
     planes, channels, cells = padded.shape
     flat = jnp.pad(padded, ((0, 0), (0, 0), (FLAT_EDGE, FLAT_EDGE)))

time: 135 us -> 140 us (1.037); the launches traced: 134 us -> 137 us
  local copies, waits for them, and re-layouts: 46.6 us -> 23.8 us
  starting transfers between devices: 44.4 us -> 59.2 us
  waiting for transfers between devices: 9.81 us -> 22.8 us
  matrix products: 9.7 us -> 5.77 us
  Pallas kernels: 7.28 us -> 11.1 us
  other arithmetic: 15.3 us -> 13.4 us
    all_to_all x2, waiting for transfers between devices: 0.01 us -> 16.9 us  [spread_gather(): copies = lax.all_to_all(copies, axis, 0, 0, tiled=True)]
    ppermute x4, starting transfers between devices: 6.54 us -> 22.1 us  [halving_sum(): lax.ppermute(send, axis, [(i, i ^ mask) for i in range(count)])]
    ppermute x4, waiting for transfers between devices: 8.5 us -> 0.01 us  [halving_sum(): lax.ppermute(send, axis, [(i, i ^ mask) for i in range(count)])]
    conv_general_dilated x5 -> x0, local copies, waits for them, and re-layouts: 5.68 us -> none  [conv_forward(): lax.conv_general_dilated(lhs, rhs, (1, 1, 1), [(0, 0), (1, 1), (1, 1)], d...]
    reshape x3 -> x1, local copies, waits for them, and re-layouts: 4.66 us -> 0.25 us  [conv_forward(): taps.reshape(rows, taps.shape[-1])]
    all_to_all x1, waiting for transfers between devices: 0.93 us -> 5.13 us  [scatter_sum(): parts = lax.all_to_all(parts, axis, 0, 0, tiled=True)]
    conv_general_dilated x1 -> x0, matrix products: 3.94 us -> none  [conv_forward(): lax.conv_general_dilated(lhs, rhs, (1, 1, 1), [(0, 0), (1, 1), (1, 1)], d...]
    pallas_call x0 -> x1, Pallas kernels: none -> 3.84 us  [conv_forward(): pl.pallas_call(forward_kernel, out_shape=jax.ShapeDtypeStruct((taps.shape...]
  transfers between devices with their start and end apart: 12 -> 12, of which waited for: 3 -> 4; matrix products, arithmetic and copies ran while one was open for 51% -> 30% of each run, Pallas kernels for 5% -> 8%
where the time goes in v6:
time: 140 us; the launch traced here: 137 us
  starting transfers between devices  59.2 us (42%)
  local copies, waits for them, and re-layouts  23.8 us (17%)
  waiting for transfers between devices  22.8 us (16%)
  other arithmetic  13.4 us (10%)
  Pallas kernels  11.1 us (8%)
  matrix products  5.77 us (4%)
    ppermute x4, starting transfers between devices, halving_sum(): lax.ppermute(send, axis, [(i, i ^ mask) for i in range(count)])  22.1 us
    all_to_all x2, waiting for transfers between devices, spread_gather(): copies = lax.all_to_all(copies, axis, 0, 0, tiled=True)  16.9 us
    all_to_all x2, starting transfers between devices, spread_gather(): copies = lax.all_to_all(copies, axis, 0, 0, tiled=True)  13.2 us
    pallas_call x1, Pallas kernels, conv_filter(): pl.pallas_call(filter_kernel, out_shape=jax.ShapeDtypeStruct((27, channel...  7.28 us
    all_to_all x1, starting transfers between devices, scatter_sum(): parts = lax.all_to_all(parts, axis, 0, 0, tiled=True)  6.27 us
    conv_general_dilated x1, matrix products, conv_backward(): lax.conv_general_dilated(lhs, rhs, (1, 1, 1), [(2, 2), (1, 1), (1, 1)], d...  5.77 us
    ppermute x1, starting transfers between devices, spill_sum(): from_low = lax.ppermute(parts[-1:], axis, forward)  5.67 us
    select_n x4, other arithmetic, halving_sum(): send = jnp.where(upper, low, high)  5.53 us
  transfers between devices with their start and end apart: 12, of which 4 were waited for; matrix products, arithmetic and copies ran while one was open for 30% of the time, Pallas kernels for 8%

profile of v6, /device:TPU:1, one launch (start us, length us, event | category | flops | bytes accessed | tf_op | source)
XLA Modules:
  0.0 137.1 jit_solution(7906797676164856147)
XLA Ops:
  0.6 4.9 %collective-permute-start = (bf16[1,32,2048]{2,1,0:T(8,128)(2,1)}, bf16[1,32,2048]{2,1,0:T(8,128)(2,1)S(1)}, u32[]{:S(2)}, u32[]{:S(2)}) collective-permute-start(bf16[1,32,2048]{2,1,0:T(8,128)(2,1)} %param.3), channel_id=1, source_target_pairs={{0,8},{8,16},{16,24},{24,32},{32,40},{40,48},{48,56},{56,64},{64,7... | collective-permute-start | bytes 393224 | tf_op jit(solution)/shard_map/ppermute | solution.py:17
  5.6 1.9 %collective-permute-start.1 = (bf16[1,32,2048]{2,1,0:T(8,128)(2,1)}, bf16[1,32,2048]{2,1,0:T(8,128)(2,1)S(1)}, u32[]{:S(2)}, u32[]{:S(2)}) collective-permute-start(bf16[1,32,2048]{2,1,0:T(8,128)(2,1)} %param.3), channel_id=1, source_target_pairs={{8,0},{16,8},{24,16},{32,24},{40,32},{48,40},{56,48},{64,56},{72,6... | collective-permute-start | bytes 393224 | tf_op jit(solution)/shard_map/ppermute | solution.py:20
  7.5 2.1 %broadcast_in_dim.7 = bf16[8,1,32,2048]{3,2,1,0:T(8,128)(2,1)} broadcast(bf16[32,2048]{1,0:T(8,128)(2,1)} %bitcast.45), dimensions={2,3} | broadcast | bytes 1179648 | tf_op jit(solution)/shard_map/broadcast_in_dim | solution.py:209
  9.6 6.7 %all-to-all-start = ((bf16[8,1,32,2048]{3,2,1,0:T(8,128)(2,1)}), bf16[8,1,32,2048]{3,2,1,0:T(8,128)(2,1)S(1)}, u32[]{:S(2)}, u32[]{:S(2)}) async-start(bf16[8,1,32,2048]{3,2,1,0:T(8,128)(2,1)} %broadcast_in_dim.7), calls=%async_computation | async-start | bytes 2097152 | tf_op jit(solution)/shard_map/all_to_all | solution.py:210
  16.3 0.2 copy.27
  16.5 0.8 pad_bitcast_fusion.w_ref
  17.4 0.8 fusion.13.x_ref
  18.2 3.8 %shard_map.58 = f32[256,2048]{1,0:T(8,128)} custom-call(bf16[3,32,2304]{2,1,0:T(8,128)(2,1)} %fusion.13.x_ref, bf16[256,896]{1,0:T(8,128)(2,1)} %pad_bitcast_fusion.w_ref), custom_call_target="tpu_custom_call" | custom-call | tf_op jit(solution)/shard_map/pallas_call | solution.py:180
  22.0 2.7 %slice_select_fusion = f32[1,128,2048]{2,1,0:T(8,128)} fusion(f32[1,256,2048]{2,1,0:T(8,128)} %bitcast.32, pred[]{:T(512)S(6)} %eq.21), kind=kLoop, calls=%fused_computation.14 | loop fusion | flops 262144 | bytes 3145729 | tf_op jit(solution)/shard_map/jit(_where)/select_n | solution.py:39
  24.7 2.9 %collective-permute-start.2 = (f32[1,128,2048]{2,1,0:T(8,128)}, f32[1,128,2048]{2,1,0:T(8,128)}, u32[]{:S(2)}, u32[]{:S(2)}) collective-permute-start(f32[1,128,2048]{2,1,0:T(8,128)} %slice_select_fusion), channel_id=1, source_target_pairs={{0,4},{1,5},{2,6},{3,7},{4,0},{5,1},{6,2},{7,3},{8,12},{9,13},{10,... | collective-permute-start | bytes 3145736 | tf_op jit(solution)/shard_map/ppermute | solution.py:40
  27.6 4.7 %all-to-all-done = bf16[8,1,32,2048]{3,2,1,0:T(8,128)(2,1)S(1)} async-done(((bf16[8,1,32,2048]{3,2,1,0:T(8,128)(2,1)}), bf16[8,1,32,2048]{3,2,1,0:T(8,128)(2,1)S(1)}, u32[]{:S(2)}, u32[]{:S(2)}) %all-to-all-start) | async-done | bytes 1048608 | tf_op jit(solution)/shard_map/all_to_all | solution.py:210
  32.2 1.3 copy.37
  33.5 7.3 %shard_map.59 = f32[27,32,256]{2,1,0:T(8,128)} custom-call(bf16[3,32,2304]{2,1,0:T(8,128)(2,1)} %fusion.13.x_ref, bf16[2048,256]{1,0:T(8,128)(2,1)} %bitcast.41), custom_call_target="tpu_custom_call" | custom-call | tf_op jit(solution)/shard_map/pallas_call | solution.py:192
  40.8 2.0 %slice_select_fusion.2 = f32[432,256]{1,0:T(8,128)} fusion(f32[864,256]{1,0:T(8,128)} %bitcast.35, pred[]{:T(512)S(6)} %eq.22), kind=kLoop, calls=%fused_computation.27 | loop fusion | flops 110592 | bytes 1327105 | tf_op jit(solution)/shard_map/jit(_where)/select_n | solution.py:39
  42.8 2.2 %reshape.53 = bf16[1,256,32,1,64]{4,2,1,3,0:T(8,128)(2,1)S(1)} reshape(bf16[8,1,32,2048]{3,2,1,0:T(8,128)(2,1)S(1)} %all-to-all-done) | data formatting | bytes 2097152 | tf_op jit(solution)/shard_map/reshape;reshape;transpose | solution.py:110
  45.0 2.7 %copy.38 = bf16[1,256,32,1,64]{1,2,4,3,0:T(8,128)(2,1)S(1)} copy(bf16[1,256,32,1,64]{4,2,1,3,0:T(8,128)(2,1)S(1)} %reshape.53) | data formatting | bytes 2097152
  47.8 0.7 copy.30
  48.5 0.3 copy-done.5
  48.8 5.8 %convolution_select_fusion = f32[3,32,8,9,32]{4,2,3,1,0:T(8,128)S(1)} fusion(bf16[3,3,3,32,256]{4,3,2,1,0:T(8,128)(2,1)S(1)} %bitcast.44, pred[8,9]{0,1:T(8,128)(4,1)S(1)} %copy-done.7, bf16[1,256,32,1,7,2]{1,4,5,2,3,0:T(8,128)(2,1)S(1)} %slice.69, bf16[1,256,32,1,8,9]{1,4,5,2,3,0:T(8,128)(2,1)S(1)} %copy.30), kind=kOutput, calls=%fused_computation.2 | convolution fusion | flops 1002528768 | bytes 2736200 | tf_op jit(solution)/shard_map/conv_general_dilated | solution.py:112
  54.5 1.2 fusion.17
  56.1 1.6 %copy.34 = f32[1,1,32,32,64]{4,3,2,1,0:T(8,128)} copy(f32[1,1,32,32,64]{2,3,4,0,1:T(8,128)S(1)} %slice_bitcast_fusion.1) | data formatting | bytes 524288 | tf_op jit(solution)/shard_map/slice | solution.py:124
  57.7 2.1 %slice.51 = f32[1,32,2048]{2,1,0:T(8,128)} reshape(f32[1,1,32,32,64]{4,3,2,1,0:T(8,128)} %copy.34) | data formatting | bytes 524288 | tf_op jit(solution)/shard_map/slice | solution.py:124
  59.8 5.7 %collective-permute-start.5 = (f32[1,32,2048]{2,1,0:T(8,128)}, f32[1,32,2048]{2,1,0:T(8,128)S(1)}, u32[]{:S(2)}, u32[]{:S(2)}) collective-permute-start(f32[1,32,2048]{2,1,0:T(8,128)} %slice.51), channel_id=1, source_target_pairs={{0,8},{8,16},{16,24},{24,32},{32,40},{40,48},{48,56},{56,64},{64,7... | collective-permute-start | bytes 786440 | tf_op jit(solution)/shard_map/ppermute | solution.py:124
  65.4 1.2 copy.35
  66.7 1.4 %select_add_fusion = f32[1,128,2048]{2,1,0:T(8,128)S(1)} fusion(f32[1,128,2048]{2,1,0:T(8,128)} %collective-permute-done.2, f32[1,256,2048]{2,1,0:T(8,128)S(1)} %bitcast.33, pred[]{:T(512)S(6)} %eq.21), kind=kLoop, calls=%fused_computation.13 | loop fusion | flops 524288 | bytes 4194305 | tf_op jit(solution)/shard_map/add | solution.py:40
  68.1 0.9 slice_select_fusion.1
  68.9 18.5 %collective-permute-start.3 = (f32[1,64,2048]{2,1,0:T(8,128)}, f32[1,64,2048]{2,1,0:T(8,128)}, u32[]{:S(2)}, u32[]{:S(2)}) collective-permute-start(f32[1,64,2048]{2,1,0:T(8,128)} %slice_select_fusion.1), channel_id=1, source_target_pairs={{0,2},{1,3},{2,0},{3,1},{4,6},{5,7},{6,4},{7,5},{8,10},{9,11},{10,... | collective-permute-start | bytes 1572872 | tf_op jit(solution)/shard_map/ppermute | solution.py:40
  87.4 1.1 select_add_fusion.2
  88.5 0.9 reshape.39
  89.4 6.3 %all-to-all-start.1 = ((f32[16,27,256]{2,1,0:T(8,128)}), f32[16,27,256]{2,1,0:T(8,128)}, u32[]{:S(2)}, u32[]{:S(2)}) async-start(f32[16,27,256]{2,1,0:T(8,128)} %reshape.39), calls=%async_computation.1 | async-start | bytes 1048576 | tf_op jit(solution)/shard_map/all_to_all | solution.py:203
  95.7 1.1 slice_bitcast_fusion
  96.8 2.0 %copy.36 = f32[1,1,32,32,64]{4,3,2,1,0:T(8,128)S(1)} copy(f32[1,1,32,32,64]{2,3,4,0,1:T(8,128)} %slice_bitcast_fusion) | data formatting | bytes 524288 | tf_op jit(solution)/shard_map/slice | solution.py:125
  98.8 0.9 slice.53
  99.7 2.3 %collective-permute-start.6 = (f32[1,32,2048]{2,1,0:T(8,128)}, f32[1,32,2048]{2,1,0:T(8,128)S(1)}, u32[]{:S(2)}, u32[]{:S(2)}) collective-permute-start(f32[1,32,2048]{2,1,0:T(8,128)} %slice.53), channel_id=1, source_target_pairs={{8,0},{16,8},{24,16},{32,24},{40,32},{48,40},{56,48},{64,56},{72,6... | collective-permute-start | bytes 786440 | tf_op jit(solution)/shard_map/ppermute | solution.py:125
  102.0 0.2 copy.31
  102.3 0.8 copy.32
  103.3 1.1 select_add_fusion.1
  104.4 5.1 %all-to-all-done.1 = f32[16,27,256]{2,1,0:T(8,128)} async-done(((f32[16,27,256]{2,1,0:T(8,128)}), f32[16,27,256]{2,1,0:T(8,128)}, u32[]{:S(2)}, u32[]{:S(2)}) %all-to-all-start.1) | async-done | bytes 442400 | tf_op jit(solution)/shard_map/all_to_all | solution.py:203
  109.5 1.1 reduce_sum.9
  110.6 0.8 broadcast_in_dim.16
  111.5 6.6 %all-to-all-start.2 = ((f32[16,27,256]{2,1,0:T(8,128)}), f32[16,27,256]{2,1,0:T(8,128)S(1)}, u32[]{:S(2)}, u32[]{:S(2)}) async-start(f32[16,27,256]{2,1,0:T(8,128)} %broadcast_in_dim.16), calls=%async_computation.2 | async-start | bytes 1048576 | tf_op jit(solution)/shard_map/all_to_all | solution.py:210
  118.1 0.7 collective-permute-start.4
  118.8 0.7 add_convert_fusion
  119.5 12.2 %all-to-all-done.2 = f32[16,27,256]{2,1,0:T(8,128)S(1)} async-done(((f32[16,27,256]{2,1,0:T(8,128)}), f32[16,27,256]{2,1,0:T(8,128)S(1)}, u32[]{:S(2)}, u32[]{:S(2)}) %all-to-all-start.2) | async-done | bytes 442400 | tf_op jit(solution)/shard_map/all_to_all | solution.py:210
  131.8 2.8 %collective-permute-start.8 = (f32[432,256]{1,0:T(8,128)S(1)}, f32[432,256]{1,0:T(8,128)S(1)}, u32[]{:S(2)}, u32[]{:S(2)}) collective-permute-start(f32[432,256]{1,0:T(8,128)S(1)} %reshape.40), channel_id=1, source_target_pairs={{0,8},{8,0},{1,9},{9,1},{2,10},{10,2},{3,11},{11,3},{4,12},{12,4},... | collective-permute-start | bytes 1327112 | tf_op jit(solution)/shard_map/ppermute | solution.py:49
  134.6 0.7 add_convert_fusion.1
  135.3 0.7 collective-permute-done.8
  136.1 1.0 pad_maximum_fusion
  (33 shorter events, 0.9 us)
Async XLA Ops:
  0.6 16.7 %collective-permute-start = (bf16[1,32,2048]{2,1,0:T(8,128)(2,1)}, bf16[1,32,2048]{2,1,0:T(8,128)(2,1)S(1)}, u32[]{:S(2)}, u32[]{:S(2)}) collective-permute-start(bf16[1,32,2048]{2,1,0:T(8,128)(2,1)} %param.3), channel_id=1, source_target_pairs={{0,8},{8,16},{16,24},{24,32},{32,40},{40,48},{48,56},{56,64},{64,7... | collective-permute-start | bytes 393224 | tf_op jit(solution)/shard_map/ppermute | solution.py:17
  5.6 11.8 %collective-permute-start.1 = (bf16[1,32,2048]{2,1,0:T(8,128)(2,1)}, bf16[1,32,2048]{2,1,0:T(8,128)(2,1)S(1)}, u32[]{:S(2)}, u32[]{:S(2)}) collective-permute-start(bf16[1,32,2048]{2,1,0:T(8,128)(2,1)} %param.3), channel_id=1, source_target_pairs={{8,0},{16,8},{24,16},{32,24},{40,32},{48,40},{56,48},{64,56},{72,6... | collective-permute-start | bytes 393224 | tf_op jit(solution)/shard_map/ppermute | solution.py:20
  7.5 8.8 %copy-start.4 = (bf16[27,32,256]{2,1,0:T(8,128)(2,1)S(1)}, bf16[27,32,256]{2,1,0:T(8,128)(2,1)}, u32[]{:S(2)}) copy-start(bf16[27,32,256]{2,1,0:T(8,128)(2,1)} %param.4) | copy-start | bytes 1327108
  9.6 22.7 %all-to-all-start = ((bf16[8,1,32,2048]{3,2,1,0:T(8,128)(2,1)}), bf16[8,1,32,2048]{3,2,1,0:T(8,128)(2,1)S(1)}, u32[]{:S(2)}, u32[]{:S(2)}) async-start(bf16[8,1,32,2048]{3,2,1,0:T(8,128)(2,1)} %broadcast_in_dim.7), calls=%async_computation | async-start | bytes 2097152 | tf_op jit(solution)/shard_map/all_to_all | solution.py:210
  16.2 1.2 copy-start.6
  24.7 42.0 %collective-permute-start.2 = (f32[1,128,2048]{2,1,0:T(8,128)}, f32[1,128,2048]{2,1,0:T(8,128)}, u32[]{:S(2)}, u32[]{:S(2)}) collective-permute-start(f32[1,128,2048]{2,1,0:T(8,128)} %slice_select_fusion), channel_id=1, source_target_pairs={{0,4},{1,5},{2,6},{3,7},{4,0},{5,1},{6,2},{7,3},{8,12},{9,13},{10,... | collective-permute-start | bytes 3145736 | tf_op jit(solution)/shard_map/ppermute | solution.py:40
  42.8 44.6 %collective-permute-start.7 = (f32[432,256]{1,0:T(8,128)}, f32[432,256]{1,0:T(8,128)}, u32[]{:S(2)}, u32[]{:S(2)}) collective-permute-start(f32[432,256]{1,0:T(8,128)} %slice_select_fusion.2), channel_id=1, source_target_pairs={{0,8},{8,0},{1,9},{9,1},{2,10},{10,2},{3,11},{11,3},{4,12},{12,4},... | collective-permute-start | bytes 1327112 | tf_op jit(solution)/shard_map/ppermute | solution.py:40
  47.7 1.0 copy-start.5
  47.8 1.0 copy-start.7
  57.7 9.0 %copy-start = (f32[256,2048]{1,0:T(8,128)S(1)}, f32[256,2048]{1,0:T(8,128)}, u32[]{:S(2)}) copy-start(f32[256,2048]{1,0:T(8,128)} %shard_map.58) | copy-start | bytes 6291460
  59.8 59.0 %collective-permute-start.5 = (f32[1,32,2048]{2,1,0:T(8,128)}, f32[1,32,2048]{2,1,0:T(8,128)S(1)}, u32[]{:S(2)}, u32[]{:S(2)}) collective-permute-start(f32[1,32,2048]{2,1,0:T(8,128)} %slice.51), channel_id=1, source_target_pairs={{0,8},{8,16},{16,24},{24,32},{32,40},{40,48},{48,56},{56,64},{64,7... | collective-permute-start | bytes 786440 | tf_op jit(solution)/shard_map/ppermute | solution.py:124
  68.1 19.4 %copy-start.1 = (f32[27,32,256]{2,1,0:T(8,128)S(1)}, f32[27,32,256]{2,1,0:T(8,128)}, u32[]{:S(2)}) copy-start(f32[27,32,256]{2,1,0:T(8,128)} %shard_map.59) | copy-start | bytes 2654212
  68.9 34.3 %collective-permute-start.3 = (f32[1,64,2048]{2,1,0:T(8,128)}, f32[1,64,2048]{2,1,0:T(8,128)}, u32[]{:S(2)}, u32[]{:S(2)}) collective-permute-start(f32[1,64,2048]{2,1,0:T(8,128)} %slice_select_fusion.1), channel_id=1, source_target_pairs={{0,2},{1,3},{2,0},{3,1},{4,6},{5,7},{6,4},{7,5},{8,10},{9,11},{10,... | collective-permute-start | bytes 1572872 | tf_op jit(solution)/shard_map/ppermute | solution.py:40
  88.5 7.1 %copy-start.3 = (f32[1,32,8,9,32]{4,1,3,2,0:T(8,128)S(1)}, f32[1,32,8,9,32]{4,1,3,2,0:T(8,128)}, u32[]{:S(2)}) copy-start(f32[1,32,8,9,32]{4,1,3,2,0:T(8,128)} %copy.35) | copy-start | bytes 884740
  89.4 20.1 %all-to-all-start.1 = ((f32[16,27,256]{2,1,0:T(8,128)}), f32[16,27,256]{2,1,0:T(8,128)}, u32[]{:S(2)}, u32[]{:S(2)}) async-start(f32[16,27,256]{2,1,0:T(8,128)} %reshape.39), calls=%async_computation.1 | async-start | bytes 1048576 | tf_op jit(solution)/shard_map/all_to_all | solution.py:203
  96.7 5.2 %copy-start.2 = (f32[1,32,8,9,32]{4,2,3,1,0:T(8,128)S(1)}, f32[1,32,8,9,32]{4,2,3,1,0:T(8,128)}, u32[]{:S(2)}) copy-start(f32[1,32,8,9,32]{4,2,3,1,0:T(8,128)} %get-tuple-element.5) | copy-start | bytes 884740
  99.7 19.1 %collective-permute-start.6 = (f32[1,32,2048]{2,1,0:T(8,128)}, f32[1,32,2048]{2,1,0:T(8,128)S(1)}, u32[]{:S(2)}, u32[]{:S(2)}) collective-permute-start(f32[1,32,2048]{2,1,0:T(8,128)} %slice.53), channel_id=1, source_target_pairs={{8,0},{16,8},{24,16},{32,24},{40,32},{48,40},{56,48},{64,56},{72,6... | collective-permute-start | bytes 786440 | tf_op jit(solution)/shard_map/ppermute | solution.py:125
  111.5 20.2 %all-to-all-start.2 = ((f32[16,27,256]{2,1,0:T(8,128)}), f32[16,27,256]{2,1,0:T(8,128)S(1)}, u32[]{:S(2)}, u32[]{:S(2)}) async-start(f32[16,27,256]{2,1,0:T(8,128)} %broadcast_in_dim.16), calls=%async_computation.2 | async-start | bytes 1048576 | tf_op jit(solution)/shard_map/all_to_all | solution.py:210
  118.1 16.5 %collective-permute-start.4 = (f32[1,32,2048]{2,1,0:T(8,128)S(1)}, f32[1,32,2048]{2,1,0:T(8,128)S(1)}, u32[]{:S(2)}, u32[]{:S(2)}) collective-permute-start(f32[1,32,2048]{2,1,0:T(8,128)S(1)} %slice_select_fusion.3), channel_id=1, source_target_pairs={{0,1},{1,0},{2,3},{3,2},{4,5},{5,4},{6,7},{7,6},{8,9},{9,8},{10,11... | collective-permute-start | bytes 786440 | tf_op jit(solution)/shard_map/ppermute | solution.py:40
  131.8 4.3 %collective-permute-start.8 = (f32[432,256]{1,0:T(8,128)S(1)}, f32[432,256]{1,0:T(8,128)S(1)}, u32[]{:S(2)}, u32[]{:S(2)}) collective-permute-start(f32[432,256]{1,0:T(8,128)S(1)} %reshape.40), channel_id=1, source_target_pairs={{0,8},{8,0},{1,9},{9,1},{2,10},{10,2},{3,11},{11,3},{4,12},{12,4},... | collective-permute-start | bytes 1327112 | tf_op jit(solution)/shard_map/ppermute | solution.py:49

commit v7 on v3

--- a/solution.py
+++ b/solution.py
@@ -32,11 +32,9 @@
     index = lax.axis_index(axis)
     for mask in masks:
         half = block.shape[dim] // 2
-        upper = (index // mask) % 2 == 1
-        low = lax.slice_in_dim(block, 0, half, axis=dim)
-        high = lax.slice_in_dim(block, half, 2 * half, axis=dim)
-        keep = jnp.where(upper, high, low)
-        send = jnp.where(upper, low, high)
+        upper = (index // mask) % 2
+        keep = lax.dynamic_slice_in_dim(block, upper * half, half, axis=dim)
+        send = lax.dynamic_slice_in_dim(block, (1 - upper) * half, half, axis=dim)
         block = keep + lax.ppermute(send, axis, [(i, i ^ mask) for i in range(count)])
     return block
 

time: 135 us -> 137 us (1.015)
  other arithmetic: 15.3 us -> 9.48 us
  local copies, waits for them, and re-layouts: 46.6 us -> 51.2 us
  waiting for transfers between devices: 9.81 us -> 11.5 us
    dynamic_slice x0 -> x6, local copies, waits for them, and re-layouts: none -> 8.02 us  [halving_sum(): send = lax.dynamic_slice_in_dim(block, (1 - upper) * half, half, axis=dim)]
    select_n x4 -> x0, other arithmetic: 4.72 us -> none  [halving_sum(): send = jnp.where(upper, low, high)]
    select_n x2 -> x0, local copies, waits for them, and re-layouts: 3.35 us -> none  [halving_sum(): send = jnp.where(upper, low, high)]
    ppermute x4, waiting for transfers between devices: 8.5 us -> 11.1 us  [halving_sum(): lax.ppermute(send, axis, [(i, i ^ mask) for i in range(count)])]
    slice x3, local copies, waits for them, and re-layouts: 1.73 us -> 3.54 us  [spill_sum(): from_low = lax.ppermute(parts[-1:], axis, forward)]
  transfers between devices with their start and end apart: 12 -> 12, of which waited for: 3 -> 3; matrix products, arithmetic and copies ran while one was open for 51% -> 50% of each run, Pallas kernels for 5% -> 5%
where the time goes in v7:
time: 137 us; the launch traced here: 136 us
  local copies, waits for them, and re-layouts  51.2 us (37%)
  starting transfers between devices  45.5 us (33%)
  waiting for transfers between devices  11.5 us (8%)
  matrix products  9.7 us (7%)
  other arithmetic  9.48 us (7%)
  Pallas kernels  7.28 us (5%)
    all_to_all x2, starting transfers between devices, spread_gather(): copies = lax.all_to_all(copies, axis, 0, 0, tiled=True)  13.9 us
    ppermute x4, waiting for transfers between devices, halving_sum(): lax.ppermute(send, axis, [(i, i ^ mask) for i in range(count)])  11.1 us
    all_to_all x1, starting transfers between devices, scatter_sum(): parts = lax.all_to_all(parts, axis, 0, 0, tiled=True)  8.31 us
    dynamic_slice x6, local copies, waits for them, and re-layouts, halving_sum(): send = lax.dynamic_slice_in_dim(block, (1 - upper) * half, half, axis=dim)  8.02 us
    pallas_call x1, Pallas kernels, conv_filter(): pl.pallas_call(filter_kernel, out_shape=jax.ShapeDtypeStruct((27, channel...  7.28 us
    ppermute x4, starting transfers between devices, halving_sum(): lax.ppermute(send, axis, [(i, i ^ mask) for i in range(count)])  6.52 us
    conv_general_dilated x1, matrix products, conv_backward(): lax.conv_general_dilated(lhs, rhs, (1, 1, 1), [(2, 2), (1, 1), (1, 1)], d...  5.76 us
    conv_general_dilated x5, local copies, waits for them, and re-layouts, conv_forward(): lax.conv_general_dilated(lhs, rhs, (1, 1, 1), [(0, 0), (1, 1), (1, 1)], d...  5.68 us
  transfers between devices with their start and end apart: 12, of which 3 were waited for; matrix products, arithmetic and copies ran while one was open for 50% of the time, Pallas kernels for 5%

profile of v7, /device:TPU:1, one launch (start us, length us, event | category | flops | bytes accessed | tf_op | source)
XLA Modules:
  0.0 135.7 jit_solution(14986689360840187258)
XLA Ops:
  0.7 5.1 %collective-permute-start = (bf16[1,32,2048]{2,1,0:T(8,128)(2,1)}, bf16[1,32,2048]{2,1,0:T(8,128)(2,1)S(1)}, u32[]{:S(2)}, u32[]{:S(2)}) collective-permute-start(bf16[1,32,2048]{2,1,0:T(8,128)(2,1)} %param.3), channel_id=1, source_target_pairs={{0,8},{8,16},{16,24},{24,32},{32,40},{40,48},{48,56},{56,64},{64,7... | collective-permute-start | bytes 393224 | tf_op jit(solution)/shard_map/ppermute | solution.py:17
  5.7 1.9 %collective-permute-start.1 = (bf16[1,32,2048]{2,1,0:T(8,128)(2,1)}, bf16[1,32,2048]{2,1,0:T(8,128)(2,1)S(1)}, u32[]{:S(2)}, u32[]{:S(2)}) collective-permute-start(bf16[1,32,2048]{2,1,0:T(8,128)(2,1)} %param.3), channel_id=1, source_target_pairs={{8,0},{16,8},{24,16},{32,24},{40,32},{48,40},{56,48},{64,56},{72,6... | collective-permute-start | bytes 393224 | tf_op jit(solution)/shard_map/ppermute | solution.py:20
  7.6 2.0 %broadcast_in_dim.7 = bf16[8,1,32,2048]{3,2,1,0:T(8,128)(2,1)} broadcast(bf16[32,2048]{1,0:T(8,128)(2,1)} %bitcast.54), dimensions={2,3} | broadcast | bytes 1179648 | tf_op jit(solution)/shard_map/broadcast_in_dim | solution.py:183
  9.6 6.7 %all-to-all-start = ((bf16[8,1,32,2048]{3,2,1,0:T(8,128)(2,1)}), bf16[8,1,32,2048]{3,2,1,0:T(8,128)(2,1)S(1)}, u32[]{:S(2)}, u32[]{:S(2)}) async-start(bf16[8,1,32,2048]{3,2,1,0:T(8,128)(2,1)} %broadcast_in_dim.7), calls=%async_computation | async-start | bytes 2097152 | tf_op jit(solution)/shard_map/all_to_all | solution.py:184
  17.2 2.1 %copy.36 = bf16[3,32,32,1,64]{2,1,4,0,3:T(8,128)(2,1)} copy(bf16[3,32,32,1,64]{4,2,1,0,3:T(8,128)(2,1)S(1)} %reshape.61) | data formatting | bytes 786432 | tf_op jit(solution)/shard_map/reshape | solution.py:108
  19.3 1.8 %pad.5 = bf16[3,32,32,1,72]{2,1,4,0,3:T(8,128)(2,1)S(1)} pad(bf16[3,32,32,1,64]{2,1,4,0,3:T(8,128)(2,1)} %copy.36, bf16[]{:T(256)} %constant.88.clone.1), padding=0_0x0_0x0_0x0_0x1_7 | pad | bytes 835586 | tf_op jit(solution)/shard_map/reshape | solution.py:108
  21.1 2.4 %copy.38 = bf16[3,32,32,1,8,9]{1,4,5,2,0,3:T(8,128)(2,1)} copy(bf16[3,32,32,1,8,9]{2,1,5,4,0,3:T(8,128)(2,1)S(1)} %bitcast.45) | data formatting | bytes 884736 | tf_op jit(solution)/shard_map/conv_general_dilated | solution.py:110
  23.4 1.1 slice.33
  24.6 3.9 %fusion.9 = f32[1,32,8,9,256]{4,2,3,1,0:T(8,128)S(1)} fusion(bf16[3,3,3,32,256]{4,3,2,1,0:T(8,128)(2,1)S(1)} %bitcast.39, bf16[3,32,32,1,7,2]{1,4,5,2,0,3:T(8,128)(2,1)S(1)} %slice.33, bf16[3,32,32,1,8,9]{1,4,5,2,0,3:T(8,128)(2,1)} %copy.38, pred[8,9]{0,1:T(8,128)(4,1)S(1)} %copy-done.6), kind=kOutput, calls=%fused_computation.12 | convolution fusion | flops 1000194048 | bytes 3330120 | tf_op jit(solution)/shard_map/conv_general_dilated | solution.py:110
  30.3 1.2 copy.40
  31.6 1.2 constant_dynamic-slice_fusion.3
  33.2 3.0 %collective-permute-start.2 = (f32[1,128,2048]{1,2,0:T(8,128)}, f32[1,128,2048]{1,2,0:T(8,128)}, u32[]{:S(2)}, u32[]{:S(2)}) collective-permute-start(f32[1,128,2048]{1,2,0:T(8,128)} %constant_dynamic-slice_fusion.3), channel_id=1, source_target_pairs={{0,4},{1,5},{2,6},{3,7},{4,0},{5,1},{6,2},{7,3},{8,12},{9,13},{10,... | collective-permute-start | bytes 3145736 | tf_op jit(solution)/shard_map/ppermute | solution.py:38
  36.2 1.3 copy.54
  37.5 7.3 %shard_map.58 = f32[27,32,256]{2,1,0:T(8,128)} custom-call(bf16[3,32,2304]{2,1,0:T(8,128)(2,1)} %pad.4.x_ref, bf16[2048,256]{1,0:T(8,128)(2,1)} %bitcast.50), custom_call_target="tpu_custom_call" | custom-call | tf_op jit(solution)/shard_map/pallas_call | solution.py:166
  44.8 1.8 %constant_dynamic-slice_fusion = f32[432,256]{1,0:T(8,128)} fusion(f32[864,256]{1,0:T(8,128)} %bitcast.51, s32[]{:T(128)S(6)} %select_n.81), kind=kLoop, calls=%fused_computation.34 | loop fusion | bytes 884740 | tf_op jit(solution)/shard_map/dynamic_slice | solution.py:37
  46.6 3.1 %reshape.65 = bf16[1,256,32,1,64]{4,2,1,3,0:T(8,128)(2,1)} reshape(bf16[8,1,32,2048]{3,2,1,0:T(8,128)(2,1)S(1)} %all-to-all-done) | data formatting | bytes 2097152 | tf_op jit(solution)/shard_map/reshape;reshape;transpose | solution.py:120
  49.7 4.1 %copy.56 = bf16[1,256,32,1,64]{1,2,4,3,0:T(8,128)(2,1)S(1)} copy(bf16[1,256,32,1,64]{4,2,1,3,0:T(8,128)(2,1)} %reshape.65) | data formatting | bytes 2097152
  54.7 5.8 %convolution_select_fusion = f32[3,32,8,9,32]{4,2,3,1,0:T(8,128)S(1)} fusion(bf16[3,3,3,32,256]{4,3,2,1,0:T(8,128)(2,1)S(1)} %bitcast.40, pred[8,9]{0,1:T(8,128)(4,1)S(1)} %copy-done.6, bf16[1,256,32,1,7,2]{1,4,5,2,3,0:T(8,128)(2,1)S(1)} %slice.35, bf16[1,256,32,1,8,9]{1,4,5,2,3,0:T(8,128)(2,1)S(1)} %copy.47), kind=kOutput, calls=%fused_computation.11 | convolution fusion | flops 1002528768 | bytes 2736200 | tf_op jit(solution)/shard_map/conv_general_dilated | solution.py:122
  60.4 1.3 fusion.26
  62.0 1.5 %copy.51 = f32[1,1,32,32,64]{4,3,2,1,0:T(8,128)} copy(f32[1,1,32,32,64]{2,3,4,0,1:T(8,128)S(1)} %slice_bitcast_fusion.2) | data formatting | bytes 524288 | tf_op jit(solution)/shard_map/slice | solution.py:134
  63.6 1.9 %slice.21 = f32[1,32,2048]{2,1,0:T(8,128)} reshape(f32[1,1,32,32,64]{4,3,2,1,0:T(8,128)} %copy.51) | data formatting | bytes 524288 | tf_op jit(solution)/shard_map/slice | solution.py:134
  65.5 4.5 %collective-permute-start.5 = (f32[1,32,2048]{2,1,0:T(8,128)}, f32[1,32,2048]{2,1,0:T(8,128)}, u32[]{:S(2)}, u32[]{:S(2)}) collective-permute-start(f32[1,32,2048]{2,1,0:T(8,128)} %slice.21), channel_id=1, source_target_pairs={{0,8},{8,16},{16,24},{24,32},{32,40},{40,48},{48,56},{56,64},{64,7... | collective-permute-start | bytes 786440 | tf_op jit(solution)/shard_map/ppermute | solution.py:134
  70.0 2.5 %copy.52 = f32[1,32,8,9,32]{4,1,3,2,0:T(8,128)} copy(f32[1,32,8,9,32]{4,2,3,1,0:T(8,128)} %get-tuple-element.13) | data formatting | bytes 589824 | tf_op jit(solution)/shard_map/conv_general_dilated | solution.py:122
  72.5 1.1 dynamic-slice_add_fusion.2
  73.6 0.8 reshape.40
  74.4 8.3 %all-to-all-start.1 = ((f32[16,27,256]{2,1,0:T(8,128)}), f32[16,27,256]{2,1,0:T(8,128)}, u32[]{:S(2)}, u32[]{:S(2)}) async-start(f32[16,27,256]{2,1,0:T(8,128)} %reshape.40), calls=%async_computation.1 | async-start | bytes 1048576 | tf_op jit(solution)/shard_map/all_to_all | solution.py:177
  82.7 1.7 %dynamic-slice_add_fusion.1 = f32[1,128,2048]{1,2,0:T(8,128)S(1)} fusion(f32[1,128,2048]{1,2,0:T(8,128)} %collective-permute-done.2, f32[1,256,2048]{1,2,0:T(8,128)} %bitcast.44, s32[]{:T(128)S(6)} %select_n.69), kind=kLoop, calls=%fused_computation.24 | loop fusion | flops 262144 | bytes 3145732 | tf_op jit(solution)/shard_map/add | solution.py:38
  84.4 1.3 constant_dynamic-slice_fusion.2
  85.7 2.3 %copy.41 = f32[1,64,2048]{2,1,0:T(8,128)} copy(f32[1,64,2048]{1,2,0:T(8,128)} %constant_dynamic-slice_fusion.2) | data formatting | bytes 1048576 | tf_op jit(solution)/shard_map/dynamic_slice | solution.py:37
  88.4 2.3 %slice_bitcast_fusion.1 = f32[1,1,32,32,64]{2,3,4,0,1:T(8,128)} fusion(f32[1,32,1,72,32]{4,1,3,2,0:T(8,128)} %bitcast.47), kind=kLoop, calls=%fused_computation.19 | loop fusion | bytes 524288 | tf_op jit(solution)/shard_map/slice | solution.py:135
  90.6 1.9 %copy.53 = f32[1,1,32,32,64]{4,3,2,1,0:T(8,128)S(1)} copy(f32[1,1,32,32,64]{2,3,4,0,1:T(8,128)} %slice_bitcast_fusion.1) | data formatting | bytes 524288 | tf_op jit(solution)/shard_map/slice | solution.py:135
  92.6 0.9 slice.23
  93.5 2.8 %collective-permute-start.6 = (f32[1,32,2048]{2,1,0:T(8,128)}, f32[1,32,2048]{2,1,0:T(8,128)}, u32[]{:S(2)}, u32[]{:S(2)}) collective-permute-start(f32[1,32,2048]{2,1,0:T(8,128)} %slice.23), channel_id=1, source_target_pairs={{8,0},{16,8},{24,16},{32,24},{40,32},{48,40},{56,48},{64,56},{72,6... | collective-permute-start | bytes 786440 | tf_op jit(solution)/shard_map/ppermute | solution.py:135
  97.5 3.7 %collective-permute-done.3 = f32[1,64,2048]{2,1,0:T(8,128)} collective-permute-done((f32[1,64,2048]{2,1,0:T(8,128)}, f32[1,64,2048]{2,1,0:T(8,128)}, u32[]{:S(2)}, u32[]{:S(2)}) %collective-permute-start.3) | collective-permute-done | bytes 524320 | tf_op jit(solution)/shard_map/ppermute | solution.py:38
  101.3 2.4 %copy.42 = f32[1,64,2048]{1,2,0:T(8,128)} copy(f32[1,64,2048]{2,1,0:T(8,128)} %collective-permute-done.3) | data formatting | bytes 1048576 | tf_op jit(solution)/shard_map/ppermute | solution.py:38
  103.6 1.1 reduce_sum.9
  104.7 0.8 broadcast_in_dim.16
  105.6 7.2 %all-to-all-start.2 = ((f32[16,27,256]{2,1,0:T(8,128)}), f32[16,27,256]{2,1,0:T(8,128)S(1)}, u32[]{:S(2)}, u32[]{:S(2)}) async-start(f32[16,27,256]{2,1,0:T(8,128)} %broadcast_in_dim.16), calls=%async_computation.2 | async-start | bytes 1048576 | tf_op jit(solution)/shard_map/all_to_all | solution.py:184
  112.8 1.6 %dynamic-slice_add_fusion = f32[1,64,2048]{1,2,0:T(8,128)S(1)} fusion(f32[1,64,2048]{1,2,0:T(8,128)} %copy.42, f32[1,128,2048]{1,2,0:T(8,128)S(1)} %dynamic-slice_add_fusion.1, s32[]{:T(128)S(6)} %select_n.73), kind=kLoop, calls=%fused_computation.23 | loop fusion | flops 131072 | bytes 1572868 | tf_op jit(solution)/shard_map/add | solution.py:38
  114.7 1.0 copy.43
  115.7 3.3 %collective-permute-start.4 = (f32[1,32,2048]{2,1,0:T(8,128)}, f32[1,32,2048]{2,1,0:T(8,128)}, u32[]{:S(2)}, u32[]{:S(2)}) collective-permute-start(f32[1,32,2048]{2,1,0:T(8,128)} %copy.43), channel_id=1, source_target_pairs={{0,1},{1,0},{2,3},{3,2},{4,5},{5,4},{6,7},{7,6},{8,9},{9,8},{10,11... | collective-permute-start | bytes 786440 | tf_op jit(solution)/shard_map/ppermute | solution.py:38
  119.0 1.7 %add_convert_fusion.1 = bf16[1,32,2048]{2,1,0:T(8,128)(2,1)} fusion(f32[1,32,2048]{2,1,0:T(8,128)} %collective-permute-done.6, f32[1,32,2048]{2,1,0:T(8,128)S(1)} %slice.19, f32[1,32,2048]{2,1,0:T(8,128)} %collective-permute-done.5), kind=kLoop, calls=%fused_computation.28 | loop fusion | flops 196608 | bytes 917504 | tf_op jit(solution)/shard_map/convert_element_type | solution.py:199
  120.7 7.4 %collective-permute-done.4 = f32[1,32,2048]{2,1,0:T(8,128)} collective-permute-done((f32[1,32,2048]{2,1,0:T(8,128)}, f32[1,32,2048]{2,1,0:T(8,128)}, u32[]{:S(2)}, u32[]{:S(2)}) %collective-permute-start.4) | collective-permute-done | bytes 262176 | tf_op jit(solution)/shard_map/ppermute | solution.py:38
  128.1 1.3 copy.44
  129.5 2.6 %collective-permute-start.8 = (f32[432,256]{1,0:T(8,128)S(1)}, f32[432,256]{1,0:T(8,128)}, u32[]{:S(2)}, u32[]{:S(2)}) collective-permute-start(f32[432,256]{1,0:T(8,128)S(1)} %reshape.41), channel_id=1, source_target_pairs={{0,8},{8,0},{1,9},{9,1},{2,10},{10,2},{3,11},{11,3},{4,12},{12,4},... | collective-permute-start | bytes 1327112 | tf_op jit(solution)/shard_map/ppermute | solution.py:47
  132.4 0.8 copy.55
  133.6 1.1 broadcast_select_fusion.1
  134.7 1.0 pad_maximum_fusion
  (45 shorter events, 6.9 us)
Async XLA Ops:
  0.6 23.9 %copy-start = (bf16[27,32,256]{2,1,0:T(8,128)(2,1)S(1)}, bf16[27,32,256]{2,1,0:T(8,128)(2,1)}, u32[]{:S(2)}) copy-start(bf16[27,32,256]{2,1,0:T(8,128)(2,1)} %param.4) | copy-start | bytes 1327108
  0.6 15.7 %copy-start.5 = (bf16[1,32,2048]{2,1,0:T(8,128)(2,1)S(1)}, bf16[1,32,2048]{2,1,0:T(8,128)(2,1)}, u32[]{:S(2)}) copy-start(bf16[1,32,2048]{2,1,0:T(8,128)(2,1)} %param.3) | copy-start | bytes 393220
  0.7 15.6 %collective-permute-start = (bf16[1,32,2048]{2,1,0:T(8,128)(2,1)}, bf16[1,32,2048]{2,1,0:T(8,128)(2,1)S(1)}, u32[]{:S(2)}, u32[]{:S(2)}) collective-permute-start(bf16[1,32,2048]{2,1,0:T(8,128)(2,1)} %param.3), channel_id=1, source_target_pairs={{0,8},{8,16},{16,24},{24,32},{32,40},{40,48},{48,56},{56,64},{64,7... | collective-permute-start | bytes 393224 | tf_op jit(solution)/shard_map/ppermute | solution.py:17
  5.7 10.6 %collective-permute-start.1 = (bf16[1,32,2048]{2,1,0:T(8,128)(2,1)}, bf16[1,32,2048]{2,1,0:T(8,128)(2,1)S(1)}, u32[]{:S(2)}, u32[]{:S(2)}) collective-permute-start(bf16[1,32,2048]{2,1,0:T(8,128)(2,1)} %param.3), channel_id=1, source_target_pairs={{8,0},{16,8},{24,16},{32,24},{40,32},{48,40},{56,48},{64,56},{72,6... | collective-permute-start | bytes 393224 | tf_op jit(solution)/shard_map/ppermute | solution.py:20
  9.6 26.5 %all-to-all-start = ((bf16[8,1,32,2048]{3,2,1,0:T(8,128)(2,1)}), bf16[8,1,32,2048]{3,2,1,0:T(8,128)(2,1)S(1)}, u32[]{:S(2)}, u32[]{:S(2)}) async-start(bf16[8,1,32,2048]{3,2,1,0:T(8,128)(2,1)} %broadcast_in_dim.7), calls=%async_computation | async-start | bytes 2097152 | tf_op jit(solution)/shard_map/all_to_all | solution.py:184
  16.4 0.8 copy-start.3
  21.1 3.5 %copy-start.6 = (pred[8,9]{0,1:T(8,128)(4,1)S(1)}, pred[8,9]{0,1:T(8,128)(4,1)}, u32[]{:S(2)}) copy-start(pred[8,9]{0,1:T(8,128)(4,1)} %constant.104) | copy-start | bytes 220
  24.6 4.0 %copy-start.4 = (bf16[3,32,2048]{2,1,0:T(8,128)(2,1)S(1)}, bf16[3,32,2048]{2,1,0:T(8,128)(2,1)}, u32[]{:S(2)}) copy-start(bf16[3,32,2048]{2,1,0:T(8,128)(2,1)} %copy-done.3) | copy-start | bytes 1179652
  31.6 1.6 %copy-start.1 = (f32[1,1,256,32,64]{2,4,3,1,0:T(8,128)}, f32[1,1,256,32,64]{2,4,3,1,0:T(8,128)S(1)}, u32[]{:S(2)}) copy-start(f32[1,1,256,32,64]{2,4,3,1,0:T(8,128)S(1)} %copy.40) | copy-start | bytes 6291460
  33.2 49.5 %collective-permute-start.2 = (f32[1,128,2048]{1,2,0:T(8,128)}, f32[1,128,2048]{1,2,0:T(8,128)}, u32[]{:S(2)}, u32[]{:S(2)}) collective-permute-start(f32[1,128,2048]{1,2,0:T(8,128)} %constant_dynamic-slice_fusion.3), channel_id=1, source_target_pairs={{0,4},{1,5},{2,6},{3,7},{4,0},{5,1},{6,2},{7,3},{8,12},{9,13},{10,... | collective-permute-start | bytes 3145736 | tf_op jit(solution)/shard_map/ppermute | solution.py:38
  46.6 25.9 %collective-permute-start.7 = (f32[432,256]{1,0:T(8,128)}, f32[432,256]{1,0:T(8,128)}, u32[]{:S(2)}, u32[]{:S(2)}) collective-permute-start(f32[432,256]{1,0:T(8,128)} %constant_dynamic-slice_fusion), channel_id=1, source_target_pairs={{0,8},{8,0},{1,9},{9,1},{2,10},{10,2},{3,11},{11,3},{4,12},{12,4},... | collective-permute-start | bytes 1327112 | tf_op jit(solution)/shard_map/ppermute | solution.py:38
  62.0 10.5 %copy-start.2 = (f32[27,32,256]{2,1,0:T(8,128)S(1)}, f32[27,32,256]{2,1,0:T(8,128)}, u32[]{:S(2)}) copy-start(f32[27,32,256]{2,1,0:T(8,128)} %shard_map.58) | copy-start | bytes 2654212
  65.5 53.5 %collective-permute-start.5 = (f32[1,32,2048]{2,1,0:T(8,128)}, f32[1,32,2048]{2,1,0:T(8,128)}, u32[]{:S(2)}, u32[]{:S(2)}) collective-permute-start(f32[1,32,2048]{2,1,0:T(8,128)} %slice.21), channel_id=1, source_target_pairs={{0,8},{8,16},{16,24},{24,32},{32,40},{40,48},{48,56},{56,64},{64,7... | collective-permute-start | bytes 786440 | tf_op jit(solution)/shard_map/ppermute | solution.py:134
  74.4 29.2 %all-to-all-start.1 = ((f32[16,27,256]{2,1,0:T(8,128)}), f32[16,27,256]{2,1,0:T(8,128)}, u32[]{:S(2)}, u32[]{:S(2)}) async-start(f32[16,27,256]{2,1,0:T(8,128)} %reshape.40), calls=%async_computation.1 | async-start | bytes 1048576 | tf_op jit(solution)/shard_map/all_to_all | solution.py:177
  88.1 13.2 %collective-permute-start.3 = (f32[1,64,2048]{2,1,0:T(8,128)}, f32[1,64,2048]{2,1,0:T(8,128)}, u32[]{:S(2)}, u32[]{:S(2)}) collective-permute-start(f32[1,64,2048]{2,1,0:T(8,128)} %copy.41), channel_id=1, source_target_pairs={{0,2},{1,3},{2,0},{3,1},{4,6},{5,7},{6,4},{7,5},{8,10},{9,11},{10,... | collective-permute-start | bytes 1572872 | tf_op jit(solution)/shard_map/ppermute | solution.py:38
  93.5 25.5 %collective-permute-start.6 = (f32[1,32,2048]{2,1,0:T(8,128)}, f32[1,32,2048]{2,1,0:T(8,128)}, u32[]{:S(2)}, u32[]{:S(2)}) collective-permute-start(f32[1,32,2048]{2,1,0:T(8,128)} %slice.23), channel_id=1, source_target_pairs={{8,0},{16,8},{24,16},{32,24},{40,32},{48,40},{56,48},{64,56},{72,6... | collective-permute-start | bytes 786440 | tf_op jit(solution)/shard_map/ppermute | solution.py:135
  105.6 23.9 %all-to-all-start.2 = ((f32[16,27,256]{2,1,0:T(8,128)}), f32[16,27,256]{2,1,0:T(8,128)S(1)}, u32[]{:S(2)}, u32[]{:S(2)}) async-start(f32[16,27,256]{2,1,0:T(8,128)} %broadcast_in_dim.16), calls=%async_computation.2 | async-start | bytes 1048576 | tf_op jit(solution)/shard_map/all_to_all | solution.py:184
  115.7 12.4 %collective-permute-start.4 = (f32[1,32,2048]{2,1,0:T(8,128)}, f32[1,32,2048]{2,1,0:T(8,128)}, u32[]{:S(2)}, u32[]{:S(2)}) collective-permute-start(f32[1,32,2048]{2,1,0:T(8,128)} %copy.43), channel_id=1, source_target_pairs={{0,1},{1,0},{2,3},{3,2},{4,5},{5,4},{6,7},{7,6},{8,9},{9,8},{10,11... | collective-permute-start | bytes 786440 | tf_op jit(solution)/shard_map/ppermute | solution.py:38
  129.5 4.1 %collective-permute-start.8 = (f32[432,256]{1,0:T(8,128)S(1)}, f32[432,256]{1,0:T(8,128)}, u32[]{:S(2)}, u32[]{:S(2)}) collective-permute-start(f32[432,256]{1,0:T(8,128)S(1)} %reshape.41), channel_id=1, source_target_pairs={{0,8},{8,0},{1,9},{9,1},{2,10},{10,2},{3,11},{11,3},{4,12},{12,4},... | collective-permute-start | bytes 1327112 | tf_op jit(solution)/shard_map/ppermute | solution.py:47

commit v8 on v3

--- a/solution.py
+++ b/solution.py
@@ -194,8 +194,18 @@
 
 def local(inputs, weights, cotangent):
     padded = extended(inputs, ((SPACE, 0),), 1)
-    partial_out = conv_forward(padded, weights)
-    chan_masks = partner_masks(lax.axis_size("chan"), 1)[::-1]
+    chan_count = lax.axis_size("chan")
+    chan_masks = partner_masks(chan_count, min(2, chan_count // 2))
+    chan_masks = [chan_masks[0]] + sorted(chan_masks[1:], reverse=True)
+    order = [0] * chan_count
+    for index in range(chan_count):
+        place = 0
+        for mask in chan_masks:
+            place = place * 2 + (index // mask) % 2
+        order[place] = index
+    kinds, rows, cols = weights.shape
+    ordered = weights.reshape(kinds, rows, chan_count, cols // chan_count)[:, :, jnp.array(order), :]
+    partial_out = conv_forward(padded, ordered.reshape(kinds, rows, cols))
     output = halving_sum(partial_out, "chan", chan_masks, 1).astype(jnp.bfloat16)
     gathered = spread_gather(cotangent, "chan", 1)
     input_grad = spill_sum(conv_backward(gathered, weights), SPACE).astype(jnp.bfloat16)

time: 135 us -> 140 us (1.037)
  local copies, waits for them, and re-layouts: 46.6 us -> 50.9 us
  other arithmetic: 15.3 us -> 12.6 us
  waiting for transfers between devices: 9.81 us -> 11.9 us
    gather x0 -> x2, local copies, waits for them, and re-layouts: none -> 4.32 us  [local(): weights.reshape(kinds, rows, chan_count, cols // chan_count)]
    reshape x0 -> x2, local copies, waits for them, and re-layouts: none -> 3.57 us  [local(): weights.reshape(kinds, rows, chan_count, cols // chan_count)]
    all_to_all x1, waiting for transfers between devices: 0.93 us -> 4.35 us  [scatter_sum(): parts = lax.all_to_all(parts, axis, 0, 0, tiled=True)]
    conv_general_dilated x6, local copies, waits for them, and re-layouts: 4.96 us -> 2.66 us  [conv_backward(): lax.conv_general_dilated(lhs, rhs, (1, 1, 1), [(2, 2), (1, 1), (1, 1)], d...]
    ppermute x2, local copies, waits for them, and re-layouts: 3.65 us -> 1.7 us  [halving_sum(): lax.ppermute(send, axis, [(i, i ^ mask) for i in range(count)])]
    another operation x0 -> x1, local copies, waits for them, and re-layouts: none -> 1.93 us  [conv_forward(): rhs = taps.reshape(3, 3, 3, channels, taps.shape[-1])]
    add x3, other arithmetic: 5.43 us -> 3.61 us  [halving_sum(): keep + lax.ppermute(send, axis, [(i, i ^ mask) for i in range(count)])]
    slice x3, local copies, waits for them, and re-layouts: 1.73 us -> 3.55 us  [spill_sum(): from_low = lax.ppermute(parts[-1:], axis, forward)]
where the time goes in v8:
time: 140 us; the launch traced here: 139 us
  local copies, waits for them, and re-layouts  50.9 us (36%)
  starting transfers between devices  45.4 us (32%)
  other arithmetic  12.6 us (9%)
  waiting for transfers between devices  11.9 us (8%)
  matrix products  9.72 us (7%)
  Pallas kernels  7.28 us (5%)
    all_to_all x2, starting transfers between devices, spread_gather(): copies = lax.all_to_all(copies, axis, 0, 0, tiled=True)  12.3 us
    all_to_all x1, starting transfers between devices, scatter_sum(): parts = lax.all_to_all(parts, axis, 0, 0, tiled=True)  8.31 us
    ppermute x4, waiting for transfers between devices, halving_sum(): lax.ppermute(send, axis, [(i, i ^ mask) for i in range(count)])  7.35 us
    pallas_call x1, Pallas kernels, conv_filter(): pl.pallas_call(filter_kernel, out_shape=jax.ShapeDtypeStruct((27, channel...  7.28 us
    ppermute x4, starting transfers between devices, halving_sum(): lax.ppermute(send, axis, [(i, i ^ mask) for i in range(count)])  7.2 us
    unnamed x22, local copies, waits for them, and re-layouts  6.06 us
    conv_general_dilated x1, matrix products, conv_backward(): lax.conv_general_dilated(lhs, rhs, (1, 1, 1), [(2, 2), (1, 1), (1, 1)], d...  5.76 us
    conv_general_dilated x5, local copies, waits for them, and re-layouts, conv_forward(): lax.conv_general_dilated(lhs, rhs, (1, 1, 1), [(0, 0), (1, 1), (1, 1)], d...  5.68 us
  transfers between devices with their start and end apart: 12, of which 3 were waited for; matrix products, arithmetic and copies ran while one was open for 51% of the time, Pallas kernels for 5%

profile of v8, /device:TPU:1, one launch (start us, length us, event | category | flops | bytes accessed | tf_op | source)
XLA Modules:
  0.0 138.9 jit_solution(3512838522281413950)
XLA Ops:
  0.6 5.1 %collective-permute-start = (bf16[1,32,2048]{2,1,0:T(8,128)(2,1)}, bf16[1,32,2048]{2,1,0:T(8,128)(2,1)}, u32[]{:S(2)}, u32[]{:S(2)}) collective-permute-start(bf16[1,32,2048]{2,1,0:T(8,128)(2,1)} %param.4), channel_id=1, source_target_pairs={{0,8},{8,16},{16,24},{24,32},{32,40},{40,48},{48,56},{56,64},{64,7... | collective-permute-start | bytes 393224 | tf_op jit(solution)/shard_map/ppermute | solution.py:17
  5.7 2.1 %collective-permute-start.1 = (bf16[1,32,2048]{2,1,0:T(8,128)(2,1)}, bf16[1,32,2048]{2,1,0:T(8,128)(2,1)S(1)}, u32[]{:S(2)}, u32[]{:S(2)}) collective-permute-start(bf16[1,32,2048]{2,1,0:T(8,128)(2,1)} %param.4), channel_id=1, source_target_pairs={{8,0},{16,8},{24,16},{32,24},{40,32},{48,40},{56,48},{64,56},{72,6... | collective-permute-start | bytes 393224 | tf_op jit(solution)/shard_map/ppermute | solution.py:20
  7.8 2.0 %broadcast_in_dim.19 = bf16[8,1,32,2048]{3,2,1,0:T(8,128)(2,1)} broadcast(bf16[32,2048]{1,0:T(8,128)(2,1)} %bitcast.57), dimensions={2,3} | broadcast | bytes 1179648 | tf_op jit(solution)/shard_map/broadcast_in_dim | solution.py:185
  9.8 6.5 %all-to-all-start = ((bf16[8,1,32,2048]{3,2,1,0:T(8,128)(2,1)}), bf16[8,1,32,2048]{3,2,1,0:T(8,128)(2,1)S(1)}, u32[]{:S(2)}, u32[]{:S(2)}) async-start(bf16[8,1,32,2048]{3,2,1,0:T(8,128)(2,1)} %broadcast_in_dim.19), calls=%async_computation | async-start | bytes 2097152 | tf_op jit(solution)/shard_map/all_to_all | solution.py:186
  16.3 1.7 %reshape.39 = bf16[27,32,8,32]{3,2,1,0:T(8,128)(2,1)} reshape(bf16[27,32,256]{2,1,0:T(8,128)(2,1)S(1)} %copy-done.4) | data formatting | bytes 884736 | tf_op jit(solution)/shard_map/reshape | solution.py:207
  18.0 1.9 %copy.42 = bf16[27,32,8,32]{3,1,2,0:T(8,128)(2,1)S(1)} copy(bf16[27,32,8,32]{3,2,1,0:T(8,128)(2,1)} %reshape.39) | data formatting | bytes 884736 | tf_op jit(solution)/shard_map/reshape | solution.py:207
  19.9 2.0 %gather_fusion = bf16[8,27,32,32]{3,2,1,0:T(8,128)(2,1)} fusion(bf16[27,32,8,32]{3,1,2,0:T(8,128)(2,1)S(1)} %copy.42, s32[1024]{0:T(1024)S(1)} %pad_clamp_fusion), kind=kCustom, calls=%fused_computation | custom fusion | bytes 884768 | tf_op jit(solution)/shard_map/gather | solution.py:207
  21.9 2.3 %copy.43 = bf16[27,32,8,32]{3,2,1,0:T(8,128)(2,1)S(1)} copy(bf16[27,32,8,32]{3,1,0,2:T(8,128)(2,1)} %bitcast.48) | data formatting | bytes 884736 | tf_op jit(solution)/shard_map/gather | solution.py:207
  24.2 1.9 %reshape_reshape.3 = bf16[3,3,3,32,256]{4,3,2,1,0:T(8,128)(2,1)} reshape(bf16[27,32,8,32]{3,2,1,0:T(8,128)(2,1)S(1)} %copy.43) | data formatting | bytes 884736 | tf_op jit(solution)/shard_map/reshape;reshape | solution.py:111
  26.2 0.9 constant_dynamic-update-slice_fusion.2
  28.0 2.1 %copy.39 = bf16[3,32,32,1,64]{2,1,4,0,3:T(8,128)(2,1)} copy(bf16[3,32,32,1,64]{4,2,1,0,3:T(8,128)(2,1)S(1)} %reshape.64) | data formatting | bytes 786432 | tf_op jit(solution)/shard_map/reshape | solution.py:110
  30.1 1.8 %pad.5 = bf16[3,32,32,1,72]{2,1,4,0,3:T(8,128)(2,1)S(1)} pad(bf16[3,32,32,1,64]{2,1,4,0,3:T(8,128)(2,1)} %copy.39, bf16[]{:T(256)} %constant.83.clone.1), padding=0_0x0_0x0_0x0_0x1_7 | pad | bytes 835586 | tf_op jit(solution)/shard_map/reshape | solution.py:110
  31.8 2.4 %copy.41 = bf16[3,32,32,1,8,9]{1,4,5,2,0,3:T(8,128)(2,1)} copy(bf16[3,32,32,1,8,9]{2,1,5,4,0,3:T(8,128)(2,1)S(1)} %bitcast.49) | data formatting | bytes 884736 | tf_op jit(solution)/shard_map/conv_general_dilated | solution.py:112
  34.2 1.1 slice.67
  35.3 4.0 %fusion.9 = f32[1,32,8,9,256]{4,2,3,1,0:T(8,128)S(1)} fusion(bf16[3,3,3,32,256]{4,3,2,1,0:T(8,128)(2,1)} %reshape_reshape.3, bf16[3,32,32,1,7,2]{1,4,5,2,0,3:T(8,128)(2,1)S(1)} %slice.67, bf16[3,32,32,1,8,9]{1,4,5,2,0,3:T(8,128)(2,1)} %copy.41, pred[8,9]{0,1:T(8,128)(4,1)S(1)} %copy-done.8), kind=kOutput, calls=%fused_computation.13 | convolution fusion | flops 1000194048 | bytes 3330120 | tf_op jit(solution)/shard_map/conv_general_dilated | solution.py:112
  41.1 1.2 copy.45
  42.3 1.3 copy-done
  43.7 1.1 slice_select_fusion.2
  44.8 1.4 %collective-permute-start.2 = (f32[1,128,2048]{1,2,0:T(8,128)}, f32[1,128,2048]{1,2,0:T(8,128)}, u32[]{:S(2)}, u32[]{:S(2)}) collective-permute-start(f32[1,128,2048]{1,2,0:T(8,128)} %slice_select_fusion.2), channel_id=1, source_target_pairs={{0,2},{1,3},{2,0},{3,1},{4,6},{5,7},{6,4},{7,5},{8,10},{9,11},{10,... | collective-permute-start | bytes 3145736 | tf_op jit(solution)/shard_map/ppermute | solution.py:40
  46.2 1.3 copy.59
  47.5 7.3 %shard_map.67 = f32[27,32,256]{2,1,0:T(8,128)} custom-call(bf16[3,32,2304]{2,1,0:T(8,128)(2,1)} %pad.4.x_ref, bf16[2048,256]{1,0:T(8,128)(2,1)} %bitcast.54), custom_call_target="tpu_custom_call" | custom-call | tf_op jit(solution)/shard_map/pallas_call | solution.py:168
  54.8 2.0 %slice_select_fusion.3 = f32[432,256]{1,0:T(8,128)} fusion(f32[864,256]{1,0:T(8,128)} %bitcast.46, pred[]{:T(512)S(6)} %eq.22), kind=kLoop, calls=%fused_computation.32 | loop fusion | flops 110592 | bytes 1327105 | tf_op jit(solution)/shard_map/jit(_where)/select_n | solution.py:39
  56.8 2.2 %reshape.68 = bf16[1,256,32,1,64]{4,2,1,3,0:T(8,128)(2,1)S(1)} reshape(bf16[8,1,32,2048]{3,2,1,0:T(8,128)(2,1)S(1)} %all-to-all-done) | data formatting | bytes 2097152 | tf_op jit(solution)/shard_map/reshape;reshape;transpose | solution.py:122
  59.0 2.7 %copy.61 = bf16[1,256,32,1,64]{1,2,4,3,0:T(8,128)(2,1)S(1)} copy(bf16[1,256,32,1,64]{4,2,1,3,0:T(8,128)(2,1)S(1)} %reshape.68) | data formatting | bytes 2097152
  62.8 5.8 %convolution_select_fusion = f32[3,32,8,9,32]{4,2,3,1,0:T(8,128)S(1)} fusion(bf16[3,3,3,32,256]{4,3,2,1,0:T(8,128)(2,1)S(1)} %bitcast.56, pred[8,9]{0,1:T(8,128)(4,1)S(1)} %copy-done.8, bf16[1,256,32,1,7,2]{1,4,5,2,3,0:T(8,128)(2,1)S(1)} %slice.75, bf16[1,256,32,1,8,9]{1,4,5,2,3,0:T(8,128)(2,1)S(1)} %copy.52), kind=kOutput, calls=%fused_computation.12 | convolution fusion | flops 1002528768 | bytes 2736200 | tf_op jit(solution)/shard_map/conv_general_dilated | solution.py:124
  69.1 1.5 %copy.56 = f32[1,1,32,32,64]{4,3,2,1,0:T(8,128)} copy(f32[1,1,32,32,64]{2,3,4,0,1:T(8,128)S(1)} %slice_bitcast_fusion.2) | data formatting | bytes 524288 | tf_op jit(solution)/shard_map/slice | solution.py:136
  70.6 1.9 %slice.51 = f32[1,32,2048]{2,1,0:T(8,128)} reshape(f32[1,1,32,32,64]{4,3,2,1,0:T(8,128)} %copy.56) | data formatting | bytes 524288 | tf_op jit(solution)/shard_map/slice | solution.py:136
  72.6 4.6 %collective-permute-start.5 = (f32[1,32,2048]{2,1,0:T(8,128)}, f32[1,32,2048]{2,1,0:T(8,128)}, u32[]{:S(2)}, u32[]{:S(2)}) collective-permute-start(f32[1,32,2048]{2,1,0:T(8,128)} %slice.51), channel_id=1, source_target_pairs={{0,8},{8,16},{16,24},{24,32},{32,40},{40,48},{48,56},{56,64},{64,7... | collective-permute-start | bytes 786440 | tf_op jit(solution)/shard_map/ppermute | solution.py:136
  77.2 1.2 copy.57
  78.4 1.4 %select_add_fusion.1 = f32[1,128,2048]{1,2,0:T(8,128)S(1)} fusion(f32[1,128,2048]{1,2,0:T(8,128)} %collective-permute-done.2, f32[1,256,2048]{1,2,0:T(8,128)S(1)} %bitcast.43, pred[]{:T(512)S(6)} %eq.21), kind=kLoop, calls=%fused_computation.25 | loop fusion | flops 524288 | bytes 4194305 | tf_op jit(solution)/shard_map/add | solution.py:40
  79.8 1.3 slice_select_fusion.1
  81.2 2.3 %copy.46 = f32[1,64,2048]{2,1,0:T(8,128)} copy(f32[1,64,2048]{1,2,0:T(8,128)} %slice_select_fusion.1) | data formatting | bytes 1048576 | tf_op jit(solution)/shard_map/jit(_where)/select_n | solution.py:39
  83.5 2.4 %collective-permute-start.3 = (f32[1,64,2048]{2,1,0:T(8,128)}, f32[1,64,2048]{2,1,0:T(8,128)}, u32[]{:S(2)}, u32[]{:S(2)}) collective-permute-start(f32[1,64,2048]{2,1,0:T(8,128)} %copy.46), channel_id=1, source_target_pairs={{0,4},{1,5},{2,6},{3,7},{4,0},{5,1},{6,2},{7,3},{8,12},{9,13},{10,... | collective-permute-start | bytes 1572872 | tf_op jit(solution)/shard_map/ppermute | solution.py:40
  85.9 1.9 %select_add_fusion.2 = f32[432,256]{1,0:T(8,128)} fusion(f32[432,256]{1,0:T(8,128)} %collective-permute-done.7, f32[864,256]{1,0:T(8,128)S(1)} %bitcast.47, pred[]{:T(512)S(6)} %eq.22), kind=kLoop, calls=%fused_computation.31 | loop fusion | flops 221184 | bytes 1769473 | tf_op jit(solution)/shard_map/add | solution.py:40
  87.8 2.0 %reshape.43 = f32[16,27,256]{2,1,0:T(8,128)} reshape(f32[432,256]{1,0:T(8,128)} %select_add_fusion.2) | data formatting | bytes 884736 | tf_op jit(solution)/shard_map/reshape | solution.py:177
  89.7 8.3 %all-to-all-start.1 = ((f32[16,27,256]{2,1,0:T(8,128)}), f32[16,27,256]{2,1,0:T(8,128)}, u32[]{:S(2)}, u32[]{:S(2)}) async-start(f32[16,27,256]{2,1,0:T(8,128)} %reshape.43), calls=%async_computation.1 | async-start | bytes 1048576 | tf_op jit(solution)/shard_map/all_to_all | solution.py:179
  98.1 1.1 slice_bitcast_fusion.1
  99.1 1.9 %copy.58 = f32[1,1,32,32,64]{4,3,2,1,0:T(8,128)S(1)} copy(f32[1,1,32,32,64]{2,3,4,0,1:T(8,128)} %slice_bitcast_fusion.1) | data formatting | bytes 524288 | tf_op jit(solution)/shard_map/slice | solution.py:137
  102.0 2.8 %collective-permute-start.6 = (f32[1,32,2048]{2,1,0:T(8,128)}, f32[1,32,2048]{2,1,0:T(8,128)}, u32[]{:S(2)}, u32[]{:S(2)}) collective-permute-start(f32[1,32,2048]{2,1,0:T(8,128)} %slice.53), channel_id=1, source_target_pairs={{8,0},{16,8},{24,16},{32,24},{40,32},{48,40},{56,48},{64,56},{72,6... | collective-permute-start | bytes 786440 | tf_op jit(solution)/shard_map/ppermute | solution.py:137
  106.0 1.4 copy.47
  107.8 4.4 %all-to-all-done.1 = f32[16,27,256]{2,1,0:T(8,128)} async-done(((f32[16,27,256]{2,1,0:T(8,128)}), f32[16,27,256]{2,1,0:T(8,128)}, u32[]{:S(2)}, u32[]{:S(2)}) %all-to-all-start.1) | async-done | bytes 442400 | tf_op jit(solution)/shard_map/all_to_all | solution.py:179
  112.1 1.1 reduce_sum.9
  114.0 5.9 %all-to-all-start.2 = ((f32[16,27,256]{2,1,0:T(8,128)}), f32[16,27,256]{2,1,0:T(8,128)S(1)}, u32[]{:S(2)}, u32[]{:S(2)}) async-start(f32[16,27,256]{2,1,0:T(8,128)} %broadcast_in_dim.20), calls=%async_computation.2 | async-start | bytes 1048576 | tf_op jit(solution)/shard_map/all_to_all | solution.py:186
  120.6 3.4 %collective-permute-start.4 = (f32[1,32,2048]{2,1,0:T(8,128)S(1)}, f32[1,32,2048]{2,1,0:T(8,128)S(1)}, u32[]{:S(2)}, u32[]{:S(2)}) collective-permute-start(f32[1,32,2048]{2,1,0:T(8,128)S(1)} %copy.48), channel_id=1, source_target_pairs={{0,1},{1,0},{2,3},{3,2},{4,5},{5,4},{6,7},{7,6},{8,9},{9,8},{10,11... | collective-permute-start | bytes 786440 | tf_op jit(solution)/shard_map/ppermute | solution.py:40
  123.9 1.7 %add_convert_fusion.1 = bf16[1,32,2048]{2,1,0:T(8,128)(2,1)} fusion(f32[1,32,2048]{2,1,0:T(8,128)} %collective-permute-done.6, f32[1,32,2048]{2,1,0:T(8,128)S(1)} %slice.49, f32[1,32,2048]{2,1,0:T(8,128)} %collective-permute-done.5), kind=kLoop, calls=%fused_computation.33 | loop fusion | flops 196608 | bytes 917504 | tf_op jit(solution)/shard_map/convert_element_type | solution.py:211
  125.7 7.3 %collective-permute-done.4 = f32[1,32,2048]{2,1,0:T(8,128)S(1)} collective-permute-done((f32[1,32,2048]{2,1,0:T(8,128)S(1)}, f32[1,32,2048]{2,1,0:T(8,128)S(1)}, u32[]{:S(2)}, u32[]{:S(2)}) %collective-permute-start.4) | collective-permute-done | bytes 262176 | tf_op jit(solution)/shard_map/ppermute | solution.py:40
  133.4 3.0 %collective-permute-start.8 = (f32[432,256]{1,0:T(8,128)S(1)}, f32[432,256]{1,0:T(8,128)S(1)}, u32[]{:S(2)}, u32[]{:S(2)}) collective-permute-start(f32[432,256]{1,0:T(8,128)S(1)} %reshape.44), channel_id=1, source_target_pairs={{0,8},{8,0},{1,9},{9,1},{2,10},{10,2},{3,11},{11,3},{4,12},{12,4},... | collective-permute-start | bytes 1327112 | tf_op jit(solution)/shard_map/ppermute | solution.py:49
  137.9 1.0 pad_maximum_fusion
  (55 shorter events, 10.2 us)
Async XLA Ops:
  0.6 15.7 %copy-start.4 = (bf16[27,32,256]{2,1,0:T(8,128)(2,1)S(1)}, bf16[27,32,256]{2,1,0:T(8,128)(2,1)}, u32[]{:S(2)}) copy-start(bf16[27,32,256]{2,1,0:T(8,128)(2,1)} %param.5) | copy-start | bytes 1327108
  0.6 25.5 %collective-permute-start = (bf16[1,32,2048]{2,1,0:T(8,128)(2,1)}, bf16[1,32,2048]{2,1,0:T(8,128)(2,1)}, u32[]{:S(2)}, u32[]{:S(2)}) collective-permute-start(bf16[1,32,2048]{2,1,0:T(8,128)(2,1)} %param.4), channel_id=1, source_target_pairs={{0,8},{8,16},{16,24},{24,32},{32,40},{40,48},{48,56},{56,64},{64,7... | collective-permute-start | bytes 393224 | tf_op jit(solution)/shard_map/ppermute | solution.py:17
  5.7 21.4 %collective-permute-start.1 = (bf16[1,32,2048]{2,1,0:T(8,128)(2,1)}, bf16[1,32,2048]{2,1,0:T(8,128)(2,1)S(1)}, u32[]{:S(2)}, u32[]{:S(2)}) collective-permute-start(bf16[1,32,2048]{2,1,0:T(8,128)(2,1)} %param.4), channel_id=1, source_target_pairs={{8,0},{16,8},{24,16},{32,24},{40,32},{48,40},{56,48},{64,56},{72,6... | collective-permute-start | bytes 393224 | tf_op jit(solution)/shard_map/ppermute | solution.py:20
  9.8 36.4 %all-to-all-start = ((bf16[8,1,32,2048]{3,2,1,0:T(8,128)(2,1)}), bf16[8,1,32,2048]{3,2,1,0:T(8,128)(2,1)S(1)}, u32[]{:S(2)}, u32[]{:S(2)}) async-start(bf16[8,1,32,2048]{3,2,1,0:T(8,128)(2,1)} %broadcast_in_dim.19), calls=%async_computation | async-start | bytes 2097152 | tf_op jit(solution)/shard_map/all_to_all | solution.py:186
  18.0 1.9 %copy-start.7 = (s32[8]{0:T(128)S(1)}, s32[8]{0:T(128)}, u32[]{:S(2)}) copy-start(s32[8]{0:T(128)} %constant.104) | copy-start | bytes 100
  24.2 2.9 %copy-start.6 = (bf16[1,32,2048]{2,1,0:T(8,128)(2,1)S(1)}, bf16[1,32,2048]{2,1,0:T(8,128)(2,1)}, u32[]{:S(2)}) copy-start(bf16[1,32,2048]{2,1,0:T(8,128)(2,1)} %param.4) | copy-start | bytes 393220
  31.8 3.5 %copy-start.8 = (pred[8,9]{0,1:T(8,128)(4,1)S(1)}, pred[8,9]{0,1:T(8,128)(4,1)}, u32[]{:S(2)}) copy-start(pred[8,9]{0,1:T(8,128)(4,1)} %constant.98) | copy-start | bytes 220
  42.3 1.3 copy-start
  44.8 33.6 %collective-permute-start.2 = (f32[1,128,2048]{1,2,0:T(8,128)}, f32[1,128,2048]{1,2,0:T(8,128)}, u32[]{:S(2)}, u32[]{:S(2)}) collective-permute-start(f32[1,128,2048]{1,2,0:T(8,128)} %slice_select_fusion.2), channel_id=1, source_target_pairs={{0,2},{1,3},{2,0},{3,1},{4,6},{5,7},{6,4},{7,5},{8,10},{9,11},{10,... | collective-permute-start | bytes 3145736 | tf_op jit(solution)/shard_map/ppermute | solution.py:40
  56.8 29.1 %collective-permute-start.7 = (f32[432,256]{1,0:T(8,128)}, f32[432,256]{1,0:T(8,128)}, u32[]{:S(2)}, u32[]{:S(2)}) collective-permute-start(f32[432,256]{1,0:T(8,128)} %slice_select_fusion.3), channel_id=1, source_target_pairs={{0,8},{8,0},{1,9},{9,1},{2,10},{10,2},{3,11},{11,3},{4,12},{12,4},... | collective-permute-start | bytes 1327112 | tf_op jit(solution)/shard_map/ppermute | solution.py:40
  61.7 1.0 copy-start.5
  72.6 5.9 %copy-start.1 = (f32[1,1,256,32,64]{2,4,3,1,0:T(8,128)S(1)}, f32[1,1,256,32,64]{2,4,3,1,0:T(8,128)}, u32[]{:S(2)}) copy-start(f32[1,1,256,32,64]{2,4,3,1,0:T(8,128)} %copy-done) | copy-start | bytes 6291460
  72.6 51.4 %collective-permute-start.5 = (f32[1,32,2048]{2,1,0:T(8,128)}, f32[1,32,2048]{2,1,0:T(8,128)}, u32[]{:S(2)}, u32[]{:S(2)}) collective-permute-start(f32[1,32,2048]{2,1,0:T(8,128)} %slice.51), channel_id=1, source_target_pairs={{0,8},{8,16},{16,24},{24,32},{32,40},{40,48},{48,56},{56,64},{64,7... | collective-permute-start | bytes 786440 | tf_op jit(solution)/shard_map/ppermute | solution.py:136
  79.8 6.1 %copy-start.2 = (f32[27,32,256]{2,1,0:T(8,128)S(1)}, f32[27,32,256]{2,1,0:T(8,128)}, u32[]{:S(2)}) copy-start(f32[27,32,256]{2,1,0:T(8,128)} %shard_map.67) | copy-start | bytes 2654212
  83.5 22.5 %collective-permute-start.3 = (f32[1,64,2048]{2,1,0:T(8,128)}, f32[1,64,2048]{2,1,0:T(8,128)}, u32[]{:S(2)}, u32[]{:S(2)}) collective-permute-start(f32[1,64,2048]{2,1,0:T(8,128)} %copy.46), channel_id=1, source_target_pairs={{0,4},{1,5},{2,6},{3,7},{4,0},{5,1},{6,2},{7,3},{8,12},{9,13},{10,... | collective-permute-start | bytes 1572872 | tf_op jit(solution)/shard_map/ppermute | solution.py:40
  87.8 10.3 %copy-start.3 = (f32[1,32,8,9,32]{4,1,3,2,0:T(8,128)S(1)}, f32[1,32,8,9,32]{4,1,3,2,0:T(8,128)}, u32[]{:S(2)}) copy-start(f32[1,32,8,9,32]{4,1,3,2,0:T(8,128)} %copy.57) | copy-start | bytes 884740
  89.7 22.4 %all-to-all-start.1 = ((f32[16,27,256]{2,1,0:T(8,128)}), f32[16,27,256]{2,1,0:T(8,128)}, u32[]{:S(2)}, u32[]{:S(2)}) async-start(f32[16,27,256]{2,1,0:T(8,128)} %reshape.43), calls=%async_computation.1 | async-start | bytes 1048576 | tf_op jit(solution)/shard_map/all_to_all | solution.py:179
  102.0 22.0 %collective-permute-start.6 = (f32[1,32,2048]{2,1,0:T(8,128)}, f32[1,32,2048]{2,1,0:T(8,128)}, u32[]{:S(2)}, u32[]{:S(2)}) collective-permute-start(f32[1,32,2048]{2,1,0:T(8,128)} %slice.53), channel_id=1, source_target_pairs={{8,0},{16,8},{24,16},{32,24},{40,32},{48,40},{56,48},{64,56},{72,6... | collective-permute-start | bytes 786440 | tf_op jit(solution)/shard_map/ppermute | solution.py:137
  114.0 19.3 %all-to-all-start.2 = ((f32[16,27,256]{2,1,0:T(8,128)}), f32[16,27,256]{2,1,0:T(8,128)S(1)}, u32[]{:S(2)}, u32[]{:S(2)}) async-start(f32[16,27,256]{2,1,0:T(8,128)} %broadcast_in_dim.20), calls=%async_computation.2 | async-start | bytes 1048576 | tf_op jit(solution)/shard_map/all_to_all | solution.py:186
  120.6 12.4 %collective-permute-start.4 = (f32[1,32,2048]{2,1,0:T(8,128)S(1)}, f32[1,32,2048]{2,1,0:T(8,128)S(1)}, u32[]{:S(2)}, u32[]{:S(2)}) collective-permute-start(f32[1,32,2048]{2,1,0:T(8,128)S(1)} %copy.48), channel_id=1, source_target_pairs={{0,1},{1,0},{2,3},{3,2},{4,5},{5,4},{6,7},{7,6},{8,9},{9,8},{10,11... | collective-permute-start | bytes 786440 | tf_op jit(solution)/shard_map/ppermute | solution.py:40
  133.4 4.4 %collective-permute-start.8 = (f32[432,256]{1,0:T(8,128)S(1)}, f32[432,256]{1,0:T(8,128)S(1)}, u32[]{:S(2)}, u32[]{:S(2)}) collective-permute-start(f32[432,256]{1,0:T(8,128)S(1)} %reshape.44), channel_id=1, source_target_pairs={{0,8},{8,0},{1,9},{9,1},{2,10},{10,2},{3,11},{11,3},{4,12},{12,4},... | collective-permute-start | bytes 1327112 | tf_op jit(solution)/shard_map/ppermute | solution.py:49

commit v9 on v8

--- a/solution.py
+++ b/solution.py
@@ -195,7 +195,7 @@
 def local(inputs, weights, cotangent):
     padded = extended(inputs, ((SPACE, 0),), 1)
     chan_count = lax.axis_size("chan")
-    chan_masks = partner_masks(chan_count, min(2, chan_count // 2))
+    chan_masks = partner_masks(chan_count, 1)
     chan_masks = [chan_masks[0]] + sorted(chan_masks[1:], reverse=True)
     order = [0] * chan_count
     for index in range(chan_count):

time: 140 us -> 142 us (1.014)
  waiting for transfers between devices: 11.9 us -> 14.3 us
    all_to_all x2, waiting for transfers between devices: 0.01 us -> 5.22 us  [spread_gather(): copies = lax.all_to_all(copies, axis, 0, 0, tiled=True)]
    ppermute x4, waiting for transfers between devices: 7.35 us -> 4.53 us  [halving_sum(): lax.ppermute(send, axis, [(i, i ^ mask) for i in range(count)])]
  transfers between devices with their start and end apart: 12 -> 12, of which waited for: 3 -> 4; matrix products, arithmetic and copies ran while one was open for 51% -> 50% of each run, Pallas kernels for 5% -> 5%
where the time goes in v9:
time: 142 us; the launch traced here: 141 us
  local copies, waits for them, and re-layouts  50.9 us (36%)
  starting transfers between devices  44.9 us (32%)
  waiting for transfers between devices  14.3 us (10%)
  other arithmetic  12.6 us (9%)
  matrix products  9.71 us (7%)
  Pallas kernels  7.28 us (5%)
    all_to_all x2, starting transfers between devices, spread_gather(): copies = lax.all_to_all(copies, axis, 0, 0, tiled=True)  12.4 us
    all_to_all x1, starting transfers between devices, scatter_sum(): parts = lax.all_to_all(parts, axis, 0, 0, tiled=True)  8.31 us
    pallas_call x1, Pallas kernels, conv_filter(): pl.pallas_call(filter_kernel, out_shape=jax.ShapeDtypeStruct((27, channel...  7.28 us
    unnamed x22, local copies, waits for them, and re-layouts  6.06 us
    ppermute x4, starting transfers between devices, halving_sum(): lax.ppermute(send, axis, [(i, i ^ mask) for i in range(count)])  5.99 us
    conv_general_dilated x1, matrix products, conv_backward(): lax.conv_general_dilated(lhs, rhs, (1, 1, 1), [(2, 2), (1, 1), (1, 1)], d...  5.76 us
    conv_general_dilated x5, local copies, waits for them, and re-layouts, conv_forward(): lax.conv_general_dilated(lhs, rhs, (1, 1, 1), [(0, 0), (1, 1), (1, 1)], d...  5.68 us
    all_to_all x2, waiting for transfers between devices, spread_gather(): copies = lax.all_to_all(copies, axis, 0, 0, tiled=True)  5.22 us
  transfers between devices with their start and end apart: 12, of which 4 were waited for; matrix products, arithmetic and copies ran while one was open for 50% of the time, Pallas kernels for 5%

profile of v9, /device:TPU:1, one launch (start us, length us, event | category | flops | bytes accessed | tf_op | source)
XLA Modules:
  0.0 140.7 jit_solution(13458706196297144449)
XLA Ops:
  0.6 5.1 %collective-permute-start = (bf16[1,32,2048]{2,1,0:T(8,128)(2,1)}, bf16[1,32,2048]{2,1,0:T(8,128)(2,1)}, u32[]{:S(2)}, u32[]{:S(2)}) collective-permute-start(bf16[1,32,2048]{2,1,0:T(8,128)(2,1)} %param.4), channel_id=1, source_target_pairs={{0,8},{8,16},{16,24},{24,32},{32,40},{40,48},{48,56},{56,64},{64,7... | collective-permute-start | bytes 393224 | tf_op jit(solution)/shard_map/ppermute | solution.py:17
  5.7 2.1 %collective-permute-start.1 = (bf16[1,32,2048]{2,1,0:T(8,128)(2,1)}, bf16[1,32,2048]{2,1,0:T(8,128)(2,1)S(1)}, u32[]{:S(2)}, u32[]{:S(2)}) collective-permute-start(bf16[1,32,2048]{2,1,0:T(8,128)(2,1)} %param.4), channel_id=1, source_target_pairs={{8,0},{16,8},{24,16},{32,24},{40,32},{48,40},{56,48},{64,56},{72,6... | collective-permute-start | bytes 393224 | tf_op jit(solution)/shard_map/ppermute | solution.py:20
  7.8 2.0 %broadcast_in_dim.19 = bf16[8,1,32,2048]{3,2,1,0:T(8,128)(2,1)} broadcast(bf16[32,2048]{1,0:T(8,128)(2,1)} %bitcast.57), dimensions={2,3} | broadcast | bytes 1179648 | tf_op jit(solution)/shard_map/broadcast_in_dim | solution.py:185
  9.8 6.5 %all-to-all-start = ((bf16[8,1,32,2048]{3,2,1,0:T(8,128)(2,1)}), bf16[8,1,32,2048]{3,2,1,0:T(8,128)(2,1)S(1)}, u32[]{:S(2)}, u32[]{:S(2)}) async-start(bf16[8,1,32,2048]{3,2,1,0:T(8,128)(2,1)} %broadcast_in_dim.19), calls=%async_computation | async-start | bytes 2097152 | tf_op jit(solution)/shard_map/all_to_all | solution.py:186
  16.3 1.7 %reshape.39 = bf16[27,32,8,32]{3,2,1,0:T(8,128)(2,1)} reshape(bf16[27,32,256]{2,1,0:T(8,128)(2,1)S(1)} %copy-done.4) | data formatting | bytes 884736 | tf_op jit(solution)/shard_map/reshape | solution.py:207
  18.0 1.9 %copy.42 = bf16[27,32,8,32]{3,1,2,0:T(8,128)(2,1)S(1)} copy(bf16[27,32,8,32]{3,2,1,0:T(8,128)(2,1)} %reshape.39) | data formatting | bytes 884736 | tf_op jit(solution)/shard_map/reshape | solution.py:207
  19.9 2.0 %gather_fusion = bf16[8,27,32,32]{3,2,1,0:T(8,128)(2,1)} fusion(bf16[27,32,8,32]{3,1,2,0:T(8,128)(2,1)S(1)} %copy.42, s32[1024]{0:T(1024)S(1)} %pad_clamp_fusion), kind=kCustom, calls=%fused_computation | custom fusion | bytes 884768 | tf_op jit(solution)/shard_map/gather | solution.py:207
  21.9 2.3 %copy.43 = bf16[27,32,8,32]{3,2,1,0:T(8,128)(2,1)S(1)} copy(bf16[27,32,8,32]{3,1,0,2:T(8,128)(2,1)} %bitcast.48) | data formatting | bytes 884736 | tf_op jit(solution)/shard_map/gather | solution.py:207
  24.2 1.9 %reshape_reshape.3 = bf16[3,3,3,32,256]{4,3,2,1,0:T(8,128)(2,1)} reshape(bf16[27,32,8,32]{3,2,1,0:T(8,128)(2,1)S(1)} %copy.43) | data formatting | bytes 884736 | tf_op jit(solution)/shard_map/reshape;reshape | solution.py:111
  26.2 0.9 constant_dynamic-update-slice_fusion.2
  28.0 2.1 %copy.39 = bf16[3,32,32,1,64]{2,1,4,0,3:T(8,128)(2,1)} copy(bf16[3,32,32,1,64]{4,2,1,0,3:T(8,128)(2,1)S(1)} %reshape.64) | data formatting | bytes 786432 | tf_op jit(solution)/shard_map/reshape | solution.py:110
  30.1 1.8 %pad.5 = bf16[3,32,32,1,72]{2,1,4,0,3:T(8,128)(2,1)S(1)} pad(bf16[3,32,32,1,64]{2,1,4,0,3:T(8,128)(2,1)} %copy.39, bf16[]{:T(256)} %constant.83.clone.1), padding=0_0x0_0x0_0x0_0x1_7 | pad | bytes 835586 | tf_op jit(solution)/shard_map/reshape | solution.py:110
  31.9 2.4 %copy.41 = bf16[3,32,32,1,8,9]{1,4,5,2,0,3:T(8,128)(2,1)} copy(bf16[3,32,32,1,8,9]{2,1,5,4,0,3:T(8,128)(2,1)S(1)} %bitcast.49) | data formatting | bytes 884736 | tf_op jit(solution)/shard_map/conv_general_dilated | solution.py:112
  34.2 1.1 slice.67
  35.3 4.0 %fusion.9 = f32[1,32,8,9,256]{4,2,3,1,0:T(8,128)S(1)} fusion(bf16[3,3,3,32,256]{4,3,2,1,0:T(8,128)(2,1)} %reshape_reshape.3, bf16[3,32,32,1,7,2]{1,4,5,2,0,3:T(8,128)(2,1)S(1)} %slice.67, bf16[3,32,32,1,8,9]{1,4,5,2,0,3:T(8,128)(2,1)} %copy.41, pred[8,9]{0,1:T(8,128)(4,1)S(1)} %copy-done.8), kind=kOutput, calls=%fused_computation.13 | convolution fusion | flops 1000194048 | bytes 3330120 | tf_op jit(solution)/shard_map/conv_general_dilated | solution.py:112
  41.1 1.2 copy.45
  42.3 1.3 copy-done
  43.7 1.1 slice_select_fusion.2
  44.8 2.9 %collective-permute-start.2 = (f32[1,128,2048]{1,2,0:T(8,128)}, f32[1,128,2048]{1,2,0:T(8,128)}, u32[]{:S(2)}, u32[]{:S(2)}) collective-permute-start(f32[1,128,2048]{1,2,0:T(8,128)} %slice_select_fusion.2), channel_id=1, source_target_pairs={{0,1},{1,0},{2,3},{3,2},{4,5},{5,4},{6,7},{7,6},{8,9},{9,8},{10,11... | collective-permute-start | bytes 3145736 | tf_op jit(solution)/shard_map/ppermute | solution.py:40
  47.7 1.3 copy.59
  49.0 7.3 %shard_map.67 = f32[27,32,256]{2,1,0:T(8,128)} custom-call(bf16[3,32,2304]{2,1,0:T(8,128)(2,1)} %pad.4.x_ref, bf16[2048,256]{1,0:T(8,128)(2,1)} %bitcast.54), custom_call_target="tpu_custom_call" | custom-call | tf_op jit(solution)/shard_map/pallas_call | solution.py:168
  56.3 2.0 %slice_select_fusion.3 = f32[432,256]{1,0:T(8,128)} fusion(f32[864,256]{1,0:T(8,128)} %bitcast.46, pred[]{:T(512)S(6)} %eq.22), kind=kLoop, calls=%fused_computation.32 | loop fusion | flops 110592 | bytes 1327105 | tf_op jit(solution)/shard_map/jit(_where)/select_n | solution.py:39
  58.3 2.2 %reshape.68 = bf16[1,256,32,1,64]{4,2,1,3,0:T(8,128)(2,1)S(1)} reshape(bf16[8,1,32,2048]{3,2,1,0:T(8,128)(2,1)S(1)} %all-to-all-done) | data formatting | bytes 2097152 | tf_op jit(solution)/shard_map/reshape;reshape;transpose | solution.py:122
  60.5 2.7 %copy.61 = bf16[1,256,32,1,64]{1,2,4,3,0:T(8,128)(2,1)S(1)} copy(bf16[1,256,32,1,64]{4,2,1,3,0:T(8,128)(2,1)S(1)} %reshape.68) | data formatting | bytes 2097152
  64.3 5.8 %convolution_select_fusion = f32[3,32,8,9,32]{4,2,3,1,0:T(8,128)S(1)} fusion(bf16[3,3,3,32,256]{4,3,2,1,0:T(8,128)(2,1)S(1)} %bitcast.56, pred[8,9]{0,1:T(8,128)(4,1)S(1)} %copy-done.8, bf16[1,256,32,1,7,2]{1,4,5,2,3,0:T(8,128)(2,1)S(1)} %slice.75, bf16[1,256,32,1,8,9]{1,4,5,2,3,0:T(8,128)(2,1)S(1)} %copy.52), kind=kOutput, calls=%fused_computation.12 | convolution fusion | flops 1002528768 | bytes 2736200 | tf_op jit(solution)/shard_map/conv_general_dilated | solution.py:124
  70.6 1.5 %copy.56 = f32[1,1,32,32,64]{4,3,2,1,0:T(8,128)} copy(f32[1,1,32,32,64]{2,3,4,0,1:T(8,128)S(1)} %slice_bitcast_fusion.2) | data formatting | bytes 524288 | tf_op jit(solution)/shard_map/slice | solution.py:136
  72.1 1.9 %slice.51 = f32[1,32,2048]{2,1,0:T(8,128)} reshape(f32[1,1,32,32,64]{4,3,2,1,0:T(8,128)} %copy.56) | data formatting | bytes 524288 | tf_op jit(solution)/shard_map/slice | solution.py:136
  74.1 4.6 %collective-permute-start.5 = (f32[1,32,2048]{2,1,0:T(8,128)}, f32[1,32,2048]{2,1,0:T(8,128)}, u32[]{:S(2)}, u32[]{:S(2)}) collective-permute-start(f32[1,32,2048]{2,1,0:T(8,128)} %slice.51), channel_id=1, source_target_pairs={{0,8},{8,16},{16,24},{24,32},{32,40},{40,48},{48,56},{56,64},{64,7... | collective-permute-start | bytes 786440 | tf_op jit(solution)/shard_map/ppermute | solution.py:136
  78.7 1.2 copy.57
  79.9 1.4 select_add_fusion.1
  81.3 1.3 slice_select_fusion.1
  82.7 2.3 %copy.46 = f32[1,64,2048]{2,1,0:T(8,128)} copy(f32[1,64,2048]{1,2,0:T(8,128)} %slice_select_fusion.1) | data formatting | bytes 1048576 | tf_op jit(solution)/shard_map/jit(_where)/select_n | solution.py:39
  85.0 2.7 %collective-permute-start.3 = (f32[1,64,2048]{2,1,0:T(8,128)}, f32[1,64,2048]{2,1,0:T(8,128)}, u32[]{:S(2)}, u32[]{:S(2)}) collective-permute-start(f32[1,64,2048]{2,1,0:T(8,128)} %copy.46), channel_id=1, source_target_pairs={{0,4},{1,5},{2,6},{3,7},{4,0},{5,1},{6,2},{7,3},{8,12},{9,13},{10,... | collective-permute-start | bytes 1572872 | tf_op jit(solution)/shard_map/ppermute | solution.py:40
  87.7 1.9 %select_add_fusion.2 = f32[432,256]{1,0:T(8,128)} fusion(f32[432,256]{1,0:T(8,128)} %collective-permute-done.7, f32[864,256]{1,0:T(8,128)S(1)} %bitcast.47, pred[]{:T(512)S(6)} %eq.22), kind=kLoop, calls=%fused_computation.31 | loop fusion | flops 221184 | bytes 1769473 | tf_op jit(solution)/shard_map/add | solution.py:40
  89.6 2.0 %reshape.43 = f32[16,27,256]{2,1,0:T(8,128)} reshape(f32[432,256]{1,0:T(8,128)} %select_add_fusion.2) | data formatting | bytes 884736 | tf_op jit(solution)/shard_map/reshape | solution.py:177
  91.5 8.3 %all-to-all-start.1 = ((f32[16,27,256]{2,1,0:T(8,128)}), f32[16,27,256]{2,1,0:T(8,128)}, u32[]{:S(2)}, u32[]{:S(2)}) async-start(f32[16,27,256]{2,1,0:T(8,128)} %reshape.43), calls=%async_computation.1 | async-start | bytes 1048576 | tf_op jit(solution)/shard_map/all_to_all | solution.py:179
  99.9 1.1 slice_bitcast_fusion.1
  100.9 1.9 %copy.58 = f32[1,1,32,32,64]{4,3,2,1,0:T(8,128)S(1)} copy(f32[1,1,32,32,64]{2,3,4,0,1:T(8,128)} %slice_bitcast_fusion.1) | data formatting | bytes 524288 | tf_op jit(solution)/shard_map/slice | solution.py:137
  103.8 2.8 %collective-permute-start.6 = (f32[1,32,2048]{2,1,0:T(8,128)}, f32[1,32,2048]{2,1,0:T(8,128)}, u32[]{:S(2)}, u32[]{:S(2)}) collective-permute-start(f32[1,32,2048]{2,1,0:T(8,128)} %slice.53), channel_id=1, source_target_pairs={{8,0},{16,8},{24,16},{32,24},{40,32},{48,40},{56,48},{64,56},{72,6... | collective-permute-start | bytes 786440 | tf_op jit(solution)/shard_map/ppermute | solution.py:137
  107.9 1.4 copy.47
  109.6 4.3 %all-to-all-done.1 = f32[16,27,256]{2,1,0:T(8,128)} async-done(((f32[16,27,256]{2,1,0:T(8,128)}), f32[16,27,256]{2,1,0:T(8,128)}, u32[]{:S(2)}, u32[]{:S(2)}) %all-to-all-start.1) | async-done | bytes 442400 | tf_op jit(solution)/shard_map/all_to_all | solution.py:179
  113.9 1.1 reduce_sum.9
  115.8 5.9 %all-to-all-start.2 = ((f32[16,27,256]{2,1,0:T(8,128)}), f32[16,27,256]{2,1,0:T(8,128)S(1)}, u32[]{:S(2)}, u32[]{:S(2)}) async-start(f32[16,27,256]{2,1,0:T(8,128)} %broadcast_in_dim.20), calls=%async_computation.2 | async-start | bytes 1048576 | tf_op jit(solution)/shard_map/all_to_all | solution.py:186
  122.7 1.7 %add_convert_fusion.1 = bf16[1,32,2048]{2,1,0:T(8,128)(2,1)} fusion(f32[1,32,2048]{2,1,0:T(8,128)} %collective-permute-done.6, f32[1,32,2048]{2,1,0:T(8,128)S(1)} %slice.49, f32[1,32,2048]{2,1,0:T(8,128)} %collective-permute-done.5), kind=kLoop, calls=%fused_computation.33 | loop fusion | flops 196608 | bytes 917504 | tf_op jit(solution)/shard_map/convert_element_type | solution.py:211
  124.5 4.5 %collective-permute-done.4 = f32[1,32,2048]{2,1,0:T(8,128)S(1)} collective-permute-done((f32[1,32,2048]{2,1,0:T(8,128)S(1)}, f32[1,32,2048]{2,1,0:T(8,128)S(1)}, u32[]{:S(2)}, u32[]{:S(2)}) %collective-permute-start.4) | collective-permute-done | bytes 262176 | tf_op jit(solution)/shard_map/ppermute | solution.py:40
  129.3 5.2 %all-to-all-done.2 = f32[16,27,256]{2,1,0:T(8,128)S(1)} async-done(((f32[16,27,256]{2,1,0:T(8,128)}), f32[16,27,256]{2,1,0:T(8,128)S(1)}, u32[]{:S(2)}, u32[]{:S(2)}) %all-to-all-start.2) | async-done | bytes 442400 | tf_op jit(solution)/shard_map/all_to_all | solution.py:186
  134.6 3.6 %collective-permute-start.8 = (f32[432,256]{1,0:T(8,128)S(1)}, f32[432,256]{1,0:T(8,128)S(1)}, u32[]{:S(2)}, u32[]{:S(2)}) collective-permute-start(f32[432,256]{1,0:T(8,128)S(1)} %reshape.44), channel_id=1, source_target_pairs={{0,8},{8,0},{1,9},{9,1},{2,10},{10,2},{3,11},{11,3},{4,12},{12,4},... | collective-permute-start | bytes 1327112 | tf_op jit(solution)/shard_map/ppermute | solution.py:49
  139.7 1.0 pad_maximum_fusion
  (55 shorter events, 10.5 us)
Async XLA Ops:
  0.6 15.7 %copy-start.4 = (bf16[27,32,256]{2,1,0:T(8,128)(2,1)S(1)}, bf16[27,32,256]{2,1,0:T(8,128)(2,1)}, u32[]{:S(2)}) copy-start(bf16[27,32,256]{2,1,0:T(8,128)(2,1)} %param.5) | copy-start | bytes 1327108
  0.6 25.5 %collective-permute-start = (bf16[1,32,2048]{2,1,0:T(8,128)(2,1)}, bf16[1,32,2048]{2,1,0:T(8,128)(2,1)}, u32[]{:S(2)}, u32[]{:S(2)}) collective-permute-start(bf16[1,32,2048]{2,1,0:T(8,128)(2,1)} %param.4), channel_id=1, source_target_pairs={{0,8},{8,16},{16,24},{24,32},{32,40},{40,48},{48,56},{56,64},{64,7... | collective-permute-start | bytes 393224 | tf_op jit(solution)/shard_map/ppermute | solution.py:17
  5.7 21.4 %collective-permute-start.1 = (bf16[1,32,2048]{2,1,0:T(8,128)(2,1)}, bf16[1,32,2048]{2,1,0:T(8,128)(2,1)S(1)}, u32[]{:S(2)}, u32[]{:S(2)}) collective-permute-start(bf16[1,32,2048]{2,1,0:T(8,128)(2,1)} %param.4), channel_id=1, source_target_pairs={{8,0},{16,8},{24,16},{32,24},{40,32},{48,40},{56,48},{64,56},{72,6... | collective-permute-start | bytes 393224 | tf_op jit(solution)/shard_map/ppermute | solution.py:20
  9.8 37.9 %all-to-all-start = ((bf16[8,1,32,2048]{3,2,1,0:T(8,128)(2,1)}), bf16[8,1,32,2048]{3,2,1,0:T(8,128)(2,1)S(1)}, u32[]{:S(2)}, u32[]{:S(2)}) async-start(bf16[8,1,32,2048]{3,2,1,0:T(8,128)(2,1)} %broadcast_in_dim.19), calls=%async_computation | async-start | bytes 2097152 | tf_op jit(solution)/shard_map/all_to_all | solution.py:186
  18.0 1.9 %copy-start.7 = (s32[8]{0:T(128)S(1)}, s32[8]{0:T(128)}, u32[]{:S(2)}) copy-start(s32[8]{0:T(128)} %constant.104) | copy-start | bytes 100
  24.2 2.9 %copy-start.6 = (bf16[1,32,2048]{2,1,0:T(8,128)(2,1)S(1)}, bf16[1,32,2048]{2,1,0:T(8,128)(2,1)}, u32[]{:S(2)}) copy-start(bf16[1,32,2048]{2,1,0:T(8,128)(2,1)} %param.4) | copy-start | bytes 393220
  31.8 3.5 %copy-start.8 = (pred[8,9]{0,1:T(8,128)(4,1)S(1)}, pred[8,9]{0,1:T(8,128)(4,1)}, u32[]{:S(2)}) copy-start(pred[8,9]{0,1:T(8,128)(4,1)} %constant.98) | copy-start | bytes 220
  42.3 1.3 copy-start
  44.8 35.1 %collective-permute-start.2 = (f32[1,128,2048]{1,2,0:T(8,128)}, f32[1,128,2048]{1,2,0:T(8,128)}, u32[]{:S(2)}, u32[]{:S(2)}) collective-permute-start(f32[1,128,2048]{1,2,0:T(8,128)} %slice_select_fusion.2), channel_id=1, source_target_pairs={{0,1},{1,0},{2,3},{3,2},{4,5},{5,4},{6,7},{7,6},{8,9},{9,8},{10,11... | collective-permute-start | bytes 3145736 | tf_op jit(solution)/shard_map/ppermute | solution.py:40
  58.3 29.4 %collective-permute-start.7 = (f32[432,256]{1,0:T(8,128)}, f32[432,256]{1,0:T(8,128)}, u32[]{:S(2)}, u32[]{:S(2)}) collective-permute-start(f32[432,256]{1,0:T(8,128)} %slice_select_fusion.3), channel_id=1, source_target_pairs={{0,8},{8,0},{1,9},{9,1},{2,10},{10,2},{3,11},{11,3},{4,12},{12,4},... | collective-permute-start | bytes 1327112 | tf_op jit(solution)/shard_map/ppermute | solution.py:40
  63.2 1.0 copy-start.5
  74.1 5.9 %copy-start.1 = (f32[1,1,256,32,64]{2,4,3,1,0:T(8,128)S(1)}, f32[1,1,256,32,64]{2,4,3,1,0:T(8,128)}, u32[]{:S(2)}) copy-start(f32[1,1,256,32,64]{2,4,3,1,0:T(8,128)} %copy-done) | copy-start | bytes 6291460
  74.1 48.7 %collective-permute-start.5 = (f32[1,32,2048]{2,1,0:T(8,128)}, f32[1,32,2048]{2,1,0:T(8,128)}, u32[]{:S(2)}, u32[]{:S(2)}) collective-permute-start(f32[1,32,2048]{2,1,0:T(8,128)} %slice.51), channel_id=1, source_target_pairs={{0,8},{8,16},{16,24},{24,32},{32,40},{40,48},{48,56},{56,64},{64,7... | collective-permute-start | bytes 786440 | tf_op jit(solution)/shard_map/ppermute | solution.py:136
  81.3 6.4 %copy-start.2 = (f32[27,32,256]{2,1,0:T(8,128)S(1)}, f32[27,32,256]{2,1,0:T(8,128)}, u32[]{:S(2)}) copy-start(f32[27,32,256]{2,1,0:T(8,128)} %shard_map.67) | copy-start | bytes 2654212
  85.0 22.8 %collective-permute-start.3 = (f32[1,64,2048]{2,1,0:T(8,128)}, f32[1,64,2048]{2,1,0:T(8,128)}, u32[]{:S(2)}, u32[]{:S(2)}) collective-permute-start(f32[1,64,2048]{2,1,0:T(8,128)} %copy.46), channel_id=1, source_target_pairs={{0,4},{1,5},{2,6},{3,7},{4,0},{5,1},{6,2},{7,3},{8,12},{9,13},{10,... | collective-permute-start | bytes 1572872 | tf_op jit(solution)/shard_map/ppermute | solution.py:40
  89.6 10.3 %copy-start.3 = (f32[1,32,8,9,32]{4,1,3,2,0:T(8,128)S(1)}, f32[1,32,8,9,32]{4,1,3,2,0:T(8,128)}, u32[]{:S(2)}) copy-start(f32[1,32,8,9,32]{4,1,3,2,0:T(8,128)} %copy.57) | copy-start | bytes 884740
  91.5 22.3 %all-to-all-start.1 = ((f32[16,27,256]{2,1,0:T(8,128)}), f32[16,27,256]{2,1,0:T(8,128)}, u32[]{:S(2)}, u32[]{:S(2)}) async-start(f32[16,27,256]{2,1,0:T(8,128)} %reshape.43), calls=%async_computation.1 | async-start | bytes 1048576 | tf_op jit(solution)/shard_map/all_to_all | solution.py:179
  103.8 19.0 %collective-permute-start.6 = (f32[1,32,2048]{2,1,0:T(8,128)}, f32[1,32,2048]{2,1,0:T(8,128)}, u32[]{:S(2)}, u32[]{:S(2)}) collective-permute-start(f32[1,32,2048]{2,1,0:T(8,128)} %slice.53), channel_id=1, source_target_pairs={{8,0},{16,8},{24,16},{32,24},{40,32},{48,40},{56,48},{64,56},{72,6... | collective-permute-start | bytes 786440 | tf_op jit(solution)/shard_map/ppermute | solution.py:137
  115.8 18.7 %all-to-all-start.2 = ((f32[16,27,256]{2,1,0:T(8,128)}), f32[16,27,256]{2,1,0:T(8,128)S(1)}, u32[]{:S(2)}, u32[]{:S(2)}) async-start(f32[16,27,256]{2,1,0:T(8,128)} %broadcast_in_dim.20), calls=%async_computation.2 | async-start | bytes 1048576 | tf_op jit(solution)/shard_map/all_to_all | solution.py:186
  122.4 6.6 %collective-permute-start.4 = (f32[1,32,2048]{2,1,0:T(8,128)S(1)}, f32[1,32,2048]{2,1,0:T(8,128)S(1)}, u32[]{:S(2)}, u32[]{:S(2)}) collective-permute-start(f32[1,32,2048]{2,1,0:T(8,128)S(1)} %copy.48), channel_id=1, source_target_pairs={{0,2},{1,3},{2,0},{3,1},{4,6},{5,7},{6,4},{7,5},{8,10},{9,11},{10,... | collective-permute-start | bytes 786440 | tf_op jit(solution)/shard_map/ppermute | solution.py:40
  134.6 5.0 %collective-permute-start.8 = (f32[432,256]{1,0:T(8,128)S(1)}, f32[432,256]{1,0:T(8,128)S(1)}, u32[]{:S(2)}, u32[]{:S(2)}) collective-permute-start(f32[432,256]{1,0:T(8,128)S(1)} %reshape.44), channel_id=1, source_target_pairs={{0,8},{8,0},{1,9},{9,1},{2,10},{10,2},{3,11},{11,3},{4,12},{12,4},... | collective-permute-start | bytes 1327112 | tf_op jit(solution)/shard_map/ppermute | solution.py:49
